TPU v7x, 128 devices: a whole 4x4x4 slice. The times are simulated.
128 devices in a mesh: dp: 8 (over x_lo, z), wshard: 4 (over y), tensor: 4 (over x_hi, core).
Axes of the slice: x: 4 (x_hi: 2, x_lo: 2; x = x_hi * 2 + x_lo), y: 4, z: 4, core: 2. Of those that a mesh axis runs over, the one named last changes fastest.
Arguments:
- expert_grads: bfloat16 [8, 4, 768, 2048], P('dp', 'wshard', None, 'tensor'), may hold values from -6 to 6
- dense_grads: bfloat16 [8, 768, 2048], P('dp', 'wshard', 'tensor'), may hold values from -6 to 6
- expert_master: float32 [4, 768, 2048], P('wshard', None, ('tensor', 'dp')), may hold values from -0.6 to 0.6
- expert_first: float32 [4, 768, 2048], P('wshard', None, ('tensor', 'dp')), may hold values from -3 to 3
- expert_second: float32 [4, 768, 2048], P('wshard', None, ('tensor', 'dp')), may hold values from 0.01 to 1
- expert_stat: float32 [4, 768, 768], P('wshard', ('tensor', 'dp')), as said below
- expert_basis: float32 [4, 768, 768], P('wshard'), may hold values from -0.21875 to 0.21875
- dense_master: float32 [768, 2048], P('wshard', ('tensor', 'dp')), may hold values from -0.6 to 0.6
- dense_first: float32 [768, 2048], P('wshard', ('tensor', 'dp')), may hold values from -3 to 3
- dense_second: float32 [768, 2048], P(None, ('tensor', 'dp')), may hold values from 0.01 to 1
- dense_stat: float32 [768, 768], P(('tensor', 'dp')), as said below
- dense_basis: float32 [768, 768], replicated, may hold values from -0.21875 to 0.21875
Outputs:
- expert_master_out: float32 [4, 768, 2048], P('wshard', None, ('tensor', 'dp'))
- expert_first_out: float32 [4, 768, 2048], P('wshard', None, ('tensor', 'dp'))
- expert_second_out: float32 [4, 768, 2048], P('wshard', None, ('tensor', 'dp'))
- expert_stat_out: float32 [4, 768, 768], P('wshard', ('tensor', 'dp'))
- expert_basis_out: float32 [4, 768, 768], P('wshard')
- expert_weights: bfloat16 [4, 768, 2048], P('wshard', None, 'tensor')
- dense_master_out: float32 [768, 2048], P('wshard', ('tensor', 'dp'))
- dense_first_out: float32 [768, 2048], P('wshard', ('tensor', 'dp'))
- dense_second_out: float32 [768, 2048], P(None, ('tensor', 'dp'))
- dense_stat_out: float32 [768, 768], P(('tensor', 'dp'))
- dense_basis_out: float32 [768, 768], replicated
- dense_weights: bfloat16 [768, 2048], P('wshard', 'tensor')
Inputs may be any that keep to these rules, and one draw needn't show every extreme that they name: `expert_stat`: symmetric running statistics of each expert. `dense_stat`: A symmetric running statistic.
All inputs are finite; a program needn't handle non-finite values.
Results may differ from a plain program's by a relative error of at most 0.001.
Values may be sent and summed in bfloat16 or wider, within the bound.
No kernel may reach another device: no remote copies, remote signals or barrier semaphores. Data moves between devices by JAX's collectives and lax.ppermute only.
A program may use at most 128 MiB of HBM per device.

v0:
```python
import jax
import jax.numpy as jnp
from jax import lax
from jax.sharding import PartitionSpec as P

NS_ITERS = 3


HIGHEST = lax.Precision.HIGHEST
linear_coef = 3.4445
cubic_coef = -4.775
quintic_coef = 2.0315


def local_gram(current):
    return jnp.einsum("bki,bkj->bij", current, current, precision=HIGHEST)


def quintic_step(current, gram_matrix):
    first_prod = jnp.einsum("bik,bkj->bij", current, gram_matrix, precision=HIGHEST)
    second_prod = jnp.einsum("bik,bkj->bij", first_prod, gram_matrix, precision=HIGHEST)
    return linear_coef * current + cubic_coef * first_prod + quintic_coef * second_prod


def shards(
    expert_grads,
    dense_grads,
    expert_master,
    expert_first,
    expert_second,
    expert_stat,
    expert_basis,
    dense_master,
    dense_first,
    dense_second,
    dense_stat,
    dense_basis,
):
    replicas = lax.axis_size("dp")
    experts_here = expert_grads.shape[1]
    expert_local = expert_grads.reshape(expert_grads.shape[1:]).astype(jnp.float32)
    dense_local = dense_grads.reshape(dense_grads.shape[1:]).astype(jnp.float32)
    expert_sum, dense_sum = (
        lax.psum_scatter(expert_local, "dp", scatter_dimension=2, tiled=True),
        lax.psum_scatter(dense_local, "dp", scatter_dimension=1, tiled=True),
    )
    expert_mean = expert_sum / replicas
    dense_mean = dense_sum / replicas
    expert_first_out = 0.9 * expert_first + 0.1 * expert_mean
    dense_first_out = 0.9 * dense_first + 0.1 * dense_mean
    dense_grad_full, dense_first_full = (
        lax.all_gather(dense_mean, "wshard", axis=0, tiled=True),
        lax.all_gather(dense_first_out, "wshard", axis=0, tiled=True),
    )
    grads_all = jnp.concatenate([expert_mean, dense_grad_full[None]], 0)
    firsts_all = jnp.concatenate([expert_first_out, dense_first_full[None]], 0)
    bases_all = jnp.concatenate([expert_basis, dense_basis[None]], 0)
    seconds_all = jnp.concatenate([expert_second, dense_second[None]], 0)
    columns = grads_all.shape[2]
    rotated = jnp.einsum(
        "bki,bkc->bic", bases_all, jnp.concatenate([grads_all, firsts_all], 2), precision=HIGHEST
    )
    grad_rot = rotated[:, :, :columns]
    first_rot = rotated[:, :, columns:]
    seconds_out = 0.95 * seconds_all + 0.05 * grad_rot * grad_rot
    scaled = first_rot / (jnp.sqrt(seconds_out) + 1e-08)
    update = jnp.einsum("bik,bkc->bic", bases_all, scaled, precision=HIGHEST)
    expert_master_out = expert_master - 0.05 * update[:experts_here]
    dense_rows_here = dense_master.shape[0]
    dense_update = lax.dynamic_slice_in_dim(
        update[experts_here], lax.axis_index("wshard") * dense_rows_here, dense_rows_here, 0
    )
    dense_master_out = dense_master - 0.05 * dense_update
    expert_weights, dense_weights = (
        lax.all_gather(expert_master_out.astype(jnp.bfloat16), "dp", axis=2, tiled=True),
        lax.all_gather(dense_master_out.astype(jnp.bfloat16), "dp", axis=1, tiled=True),
    )
    summed = lax.psum_scatter(
        jnp.einsum("bic,bjc->ibj", grads_all, grads_all, precision=HIGHEST),
        ("tensor", "dp"),
        scatter_dimension=0,
        tiled=True,
    )
    stats_all = jnp.concatenate([expert_stat, dense_stat[None]], 0)
    stats_out = 0.95 * stats_all + 0.05 * jnp.transpose(summed, (1, 0, 2))
    power = jnp.einsum("bik,bkj->bij", stats_out, bases_all, precision=HIGHEST)
    square_sum = lax.psum(jnp.sum(power * power, (1, 2)), ("tensor", "dp"))
    current = power * lax.rsqrt(square_sum + 1e-06)[:, None, None]
    for repeat in range(NS_ITERS):
        gram_matrix = lax.psum(local_gram(current), ("tensor", "dp"))
        current = quintic_step(current, gram_matrix)
    bases_out = lax.all_gather(current, ("tensor", "dp"), axis=1, tiled=True)
    return (
        expert_master_out,
        expert_first_out,
        seconds_out[:experts_here],
        stats_out[:experts_here],
        bases_out[:experts_here],
        expert_weights,
        dense_master_out,
        dense_first_out,
        seconds_out[experts_here],
        stats_out[experts_here],
        bases_out[experts_here],
        dense_weights,
    )


def solution(mesh):
    in_specs = (
        P("dp", "wshard", None, "tensor"),
        P("dp", "wshard", "tensor"),
        P("wshard", None, ("tensor", "dp")),
        P("wshard", None, ("tensor", "dp")),
        P("wshard", None, ("tensor", "dp")),
        P("wshard", ("tensor", "dp"), None),
        P("wshard", None, None),
        P("wshard", ("tensor", "dp")),
        P("wshard", ("tensor", "dp")),
        P(None, ("tensor", "dp")),
        P(("tensor", "dp"), None),
        P(),
    )
    out_specs = (
        P("wshard", None, ("tensor", "dp")),
        P("wshard", None, ("tensor", "dp")),
        P("wshard", None, ("tensor", "dp")),
        P("wshard", ("tensor", "dp"), None),
        P("wshard", None, None),
        P("wshard", None, "tensor"),
        P("wshard", ("tensor", "dp")),
        P("wshard", ("tensor", "dp")),
        P(None, ("tensor", "dp")),
        P(("tensor", "dp"), None),
        P(),
        P("wshard", "tensor"),
    )
    return jax.shard_map(shards, mesh=mesh, in_specs=in_specs, out_specs=out_specs, check_vma=False)
```

profile of v0, /device:TPU:0, one launch (start us, length us, event | category | flops | bytes accessed | tf_op | source)
XLA Modules:
  0.0 765.4 jit_solution(16698547838578307762)
XLA Ops:
  7.2 1.1 copy.46
  9.3 1.4 copy.45
  10.7 1.3 bitcast_convert_fusion
  12.0 39.9 %reduce-scatter.5.cloned.1.call-done = f32[192,64]{0,1:T(8,128)} async-done(((f32[192,512]{0,1:T(8,128)}), f32[192,64]{0,1:T(8,128)}) %reduce-scatter.5.cloned.1.call-update) | async-done | bytes 49168 | tf_op jit(solution)/shard_map/reduce_scatter | solution.py:45
  52.8 12.6 %all-gather = f32[4,192,64]{1,2,0:T(8,128)S(1)} all-gather(f32[1,192,64]{1,2,0:T(8,128)S(1)} %get-tuple-element.61), channel_id=1, replica_groups=mesh['dp'=8,'wshard'=4,'tensor'=4] {'wshard'}, dimensions={0}, use_global_device_ids=true | all-gather | bytes 245760 | tf_op jit(solution)/shard_map/all_gather | solution.py:52
  65.7 29.1 %reduce-scatter.3.cloned.1.call-done = f32[1,768,64]{1,2,0:T(8,128)} async-done(((f32[1,768,512]{1,2,0:T(8,128)}), f32[1,768,64]{1,2,0:T(8,128)}) %reduce-scatter.3.cloned.1.call-update) | async-done | bytes 196624 | tf_op jit(solution)/shard_map/reduce_scatter | solution.py:44
  94.8 1.6 broadcast_multiply_fusion
  96.5 5.6 convolution_bitcast_fusion
  102.1 8.2 %copy.49 = f32[768,2,768]{2,1,0:T(2,128)} copy(f32[768,2,768]{0,2,1:T(8,128)} %convolution_bitcast_fusion) | data formatting | bytes 9437184 | tf_op jit(solution)/shard_map/bic,bjc->ibj/transpose | solution.py:79
  112.2 109.5 %all-reduce.12.cloned.1.call-done = f32[768,2,768]{2,1,0:T(2,128)} async-done(((f32[768,2,768]{2,1,0:T(2,128)}), f32[768,2,768]{2,1,0:T(2,128)}) %all-reduce.12.cloned.1.call-update) | async-done | bytes 4718608
  222.7 4.1 multiply_reduce_fusion
  226.8 66.3 %psum.28 = f32[2]{0:T(128)S(1)} all-reduce(f32[2]{0:T(128)S(1)} %get-tuple-element.63), channel_id=1, replica_groups=mesh['dp'=8,'wshard'=4,'tensor'=4] {'tensor','dp'}, use_global_device_ids=true, to_apply=%region_4.0 | all-reduce | flops 2 | bytes 16 | tf_op jit(solution)/shard_map/psum | solution.py:87
  293.1 5.7 fusion.24
  299.0 108.7 %all-reduce.6.cloned.1.call-done = f32[2,768,768]{2,1,0:T(8,128)} async-done(((f32[2,768,768]{2,1,0:T(8,128)}), f32[2,768,768]{2,1,0:T(8,128)}) %all-reduce.6.cloned.1.call-update) | async-done | bytes 4718608 | tf_op jit(solution)/shard_map/psum | solution.py:90
  407.8 4.8 fusion.22
  412.6 2.4 fusion.5
  415.0 5.6 fusion.36
  420.9 112.1 %all-reduce.8.cloned.1.call-done = f32[2,768,768]{2,1,0:T(8,128)} async-done(((f32[2,768,768]{2,1,0:T(8,128)}), f32[2,768,768]{2,1,0:T(8,128)}) %all-reduce.8.cloned.1.call-update) | async-done | bytes 4718608 | tf_op jit(solution)/shard_map/psum | solution.py:90
  533.0 4.8 fusion.37
  537.9 2.4 fusion.4
  540.2 5.6 fusion.38
  545.9 112.3 %all-reduce.10.cloned.1.call-done = f32[2,768,768]{2,1,0:T(8,128)} async-done(((f32[2,768,768]{2,1,0:T(8,128)}), f32[2,768,768]{2,1,0:T(8,128)}) %all-reduce.10.cloned.1.call-update) | async-done | bytes 4718608 | tf_op jit(solution)/shard_map/psum | solution.py:90
  658.2 4.8 fusion.39
  663.1 3.0 fusion.3
  666.2 12.9 %all-gather.1 = f32[4,192,64]{1,2,0:T(8,128)S(1)} all-gather(f32[1,192,64]{1,2,0:T(8,128)S(1)} %bitcast.49), channel_id=1, replica_groups=mesh['dp'=8,'wshard'=4,'tensor'=4] {'wshard'}, dimensions={0}, use_global_device_ids=true | all-gather | bytes 245760 | tf_op jit(solution)/shard_map/all_gather | solution.py:53
  679.4 4.6 fusion.2
  684.0 1.1 fusion.13
  685.1 4.8 fusion.1
  691.4 28.6 %all_gather.19 = bf16[192,512]{0,1:T(8,128)(2,1)S(1)} all-gather(bf16[192,64]{0,1:T(8,128)(2,1)S(1)} %get-tuple-element.48), channel_id=1, replica_groups=mesh['dp'=8,'wshard'=4,'tensor'=4] {'dp'}, dimensions={1}, use_global_device_ids=true | all-gather | bytes 221184 | tf_op jit(solution)/shard_map/all_gather | solution.py:76
  720.7 30.2 %all_gather.18 = bf16[1,768,512]{1,2,0:T(8,128)(2,1)S(1)} all-gather(bf16[1,768,64]{1,2,0:T(8,128)(2,1)S(1)} %get-tuple-element.50), channel_id=1, replica_groups=mesh['dp'=8,'wshard'=4,'tensor'=4] {'dp'}, dimensions={2}, use_global_device_ids=true | all-gather | bytes 884736 | tf_op jit(solution)/shard_map/all_gather | solution.py:75
  751.0 1.2 copy.51
  753.7 4.9 slice_bitcast_fusion
  (56 shorter events, 9.2 us)
Async XLA Ops:
  7.2 44.8 %copy-start.11 = (f32[192,64]{0,1:T(8,128)S(1)}, f32[192,64]{0,1:T(8,128)}, u32[]{:S(2)}) copy-start(f32[192,64]{0,1:T(8,128)} %param.20) | copy-start | bytes 147460
  7.2 87.6 %copy-start.6 = (f32[1,768,64]{1,2,0:T(8,128)S(1)}, f32[1,768,64]{1,2,0:T(8,128)}, u32[]{:S(2)}) copy-start(f32[1,768,64]{1,2,0:T(8,128)} %param.15) | copy-start | bytes 589828
  7.2 44.7 %reduce-scatter.5.cloned.1.call-start = ((), (), s32[]{:S(2)}) async-start(), calls=%async_computation.3 | async-start | bytes 589824 | tf_op jit(solution)/shard_map/reduce_scatter | solution.py:45
  9.2 85.6 %reduce-scatter.3.cloned.1.call-start = ((), (), s32[]{:S(2)}) async-start(), calls=%async_computation.2 | async-start | bytes 1769472 | tf_op jit(solution)/shard_map/reduce_scatter | solution.py:44
  12.0 209.7 %all-reduce.12.cloned.1.call-start = ((), (), s32[]{:S(2)}) async-start(), calls=%async_computation.8 | async-start | bytes 9437184
  52.8 613.3 %copy-start.5 = (f32[192,64]{0,1:T(8,128)}, f32[192,64]{0,1:T(8,128)S(1)}, u32[]{:S(2)}) copy-start(f32[192,64]{0,1:T(8,128)S(1)} %get-tuple-element.62) | copy-start | bytes 147460
  110.3 0.7 copy-start.12
  110.3 112.3 %copy-start.8 = (f32[24,768]{1,0:T(8,128)S(1)}, f32[24,768]{1,0:T(8,128)}, u32[]{:S(2)}) copy-start(f32[24,768]{1,0:T(8,128)} %param.22) | copy-start | bytes 221188
  110.3 112.3 %copy-start.9 = (f32[1,24,768]{2,1,0:T(8,128)S(1)}, f32[1,24,768]{2,1,0:T(8,128)}, u32[]{:S(2)}) copy-start(f32[1,24,768]{2,1,0:T(8,128)} %param.17) | copy-start | bytes 221188
  110.3 112.4 %copy-start.3 = (f32[768,768]{1,0:T(8,128)S(1)}, f32[768,768]{1,0:T(8,128)}, u32[]{:S(2)}) copy-start(f32[768,768]{1,0:T(8,128)} %param.23) | copy-start | bytes 7077892
  110.3 297.4 %all-reduce.6.cloned.1.call-start = ((), (), s32[]{:S(2)}) async-start(), calls=%async_computation.4 | async-start | bytes 9437184 | tf_op jit(solution)/shard_map/psum | solution.py:90
  298.8 234.2 %all-reduce.8.cloned.1.call-start = ((), (), s32[]{:S(2)}) async-start(), calls=%async_computation.5 | async-start | bytes 9437184 | tf_op jit(solution)/shard_map/psum | solution.py:90
  407.8 4.9 copy-start.2
  420.6 237.6 %all-reduce.10.cloned.1.call-start = ((), (), s32[]{:S(2)}) async-start(), calls=%async_computation.6 | async-start | bytes 9437184 | tf_op jit(solution)/shard_map/psum | solution.py:90
  533.0 4.8 copy-start
  545.8 207.8 %all-gather.4.cloned.1.call-start = ((), (), s32[]{:S(2)}) async-start(), calls=%async_computation.7 | async-start | bytes 4866048 | tf_op jit(solution)/shard_map/all_gather | solution.py:92
  658.2 4.8 copy-start.1
  679.4 5.8 copy-start.4
  684.0 5.9 copy-start.7
  684.0 6.7 copy-start.10
Sparse Core Ops, SparseCore 0:
  10.9 40.9 reduce-scatter.4
  54.9 39.8 reduce-scatter.2
  110.4 111.1 all-reduce.11
  298.9 108.7 all-reduce.5
  420.7 112.2 all-reduce.7
  546.0 112.2 all-reduce.9
  666.3 87.3 all-gather.3
where the time goes:
time: 767 us; the launch traced here: 765 us
  waiting for transfers between devices  512 us (67%)
  blocking collectives  150 us (20%)
  matrix products  58.3 us (8%)
  local copies, waits for them, and re-layouts  21.8 us (3%)
  between operations  15 us (2%)
    psum x3, waiting for transfers between devices, shards(): gram_matrix = lax.psum(local_gram(current), ('tensor', 'dp'))  333 us
    unnamed x8, waiting for transfers between devices  110 us
    psum x1, blocking collectives, shards(): square_sum = lax.psum(jnp.sum(power * power, (1, 2)), ('tensor', 'dp'))  66.3 us
    reduce_scatter x1, waiting for transfers between devices, shards(): lax.psum_scatter(dense_local, 'dp', scatter_dimension=1, tiled=True)  39.9 us
    all_gather x1, blocking collectives, shards(): lax.all_gather(expert_master_out.astype(jnp.bfloat16), 'dp', axis=2, tile...  30.2 us
    reduce_scatter x1, waiting for transfers between devices, shards(): lax.psum_scatter(expert_local, 'dp', scatter_dimension=2, tiled=True)  29.1 us
    all_gather x1, blocking collectives, shards(): lax.all_gather(dense_master_out.astype(jnp.bfloat16), 'dp', axis=1, tiled...  28.6 us
    dot_general x3, matrix products, local_gram(): return jnp.einsum('bki,bkj->bij', current, current, precision=HIGHEST)  16.9 us
  transfers between devices with their start and end apart: 7, of which 7 were waited for; matrix products, arithmetic and copies ran while one was open for 3% of the time, Pallas kernels for 0%

commit v1 on v0

--- a/solution.py
+++ b/solution.py
@@ -75,21 +75,19 @@
         lax.all_gather(expert_master_out.astype(jnp.bfloat16), "dp", axis=2, tiled=True),
         lax.all_gather(dense_master_out.astype(jnp.bfloat16), "dp", axis=1, tiled=True),
     )
-    summed = lax.psum_scatter(
-        jnp.einsum("bic,bjc->ibj", grads_all, grads_all, precision=HIGHEST),
-        ("tensor", "dp"),
-        scatter_dimension=0,
-        tiled=True,
-    )
+    partial_stat = jnp.einsum("bic,bjc->bji", grads_all, grads_all, precision=HIGHEST)
+    summed = lax.psum_scatter(partial_stat, ("tensor", "dp"), scatter_dimension=2, tiled=True)
     stats_all = jnp.concatenate([expert_stat, dense_stat[None]], 0)
-    stats_out = 0.95 * stats_all + 0.05 * jnp.transpose(summed, (1, 0, 2))
-    power = jnp.einsum("bik,bkj->bij", stats_out, bases_all, precision=HIGHEST)
-    square_sum = lax.psum(jnp.sum(power * power, (1, 2)), ("tensor", "dp"))
+    stats_out = 0.95 * stats_all + 0.05 * jnp.transpose(summed, (0, 2, 1))
+    power_rows = jnp.einsum("bik,bkj->bij", stats_out, bases_all, precision=HIGHEST)
+    power = lax.all_gather(power_rows, ("tensor", "dp"), axis=1, tiled=True)
+    square_sum = jnp.sum(power * power, (1, 2))
     current = power * lax.rsqrt(square_sum + 1e-06)[:, None, None]
-    for repeat in range(NS_ITERS):
-        gram_matrix = lax.psum(local_gram(current), ("tensor", "dp"))
-        current = quintic_step(current, gram_matrix)
-    bases_out = lax.all_gather(current, ("tensor", "dp"), axis=1, tiled=True)
+    def ns_iteration(repeat, current):
+        return quintic_step(current, local_gram(current))
+
+    current = lax.fori_loop(0, NS_ITERS, ns_iteration, current)
+    bases_out = current
     return (
         expert_master_out,
         expert_first_out,

time: 767 us -> 535 us (0.70)
  waiting for transfers between devices: 512 us -> 210 us
  matrix products: 58.3 us -> 155 us
  blocking collectives: 150 us -> 84.2 us
  loops' own time: 0 us -> 22.7 us
  local copies, waits for them, and re-layouts: 21.8 us -> 30.7 us
    psum x3 -> x0, waiting for transfers between devices: 333 us -> none  [shards(): gram_matrix = lax.psum(local_gram(current), ('tensor', 'dp'))]
    reduce_scatter x0 -> x1, waiting for transfers between devices: none -> 141 us  [shards(): lax.psum_scatter(partial_stat, ('tensor', 'dp'), scatter_dimension=2, til...]
    unnamed x8 -> x4, waiting for transfers between devices: 110 us -> 0.07 us
    psum x1 -> x0, blocking collectives: 66.3 us -> none  [shards(): square_sum = lax.psum(jnp.sum(power * power, (1, 2)), ('tensor', 'dp'))]
    dot_general x3, matrix products: 7.76 us -> 46.9 us  [quintic_step(): jnp.einsum('bik,bkj->bij', first_prod, gram_matrix, precision=HIGHEST)]
    dot_general x3, matrix products: 16.9 us -> 46.6 us  [local_gram(): return jnp.einsum('bki,bkj->bij', current, current, precision=HIGHEST)]
    dot_general x3, matrix products: 14.5 us -> 41.9 us  [quintic_step(): jnp.einsum('bik,bkj->bij', current, gram_matrix, precision=HIGHEST)]
    another operation x0 -> x1, loops' own time: none -> 22.7 us  [shards(): current = lax.fori_loop(0, NS_ITERS, ns_iteration, current)]
  transfers between devices with their start and end apart: 7 -> 4, of which waited for: 7 -> 3; matrix products, arithmetic and copies ran while one was open for 3% -> 3% of each run, Pallas kernels for 0% -> 0%
where the time goes in v1:
time: 535 us; the launch traced here: 529 us
  waiting for transfers between devices  210 us (39%)
  matrix products  155 us (29%)
  blocking collectives  84.2 us (16%)
  local copies, waits for them, and re-layouts  30.7 us (6%)
  loops' own time  22.7 us (4%)
  between operations  14.4 us (3%)
  other arithmetic  12.1 us (2%)
    reduce_scatter x1, waiting for transfers between devices, shards(): lax.psum_scatter(partial_stat, ('tensor', 'dp'), scatter_dimension=2, til...  141 us
    dot_general x3, matrix products, quintic_step(): jnp.einsum('bik,bkj->bij', first_prod, gram_matrix, precision=HIGHEST)  46.9 us
    dot_general x3, matrix products, local_gram(): return jnp.einsum('bki,bkj->bij', current, current, precision=HIGHEST)  46.6 us
    dot_general x3, matrix products, quintic_step(): jnp.einsum('bik,bkj->bij', current, gram_matrix, precision=HIGHEST)  41.9 us
    reduce_scatter x1, waiting for transfers between devices, shards(): lax.psum_scatter(dense_local, 'dp', scatter_dimension=1, tiled=True)  39.9 us
    all_gather x1, blocking collectives, shards(): lax.all_gather(expert_master_out.astype(jnp.bfloat16), 'dp', axis=2, tile...  30.2 us
    reduce_scatter x1, waiting for transfers between devices, shards(): lax.psum_scatter(expert_local, 'dp', scatter_dimension=2, tiled=True)  29.1 us
    all_gather x1, blocking collectives, shards(): lax.all_gather(dense_master_out.astype(jnp.bfloat16), 'dp', axis=1, tiled...  28.6 us
  transfers between devices with their start and end apart: 4, of which 3 were waited for; matrix products, arithmetic and copies ran while one was open for 3% of the time, Pallas kernels for 0%

profile of v1, /device:TPU:0, one launch (start us, length us, event | category | flops | bytes accessed | tf_op | source)
XLA Modules:
  0.0 529.5 jit_solution(3685827387022544564)
XLA Ops:
  9.3 1.4 copy.43
  10.7 1.3 bitcast_convert_fusion
  12.0 39.9 %reduce-scatter.6.cloned.1.call-done = f32[192,64]{0,1:T(8,128)} async-done(((f32[192,512]{0,1:T(8,128)}), f32[192,64]{0,1:T(8,128)}) %reduce-scatter.6.cloned.1.call-update) | async-done | bytes 49168 | tf_op jit(solution)/shard_map/reduce_scatter | solution.py:45
  52.8 12.6 %all-gather = f32[4,192,64]{1,2,0:T(8,128)S(1)} all-gather(f32[1,192,64]{1,2,0:T(8,128)S(1)} %get-tuple-element.70), channel_id=1, replica_groups=mesh['dp'=8,'wshard'=4,'tensor'=4] {'wshard'}, dimensions={0}, use_global_device_ids=true | all-gather | bytes 245760 | tf_op jit(solution)/shard_map/all_gather | solution.py:52
  65.7 29.1 %reduce-scatter.4.cloned.1.call-done = f32[1,768,64]{1,2,0:T(8,128)} async-done(((f32[1,768,512]{1,2,0:T(8,128)}), f32[1,768,64]{1,2,0:T(8,128)}) %reduce-scatter.4.cloned.1.call-update) | async-done | bytes 196624 | tf_op jit(solution)/shard_map/reduce_scatter | solution.py:44
  95.9 5.6 %fusion.12 = f32[2,768,768]{1,2,0:T(8,128)} fusion(f32[1,768,64]{1,2,0:T(8,128)S(1)} %broadcast_in_dim.17, f32[1,768,64]{1,2,0:T(8,128)S(1)} %get-tuple-element.66), kind=kOutput, calls=%fused_computation.20 | convolution fusion | flops 906067968 | bytes 5111808 | tf_op jit(solution)/shard_map/bic,bjc->bji/dot_general | solution.py:78
  101.5 141.2 %reduce-scatter.8.cloned.1.call-done = f32[2,768,24]{1,2,0:T(8,128)} async-done(((f32[2,768,768]{1,2,0:T(8,128)}), f32[2,768,24]{1,2,0:T(8,128)}) %reduce-scatter.8.cloned.1.call-update) | async-done | bytes 147472 | tf_op jit(solution)/shard_map/reduce_scatter | solution.py:79
  243.7 4.7 fusion.1
  248.4 12.8 %all-gather.1 = f32[4,192,64]{1,2,0:T(8,128)S(1)} all-gather(f32[1,192,64]{1,2,0:T(8,128)S(1)} %bitcast.55), channel_id=1, replica_groups=mesh['dp'=8,'wshard'=4,'tensor'=4] {'wshard'}, dimensions={0}, use_global_device_ids=true | all-gather | bytes 245760 | tf_op jit(solution)/shard_map/all_gather | solution.py:53
  261.6 4.6 fusion.3
  266.3 4.8 fusion.2
  271.8 30.2 %all_gather.18 = bf16[1,768,512]{1,2,0:T(8,128)(2,1)S(1)} all-gather(bf16[1,768,64]{1,2,0:T(8,128)(2,1)S(1)} %get-tuple-element.59), channel_id=1, replica_groups=mesh['dp'=8,'wshard'=4,'tensor'=4] {'dp'}, dimensions={2}, use_global_device_ids=true | all-gather | bytes 884736 | tf_op jit(solution)/shard_map/all_gather | solution.py:75
  302.0 1.2 copy.50
  303.9 28.6 %all_gather.19 = bf16[192,512]{0,1:T(8,128)(2,1)S(1)} all-gather(bf16[192,64]{0,1:T(8,128)(2,1)S(1)} %get-tuple-element.57), channel_id=1, replica_groups=mesh['dp'=8,'wshard'=4,'tensor'=4] {'dp'}, dimensions={1}, use_global_device_ids=true | all-gather | bytes 221184 | tf_op jit(solution)/shard_map/all_gather | solution.py:76
  334.7 3.2 multiply_reduce_fusion
  338.5 2.6 broadcast_multiply_fusion
  341.0 6.1 %copy.47 = f32[2,768,768]{1,2,0:T(8,128)} copy(f32[2,768,768]{2,1,0:T(8,128)} %broadcast_multiply_fusion) | data formatting | bytes 9437184 | tf_op jit(solution)/shard_map/while | solution.py:89
  347.1 164.5 %while.10 = (s32[]{:T(128)}, f32[2,768,768]{1,2,0:T(8,128)}, s32[]{:T(128)}) while((s32[]{:T(128)}, f32[2,768,768]{1,2,0:T(8,128)}, s32[]{:T(128)}) %tuple.34), condition=%wide.region_5.0_spmd, body=%wide.region_4.0_spmd.sunk | while | flops 32620806144 | bytes 80216168 | solution.py:89
  369.7 15.5 %fusion.53 = f32[2,768,768]{2,1,0:T(8,128)S(1)} fusion(f32[2,768,768]{1,2,0:T(8,128)} %get-tuple-element.89), kind=kOutput, calls=%fused_computation.48.clone.1 | convolution fusion | flops 10871635968 | bytes 9437184 | tf_op jit(solution)/shard_map/while/body/eval_jaxpr/bki,bkj->bij/dot_general | solution.py:16
  385.3 14.0 %fusion.54 = f32[2,768,768]{2,1,0:T(8,128)S(1)} fusion(f32[2,768,768]{2,1,0:T(8,128)S(1)} %fusion.53, f32[2,768,768]{1,2,0:T(8,128)S(1)} %copy-done), kind=kOutput, calls=%fused_computation.49.clone.1 | convolution fusion | flops 10871635968 | bytes 14155776 | tf_op jit(solution)/shard_map/while/body/eval_jaxpr/bik,bkj->bij/dot_general | solution.py:20
  399.3 15.6 %fusion.55 = f32[2,768,768]{1,2,0:T(8,128)S(1)} fusion(f32[2,768,768]{2,1,0:T(8,128)S(1)} %fusion.54, f32[2,768,768]{1,2,0:T(8,128)S(1)} %copy-done, f32[2,768,768]{2,1,0:T(8,128)S(1)} %fusion.53), kind=kOutput, calls=%fused_computation.1.clone.1 | convolution fusion | flops 10877534208 | bytes 18874368 | tf_op jit(solution)/shard_map/while/body/eval_jaxpr/bik,bkj->bij/dot_general | solution.py:21
  414.9 2.1 copy-done.1
  417.0 15.5 %fusion.53 = f32[2,768,768]{2,1,0:T(8,128)S(1)} fusion(f32[2,768,768]{1,2,0:T(8,128)} %get-tuple-element.89), kind=kOutput, calls=%fused_computation.48.clone.1 | convolution fusion | flops 10871635968 | bytes 9437184 | tf_op jit(solution)/shard_map/while/body/eval_jaxpr/bki,bkj->bij/dot_general | solution.py:16
  432.6 14.0 %fusion.54 = f32[2,768,768]{2,1,0:T(8,128)S(1)} fusion(f32[2,768,768]{2,1,0:T(8,128)S(1)} %fusion.53, f32[2,768,768]{1,2,0:T(8,128)S(1)} %copy-done), kind=kOutput, calls=%fused_computation.49.clone.1 | convolution fusion | flops 10871635968 | bytes 14155776 | tf_op jit(solution)/shard_map/while/body/eval_jaxpr/bik,bkj->bij/dot_general | solution.py:20
  446.5 15.6 %fusion.55 = f32[2,768,768]{1,2,0:T(8,128)S(1)} fusion(f32[2,768,768]{2,1,0:T(8,128)S(1)} %fusion.54, f32[2,768,768]{1,2,0:T(8,128)S(1)} %copy-done, f32[2,768,768]{2,1,0:T(8,128)S(1)} %fusion.53), kind=kOutput, calls=%fused_computation.1.clone.1 | convolution fusion | flops 10877534208 | bytes 18874368 | tf_op jit(solution)/shard_map/while/body/eval_jaxpr/bik,bkj->bij/dot_general | solution.py:21
  462.2 2.1 copy-done.1
  464.3 15.5 %fusion.53 = f32[2,768,768]{2,1,0:T(8,128)S(1)} fusion(f32[2,768,768]{1,2,0:T(8,128)} %get-tuple-element.89), kind=kOutput, calls=%fused_computation.48.clone.1 | convolution fusion | flops 10871635968 | bytes 9437184 | tf_op jit(solution)/shard_map/while/body/eval_jaxpr/bki,bkj->bij/dot_general | solution.py:16
  479.8 14.0 %fusion.54 = f32[2,768,768]{2,1,0:T(8,128)S(1)} fusion(f32[2,768,768]{2,1,0:T(8,128)S(1)} %fusion.53, f32[2,768,768]{1,2,0:T(8,128)S(1)} %copy-done), kind=kOutput, calls=%fused_computation.49.clone.1 | convolution fusion | flops 10871635968 | bytes 14155776 | tf_op jit(solution)/shard_map/while/body/eval_jaxpr/bik,bkj->bij/dot_general | solution.py:20
  493.8 15.6 %fusion.55 = f32[2,768,768]{1,2,0:T(8,128)S(1)} fusion(f32[2,768,768]{2,1,0:T(8,128)S(1)} %fusion.54, f32[2,768,768]{1,2,0:T(8,128)S(1)} %copy-done, f32[2,768,768]{2,1,0:T(8,128)S(1)} %fusion.53), kind=kOutput, calls=%fused_computation.1.clone.1 | convolution fusion | flops 10877534208 | bytes 18874368 | tf_op jit(solution)/shard_map/while/body/eval_jaxpr/bik,bkj->bij/dot_general | solution.py:21
  509.5 2.1 copy-done.1
  511.6 6.1 %copy.48 = f32[2,768,768]{2,1,0:T(8,128)} copy(f32[2,768,768]{1,2,0:T(8,128)} %get-tuple-element.24) | data formatting | bytes 9437184 | tf_op jit(solution)/shard_map/while | solution.py:89
  517.7 4.9 slice_bitcast_fusion
  (60 shorter events, 10.0 us)
Async XLA Ops:
  7.2 44.8 %copy-start.14 = (f32[192,64]{0,1:T(8,128)S(1)}, f32[192,64]{0,1:T(8,128)}, u32[]{:S(2)}) copy-start(f32[192,64]{0,1:T(8,128)} %param.22) | copy-start | bytes 147460
  7.2 87.6 %copy-start.9 = (f32[1,768,64]{1,2,0:T(8,128)S(1)}, f32[1,768,64]{1,2,0:T(8,128)}, u32[]{:S(2)}) copy-start(f32[1,768,64]{1,2,0:T(8,128)} %param.17) | copy-start | bytes 589828
  7.2 44.7 %reduce-scatter.6.cloned.1.call-start = ((), (), s32[]{:S(2)}) async-start(), calls=%async_computation.4 | async-start | bytes 589824 | tf_op jit(solution)/shard_map/reduce_scatter | solution.py:45
  9.2 85.6 %reduce-scatter.4.cloned.1.call-start = ((), (), s32[]{:S(2)}) async-start(), calls=%async_computation.3 | async-start | bytes 1769472 | tf_op jit(solution)/shard_map/reduce_scatter | solution.py:44
  12.0 230.8 %reduce-scatter.8.cloned.1.call-start = ((), (), s32[]{:S(2)}) async-start(), calls=%async_computation.5 | async-start | bytes 4866048 | tf_op jit(solution)/shard_map/reduce_scatter | solution.py:79
  52.8 195.6 %copy-start.6 = (f32[192,64]{0,1:T(8,128)}, f32[192,64]{0,1:T(8,128)S(1)}, u32[]{:S(2)}) copy-start(f32[192,64]{0,1:T(8,128)S(1)} %get-tuple-element.71) | copy-start | bytes 147460
  95.8 165.8 %copy-start.5 = (f32[1,768,64]{1,2,0:T(8,128)}, f32[1,768,64]{1,2,0:T(8,128)S(1)}, u32[]{:S(2)}) copy-start(f32[1,768,64]{1,2,0:T(8,128)S(1)} %get-tuple-element.67) | copy-start | bytes 589828
  95.8 146.9 %copy-start.11 = (f32[24,768]{1,0:T(8,128)S(1)}, f32[24,768]{1,0:T(8,128)}, u32[]{:S(2)}) copy-start(f32[24,768]{1,0:T(8,128)} %param.24) | copy-start | bytes 221188
  95.8 146.9 %copy-start.12 = (f32[1,24,768]{2,1,0:T(8,128)S(1)}, f32[1,24,768]{2,1,0:T(8,128)}, u32[]{:S(2)}) copy-start(f32[1,24,768]{2,1,0:T(8,128)} %param.19) | copy-start | bytes 221188
  95.8 147.8 %copy-start.3 = (f32[768,768]{1,0:T(8,128)S(1)}, f32[768,768]{1,0:T(8,128)}, u32[]{:S(2)}) copy-start(f32[768,768]{1,0:T(8,128)} %param.25) | copy-start | bytes 7077892
  101.4 233.3 %all-gather.4.cloned.1.call-start = ((), (), s32[]{:S(2)}) async-start(), calls=%async_computation.6 | async-start | bytes 4866048 | tf_op jit(solution)/shard_map/all_gather | solution.py:83
  261.6 4.6 copy-start.7
  261.6 4.6 copy-start.8
  261.6 4.7 copy-start.4
  266.2 4.9 copy-start.10
  266.3 36.9 %copy-start.13 = (f32[192,64]{0,1:T(8,128)S(1)}, f32[192,64]{0,1:T(8,128)}, u32[]{:S(2)}) copy-start(f32[192,64]{0,1:T(8,128)} %param.21) | copy-start | bytes 147460
  334.7 3.8 copy-start.2
  369.7 15.5 %copy-start = (f32[2,768,768]{1,2,0:T(8,128)S(1)}, f32[2,768,768]{1,2,0:T(8,128)}, u32[]{:S(2)}) copy-start(f32[2,768,768]{1,2,0:T(8,128)} %get-tuple-element.89) | copy-start | bytes 14155780 | tf_op jit(solution)/shard_map/while
  414.9 2.1 copy-start.1
  417.0 15.5 %copy-start = (f32[2,768,768]{1,2,0:T(8,128)S(1)}, f32[2,768,768]{1,2,0:T(8,128)}, u32[]{:S(2)}) copy-start(f32[2,768,768]{1,2,0:T(8,128)} %get-tuple-element.89) | copy-start | bytes 14155780 | tf_op jit(solution)/shard_map/while
  462.2 2.1 copy-start.1
  464.3 15.5 %copy-start = (f32[2,768,768]{1,2,0:T(8,128)S(1)}, f32[2,768,768]{1,2,0:T(8,128)}, u32[]{:S(2)}) copy-start(f32[2,768,768]{1,2,0:T(8,128)} %get-tuple-element.89) | copy-start | bytes 14155780 | tf_op jit(solution)/shard_map/while
  509.5 2.1 copy-start.1
Sparse Core Ops, SparseCore 0:
  10.9 40.9 reduce-scatter.5
  54.9 39.8 reduce-scatter.3
  101.6 141.1 reduce-scatter.7
  248.5 84.4 all-gather.3

commit v2 on v1

--- a/solution.py
+++ b/solution.py
@@ -7,18 +7,19 @@
 
 
 HIGHEST = lax.Precision.HIGHEST
+HIGH = lax.Precision.HIGH
 linear_coef = 3.4445
 cubic_coef = -4.775
 quintic_coef = 2.0315
 
 
 def local_gram(current):
-    return jnp.einsum("bki,bkj->bij", current, current, precision=HIGHEST)
+    return jnp.einsum("bki,bkj->bij", current, current, precision=HIGH)
 
 
 def quintic_step(current, gram_matrix):
-    first_prod = jnp.einsum("bik,bkj->bij", current, gram_matrix, precision=HIGHEST)
-    second_prod = jnp.einsum("bik,bkj->bij", first_prod, gram_matrix, precision=HIGHEST)
+    first_prod = jnp.einsum("bik,bkj->bij", current, gram_matrix, precision=HIGH)
+    second_prod = jnp.einsum("bik,bkj->bij", first_prod, gram_matrix, precision=HIGH)
     return linear_coef * current + cubic_coef * first_prod + quintic_coef * second_prod
 
 
@@ -79,7 +80,7 @@
     summed = lax.psum_scatter(partial_stat, ("tensor", "dp"), scatter_dimension=2, tiled=True)
     stats_all = jnp.concatenate([expert_stat, dense_stat[None]], 0)
     stats_out = 0.95 * stats_all + 0.05 * jnp.transpose(summed, (0, 2, 1))
-    power_rows = jnp.einsum("bik,bkj->bij", stats_out, bases_all, precision=HIGHEST)
+    power_rows = jnp.einsum("bik,bkj->bij", stats_out, bases_all, precision=HIGH)
     power = lax.all_gather(power_rows, ("tensor", "dp"), axis=1, tiled=True)
     square_sum = jnp.sum(power * power, (1, 2))
     current = power * lax.rsqrt(square_sum + 1e-06)[:, None, None]

time: 535 us -> 449 us (0.84); the launches traced: 529 us -> 449 us
  matrix products: 155 us -> 97 us
  loops' own time: 22.7 us -> 0.11 us
    dot_general x10, matrix products: 140 us -> 82.1 us  [the longest x3 29.2 us: local_gram(): return jnp.einsum('bki,bkj->bij', current, current, precision=HIGH)]
    another operation x1, loops' own time: 22.7 us -> 0.11 us  [shards(): current = lax.fori_loop(0, NS_ITERS, ns_iteration, current)]
  transfers between devices with their start and end apart: 4 -> 4, of which waited for: 3 -> 3; matrix products, arithmetic and copies ran while one was open for 3% -> 4% of each run, Pallas kernels for 0% -> 0%
where the time goes in v2:
time: 449 us
  waiting for transfers between devices  211 us (47%)
  matrix products  97 us (22%)
  blocking collectives  84.3 us (19%)
  local copies, waits for them, and re-layouts  30.7 us (7%)
  between operations  14 us (3%)
  other arithmetic  12.1 us (3%)
    reduce_scatter x1, waiting for transfers between devices, shards(): lax.psum_scatter(partial_stat, ('tensor', 'dp'), scatter_dimension=2, til...  142 us
    reduce_scatter x1, waiting for transfers between devices, shards(): lax.psum_scatter(dense_local, 'dp', scatter_dimension=1, tiled=True)  39.9 us
    all_gather x1, blocking collectives, shards(): lax.all_gather(expert_master_out.astype(jnp.bfloat16), 'dp', axis=2, tile...  30.4 us
    dot_general x3, matrix products, local_gram(): return jnp.einsum('bki,bkj->bij', current, current, precision=HIGH)  29.2 us
    reduce_scatter x1, waiting for transfers between devices, shards(): lax.psum_scatter(expert_local, 'dp', scatter_dimension=2, tiled=True)  29.1 us
    all_gather x1, blocking collectives, shards(): lax.all_gather(dense_master_out.astype(jnp.bfloat16), 'dp', axis=1, tiled...  28.7 us
    dot_general x3, matrix products, quintic_step(): jnp.einsum('bik,bkj->bij', first_prod, gram_matrix, precision=HIGH)  27.2 us
    dot_general x3, matrix products, quintic_step(): jnp.einsum('bik,bkj->bij', current, gram_matrix, precision=HIGH)  22 us
  transfers between devices with their start and end apart: 4, of which 3 were waited for; matrix products, arithmetic and copies ran while one was open for 4% of the time, Pallas kernels for 0%

profile of v2, /device:TPU:0, one launch (start us, length us, event | category | flops | bytes accessed | tf_op | source)
XLA Modules:
  0.0 449.0 jit_solution(6278986490455268092)
XLA Ops:
  9.3 1.4 copy.43
  10.7 1.3 bitcast_convert_fusion
  12.0 39.9 %reduce-scatter.6.cloned.1.call-done = f32[192,64]{0,1:T(8,128)} async-done(((f32[192,512]{0,1:T(8,128)}), f32[192,64]{0,1:T(8,128)}) %reduce-scatter.6.cloned.1.call-update) | async-done | bytes 49168 | tf_op jit(solution)/shard_map/reduce_scatter | solution.py:46
  52.8 12.6 %all-gather = f32[4,192,64]{1,2,0:T(8,128)S(1)} all-gather(f32[1,192,64]{1,2,0:T(8,128)S(1)} %get-tuple-element.70), channel_id=1, replica_groups=mesh['dp'=8,'wshard'=4,'tensor'=4] {'wshard'}, dimensions={0}, use_global_device_ids=true | all-gather | bytes 245760 | tf_op jit(solution)/shard_map/all_gather | solution.py:53
  65.7 29.1 %reduce-scatter.4.cloned.1.call-done = f32[1,768,64]{1,2,0:T(8,128)} async-done(((f32[1,768,512]{1,2,0:T(8,128)}), f32[1,768,64]{1,2,0:T(8,128)}) %reduce-scatter.4.cloned.1.call-update) | async-done | bytes 196624 | tf_op jit(solution)/shard_map/reduce_scatter | solution.py:45
  95.9 5.6 %fusion.12 = f32[2,768,768]{1,2,0:T(8,128)} fusion(f32[1,768,64]{1,2,0:T(8,128)S(1)} %broadcast_in_dim.17, f32[1,768,64]{1,2,0:T(8,128)S(1)} %get-tuple-element.66), kind=kOutput, calls=%fused_computation.20 | convolution fusion | flops 906067968 | bytes 5111808 | tf_op jit(solution)/shard_map/bic,bjc->bji/dot_general | solution.py:79
  101.5 141.6 %reduce-scatter.8.cloned.1.call-done = f32[2,768,24]{1,2,0:T(8,128)} async-done(((f32[2,768,768]{1,2,0:T(8,128)}), f32[2,768,24]{1,2,0:T(8,128)}) %reduce-scatter.8.cloned.1.call-update) | async-done | bytes 147472 | tf_op jit(solution)/shard_map/reduce_scatter | solution.py:80
  244.0 3.6 fusion.1
  247.7 12.6 %all-gather.1 = f32[4,192,64]{1,2,0:T(8,128)S(1)} all-gather(f32[1,192,64]{1,2,0:T(8,128)S(1)} %bitcast.55), channel_id=1, replica_groups=mesh['dp'=8,'wshard'=4,'tensor'=4] {'wshard'}, dimensions={0}, use_global_device_ids=true | all-gather | bytes 245760 | tf_op jit(solution)/shard_map/all_gather | solution.py:54
  260.8 4.6 %fusion.3 = f32[2,768,128]{1,2,0:T(8,128)S(1)} fusion(f32[1,768,768]{2,1,0:T(8,128)S(1)} %bitcast.53, f32[1,768,768]{2,1,0:T(8,128)} %param.20, f32[1,768,64]{1,2,0:T(8,128)S(1)} %broadcast_in_dim.18, f32[1,768,64]{1,2,0:T(8,128)S(1)} %get-tuple-element.67, f32[1,768,64]{1,2,0:T(8,128)S(1)} %broadcast_in_dim.17, f32[1,768,64]{1,2,0:T(8,128)S(1)} %get-tuple-element.66), kind=kOutput, calls=%fused_computation.6 | convolution fusion | flops 1813708800 | bytes 6291456 | tf_op jit(solution)/shard_map/bki,bkc->bic/dot_general | solution.py:61
  265.5 4.8 %fusion.2 = f32[2,768,64]{1,2,0:T(8,128)S(1)} fusion(f32[1,768,768]{2,1,0:T(8,128)S(1)} %bitcast.54, f32[1,768,768]{2,1,0:T(8,128)S(1)} %copy-done.4, f32[2,768,128]{1,2,0:T(8,128)S(1)} %fusion.3, f32[2,768,64]{1,2,0:T(8,128)S(1)} %fusion.11), kind=kOutput, calls=%fused_computation.5 | convolution fusion | flops 907345920 | bytes 5898240 | tf_op jit(solution)/shard_map/bik,bkc->bic/dot_general | solution.py:68
  271.0 30.4 %all_gather.18 = bf16[1,768,512]{1,2,0:T(8,128)(2,1)S(1)} all-gather(bf16[1,768,64]{1,2,0:T(8,128)(2,1)S(1)} %get-tuple-element.59), channel_id=1, replica_groups=mesh['dp'=8,'wshard'=4,'tensor'=4] {'dp'}, dimensions={2}, use_global_device_ids=true | all-gather | bytes 884736 | tf_op jit(solution)/shard_map/all_gather | solution.py:76
  301.3 1.2 copy.50
  303.2 28.7 %all_gather.19 = bf16[192,512]{0,1:T(8,128)(2,1)S(1)} all-gather(bf16[192,64]{0,1:T(8,128)(2,1)S(1)} %get-tuple-element.57), channel_id=1, replica_groups=mesh['dp'=8,'wshard'=4,'tensor'=4] {'dp'}, dimensions={1}, use_global_device_ids=true | all-gather | bytes 221184 | tf_op jit(solution)/shard_map/all_gather | solution.py:77
  334.2 3.2 multiply_reduce_fusion
  337.9 2.6 broadcast_multiply_fusion
  340.5 6.1 %copy.47 = f32[2,768,768]{1,2,0:T(8,128)} copy(f32[2,768,768]{2,1,0:T(8,128)} %broadcast_multiply_fusion) | data formatting | bytes 9437184 | tf_op jit(solution)/shard_map/while | solution.py:90
  346.6 85.0 %while.10 = (s32[]{:T(128)}, f32[2,768,768]{1,2,0:T(8,128)}, s32[]{:T(128)}) while((s32[]{:T(128)}, f32[2,768,768]{1,2,0:T(8,128)}, s32[]{:T(128)}) %tuple.34), condition=%wide.region_5.0_spmd, body=%wide.region_4.0_spmd.sunk | while | flops 16313352192 | bytes 80216168 | solution.py:90
  346.6 9.7 %fusion.53 = f32[2,768,768]{2,1,0:T(8,128)S(1)} fusion(f32[2,768,768]{1,2,0:T(8,128)} %get-tuple-element.89), kind=kOutput, calls=%fused_computation.48.clone.1 | convolution fusion | flops 5435817984 | bytes 9437184 | tf_op jit(solution)/shard_map/while/body/eval_jaxpr/bki,bkj->bij/dot_general | solution.py:17
  356.3 7.3 %fusion.54 = f32[2,768,768]{2,1,0:T(8,128)S(1)} fusion(f32[2,768,768]{2,1,0:T(8,128)S(1)} %fusion.53, f32[2,768,768]{1,2,0:T(8,128)S(1)} %copy-done), kind=kOutput, calls=%fused_computation.49.clone.1 | convolution fusion | flops 5435817984 | bytes 14155776 | tf_op jit(solution)/shard_map/while/body/eval_jaxpr/bik,bkj->bij/dot_general | solution.py:21
  363.6 9.1 %fusion.55 = f32[2,768,768]{1,2,0:T(8,128)S(1)} fusion(f32[2,768,768]{2,1,0:T(8,128)S(1)} %fusion.54, f32[2,768,768]{1,2,0:T(8,128)S(1)} %copy-done, f32[2,768,768]{2,1,0:T(8,128)S(1)} %fusion.53), kind=kOutput, calls=%fused_computation.1.clone.1 | convolution fusion | flops 5441716224 | bytes 18874368 | tf_op jit(solution)/shard_map/while/body/eval_jaxpr/bik,bkj->bij/dot_general | solution.py:22
  372.7 2.1 copy-done.1
  374.9 9.7 %fusion.53 = f32[2,768,768]{2,1,0:T(8,128)S(1)} fusion(f32[2,768,768]{1,2,0:T(8,128)} %get-tuple-element.89), kind=kOutput, calls=%fused_computation.48.clone.1 | convolution fusion | flops 5435817984 | bytes 9437184 | tf_op jit(solution)/shard_map/while/body/eval_jaxpr/bki,bkj->bij/dot_general | solution.py:17
  384.6 7.3 %fusion.54 = f32[2,768,768]{2,1,0:T(8,128)S(1)} fusion(f32[2,768,768]{2,1,0:T(8,128)S(1)} %fusion.53, f32[2,768,768]{1,2,0:T(8,128)S(1)} %copy-done), kind=kOutput, calls=%fused_computation.49.clone.1 | convolution fusion | flops 5435817984 | bytes 14155776 | tf_op jit(solution)/shard_map/while/body/eval_jaxpr/bik,bkj->bij/dot_general | solution.py:21
  392.0 9.1 %fusion.55 = f32[2,768,768]{1,2,0:T(8,128)S(1)} fusion(f32[2,768,768]{2,1,0:T(8,128)S(1)} %fusion.54, f32[2,768,768]{1,2,0:T(8,128)S(1)} %copy-done, f32[2,768,768]{2,1,0:T(8,128)S(1)} %fusion.53), kind=kOutput, calls=%fused_computation.1.clone.1 | convolution fusion | flops 5441716224 | bytes 18874368 | tf_op jit(solution)/shard_map/while/body/eval_jaxpr/bik,bkj->bij/dot_general | solution.py:22
  401.1 2.1 copy-done.1
  403.2 9.7 %fusion.53 = f32[2,768,768]{2,1,0:T(8,128)S(1)} fusion(f32[2,768,768]{1,2,0:T(8,128)} %get-tuple-element.89), kind=kOutput, calls=%fused_computation.48.clone.1 | convolution fusion | flops 5435817984 | bytes 9437184 | tf_op jit(solution)/shard_map/while/body/eval_jaxpr/bki,bkj->bij/dot_general | solution.py:17
  412.9 7.3 %fusion.54 = f32[2,768,768]{2,1,0:T(8,128)S(1)} fusion(f32[2,768,768]{2,1,0:T(8,128)S(1)} %fusion.53, f32[2,768,768]{1,2,0:T(8,128)S(1)} %copy-done), kind=kOutput, calls=%fused_computation.49.clone.1 | convolution fusion | flops 5435817984 | bytes 14155776 | tf_op jit(solution)/shard_map/while/body/eval_jaxpr/bik,bkj->bij/dot_general | solution.py:21
  420.3 9.1 %fusion.55 = f32[2,768,768]{1,2,0:T(8,128)S(1)} fusion(f32[2,768,768]{2,1,0:T(8,128)S(1)} %fusion.54, f32[2,768,768]{1,2,0:T(8,128)S(1)} %copy-done, f32[2,768,768]{2,1,0:T(8,128)S(1)} %fusion.53), kind=kOutput, calls=%fused_computation.1.clone.1 | convolution fusion | flops 5441716224 | bytes 18874368 | tf_op jit(solution)/shard_map/while/body/eval_jaxpr/bik,bkj->bij/dot_general | solution.py:22
  429.4 2.1 copy-done.1
  431.5 6.1 %copy.48 = f32[2,768,768]{2,1,0:T(8,128)} copy(f32[2,768,768]{1,2,0:T(8,128)} %get-tuple-element.24) | data formatting | bytes 9437184 | tf_op jit(solution)/shard_map/while | solution.py:90
  437.6 4.9 %slice_bitcast_fusion = (f32[768,768]{1,0:T(8,128)}, f32[1,768,768]{2,1,0:T(8,128)}) fusion(f32[2,768,768]{2,1,0:T(8,128)} %copy.48), kind=kLoop, calls=%fused_computation.7 | loop fusion | bytes 9437184 | tf_op jit(solution)/shard_map/squeeze | solution.py:103
  (60 shorter events, 10.0 us)
Async XLA Ops:
  7.2 44.8 %copy-start.14 = (f32[192,64]{0,1:T(8,128)S(1)}, f32[192,64]{0,1:T(8,128)}, u32[]{:S(2)}) copy-start(f32[192,64]{0,1:T(8,128)} %param.22) | copy-start | bytes 147460
  7.2 87.6 %copy-start.9 = (f32[1,768,64]{1,2,0:T(8,128)S(1)}, f32[1,768,64]{1,2,0:T(8,128)}, u32[]{:S(2)}) copy-start(f32[1,768,64]{1,2,0:T(8,128)} %param.17) | copy-start | bytes 589828
  7.2 44.7 %reduce-scatter.6.cloned.1.call-start = ((), (), s32[]{:S(2)}) async-start(), calls=%async_computation.4 | async-start | bytes 589824 | tf_op jit(solution)/shard_map/reduce_scatter | solution.py:46
  9.2 85.6 %reduce-scatter.4.cloned.1.call-start = ((), (), s32[]{:S(2)}) async-start(), calls=%async_computation.3 | async-start | bytes 1769472 | tf_op jit(solution)/shard_map/reduce_scatter | solution.py:45
  12.0 231.1 %reduce-scatter.8.cloned.1.call-start = ((), (), s32[]{:S(2)}) async-start(), calls=%async_computation.5 | async-start | bytes 4866048 | tf_op jit(solution)/shard_map/reduce_scatter | solution.py:80
  52.8 194.9 %copy-start.6 = (f32[192,64]{0,1:T(8,128)}, f32[192,64]{0,1:T(8,128)S(1)}, u32[]{:S(2)}) copy-start(f32[192,64]{0,1:T(8,128)S(1)} %get-tuple-element.71) | copy-start | bytes 147460
  95.8 164.9 %copy-start.5 = (f32[1,768,64]{1,2,0:T(8,128)}, f32[1,768,64]{1,2,0:T(8,128)S(1)}, u32[]{:S(2)}) copy-start(f32[1,768,64]{1,2,0:T(8,128)S(1)} %get-tuple-element.67) | copy-start | bytes 589828
  95.8 147.3 %copy-start.11 = (f32[24,768]{1,0:T(8,128)S(1)}, f32[24,768]{1,0:T(8,128)}, u32[]{:S(2)}) copy-start(f32[24,768]{1,0:T(8,128)} %param.24) | copy-start | bytes 221188
  95.8 147.3 %copy-start.12 = (f32[1,24,768]{2,1,0:T(8,128)S(1)}, f32[1,24,768]{2,1,0:T(8,128)}, u32[]{:S(2)}) copy-start(f32[1,24,768]{2,1,0:T(8,128)} %param.19) | copy-start | bytes 221188
  95.8 148.2 %copy-start.3 = (f32[768,768]{1,0:T(8,128)S(1)}, f32[768,768]{1,0:T(8,128)}, u32[]{:S(2)}) copy-start(f32[768,768]{1,0:T(8,128)} %param.25) | copy-start | bytes 7077892
  101.5 232.7 %all-gather.4.cloned.1.call-start = ((), (), s32[]{:S(2)}) async-start(), calls=%async_computation.6 | async-start | bytes 4866048 | tf_op jit(solution)/shard_map/all_gather | solution.py:84
  260.7 4.6 %copy-start.7 = (f32[768,64]{0,1:T(8,128)S(1)}, f32[768,64]{0,1:T(8,128)}, u32[]{:S(2)}) copy-start(f32[768,64]{0,1:T(8,128)} %param.23) | copy-start | bytes 589828
  260.7 4.6 %copy-start.8 = (f32[1,768,64]{1,2,0:T(8,128)S(1)}, f32[1,768,64]{1,2,0:T(8,128)}, u32[]{:S(2)}) copy-start(f32[1,768,64]{1,2,0:T(8,128)} %param.18) | copy-start | bytes 589828
  260.7 4.7 %copy-start.4 = (f32[1,768,768]{2,1,0:T(8,128)S(1)}, f32[1,768,768]{2,1,0:T(8,128)}, u32[]{:S(2)}) copy-start(f32[1,768,768]{2,1,0:T(8,128)} %param.20) | copy-start | bytes 7077892
  265.3 4.9 %copy-start.10 = (f32[1,768,64]{1,2,0:T(8,128)S(1)}, f32[1,768,64]{1,2,0:T(8,128)}, u32[]{:S(2)}) copy-start(f32[1,768,64]{1,2,0:T(8,128)} %param.16) | copy-start | bytes 589828
  265.4 37.0 %copy-start.13 = (f32[192,64]{0,1:T(8,128)S(1)}, f32[192,64]{0,1:T(8,128)}, u32[]{:S(2)}) copy-start(f32[192,64]{0,1:T(8,128)} %param.21) | copy-start | bytes 147460
  334.2 3.8 copy-start.2
  346.6 9.7 %copy-start = (f32[2,768,768]{1,2,0:T(8,128)S(1)}, f32[2,768,768]{1,2,0:T(8,128)}, u32[]{:S(2)}) copy-start(f32[2,768,768]{1,2,0:T(8,128)} %get-tuple-element.89) | copy-start | bytes 14155780 | tf_op jit(solution)/shard_map/while
  372.7 2.1 copy-start.1
  374.9 9.7 %copy-start = (f32[2,768,768]{1,2,0:T(8,128)S(1)}, f32[2,768,768]{1,2,0:T(8,128)}, u32[]{:S(2)}) copy-start(f32[2,768,768]{1,2,0:T(8,128)} %get-tuple-element.89) | copy-start | bytes 14155780 | tf_op jit(solution)/shard_map/while
  401.1 2.1 copy-start.1
  403.2 9.7 %copy-start = (f32[2,768,768]{1,2,0:T(8,128)S(1)}, f32[2,768,768]{1,2,0:T(8,128)}, u32[]{:S(2)}) copy-start(f32[2,768,768]{1,2,0:T(8,128)} %get-tuple-element.89) | copy-start | bytes 14155780 | tf_op jit(solution)/shard_map/while
  429.4 2.1 copy-start.1
Sparse Core Ops, SparseCore 0:
  10.9 40.9 reduce-scatter.5
  54.9 39.8 reduce-scatter.3
  101.6 141.4 reduce-scatter.7
  247.8 83.9 all-gather.3

commit v3 on v2

--- a/solution.py
+++ b/solution.py
@@ -76,12 +76,16 @@
         lax.all_gather(expert_master_out.astype(jnp.bfloat16), "dp", axis=2, tiled=True),
         lax.all_gather(dense_master_out.astype(jnp.bfloat16), "dp", axis=1, tiled=True),
     )
-    partial_stat = jnp.einsum("bic,bjc->bji", grads_all, grads_all, precision=HIGHEST)
-    summed = lax.psum_scatter(partial_stat, ("tensor", "dp"), scatter_dimension=2, tiled=True)
+    partial_stat = jnp.einsum("bic,bjc->bij", grads_all, grads_all, precision=HIGHEST)
     stats_all = jnp.concatenate([expert_stat, dense_stat[None]], 0)
-    stats_out = 0.95 * stats_all + 0.05 * jnp.transpose(summed, (0, 2, 1))
-    power_rows = jnp.einsum("bik,bkj->bij", stats_out, bases_all, precision=HIGH)
-    power = lax.all_gather(power_rows, ("tensor", "dp"), axis=1, tiled=True)
+    stat_rows = stats_all.shape[1]
+    row_start = lax.axis_index(("tensor", "dp")) * stat_rows
+    placed = lax.dynamic_update_slice_in_dim(
+        jnp.zeros_like(partial_stat), 0.95 * stats_all, row_start, 1
+    )
+    stats_full = lax.psum(placed + 0.05 * partial_stat, ("tensor", "dp"))
+    stats_out = lax.dynamic_slice_in_dim(stats_full, row_start, stat_rows, 1)
+    power = jnp.einsum("bik,bkj->bij", stats_full, bases_all, precision=HIGH)
     square_sum = jnp.sum(power * power, (1, 2))
     current = power * lax.rsqrt(square_sum + 1e-06)[:, None, None]
     def ns_iteration(repeat, current):

time: 449 us -> 340 us (0.76)
  waiting for transfers between devices: 211 us -> 96 us
  matrix products: 97 us -> 103 us
    reduce_scatter x1 -> x0, waiting for transfers between devices: 142 us -> none  [shards(): lax.psum_scatter(partial_stat, ('tensor', 'dp'), scatter_dimension=2, til...]
    psum x0 -> x1, waiting for transfers between devices: none -> 26.9 us  [shards(): stats_full = lax.psum(placed + 0.05 * partial_stat, ('tensor', 'dp'))]
    dot_general x2, matrix products: 9.2 us -> 15 us  [the longest x1 9.35 us: shards(): power = jnp.einsum('bik,bkj->bij', stats_full, bases_all, precision=HIGH)]
  transfers between devices with their start and end apart: 4 -> 3, of which waited for: 3 -> 3; matrix products, arithmetic and copies ran while one was open for 4% -> 6% of each run, Pallas kernels for 0% -> 0%
where the time goes in v3:
time: 340 us; the launch traced here: 339 us
  matrix products  103 us (30%)
  waiting for transfers between devices  96 us (28%)
  blocking collectives  84.2 us (25%)
  local copies, waits for them, and re-layouts  31.1 us (9%)
  between operations  14 us (4%)
  other arithmetic  10.6 us (3%)
    reduce_scatter x1, waiting for transfers between devices, shards(): lax.psum_scatter(dense_local, 'dp', scatter_dimension=1, tiled=True)  39.9 us
    all_gather x1, blocking collectives, shards(): lax.all_gather(expert_master_out.astype(jnp.bfloat16), 'dp', axis=2, tile...  30.3 us
    dot_general x3, matrix products, local_gram(): return jnp.einsum('bki,bkj->bij', current, current, precision=HIGH)  29.5 us
    reduce_scatter x1, waiting for transfers between devices, shards(): lax.psum_scatter(expert_local, 'dp', scatter_dimension=2, tiled=True)  29.1 us
    all_gather x1, blocking collectives, shards(): lax.all_gather(dense_master_out.astype(jnp.bfloat16), 'dp', axis=1, tiled...  28.8 us
    dot_general x3, matrix products, quintic_step(): jnp.einsum('bik,bkj->bij', first_prod, gram_matrix, precision=HIGH)  27.2 us
    psum x1, waiting for transfers between devices, shards(): stats_full = lax.psum(placed + 0.05 * partial_stat, ('tensor', 'dp'))  26.9 us
    dot_general x3, matrix products, quintic_step(): jnp.einsum('bik,bkj->bij', current, gram_matrix, precision=HIGH)  22 us
  transfers between devices with their start and end apart: 3, of which 3 were waited for; matrix products, arithmetic and copies ran while one was open for 6% of the time, Pallas kernels for 0%

profile of v3, /device:TPU:0, one launch (start us, length us, event | category | flops | bytes accessed | tf_op | source)
XLA Modules:
  0.0 339.1 jit_solution(16449666936567062266)
XLA Ops:
  9.3 1.4 copy.43
  12.0 39.9 %reduce-scatter.5.cloned.1.call-done = f32[192,64]{0,1:T(8,128)} async-done(((f32[192,512]{0,1:T(8,128)}), f32[192,64]{0,1:T(8,128)}) %reduce-scatter.5.cloned.1.call-update) | async-done | bytes 49168 | tf_op jit(solution)/shard_map/reduce_scatter | solution.py:46
  52.8 12.6 %all-gather = f32[4,192,64]{1,2,0:T(8,128)S(1)} all-gather(f32[1,192,64]{1,2,0:T(8,128)S(1)} %get-tuple-element.70), channel_id=1, replica_groups=mesh['dp'=8,'wshard'=4,'tensor'=4] {'wshard'}, dimensions={0}, use_global_device_ids=true | all-gather | bytes 245760 | tf_op jit(solution)/shard_map/all_gather | solution.py:53
  65.7 29.1 %reduce-scatter.3.cloned.1.call-done = f32[1,768,64]{1,2,0:T(8,128)} async-done(((f32[1,768,512]{1,2,0:T(8,128)}), f32[1,768,64]{1,2,0:T(8,128)}) %reduce-scatter.3.cloned.1.call-update) | async-done | bytes 196624 | tf_op jit(solution)/shard_map/reduce_scatter | solution.py:45
  95.8 5.6 %broadcast_multiply_fusion.1 = f32[2,768,768]{2,1,0:T(8,128)} fusion(f32[1,768,64]{1,2,0:T(8,128)S(1)} %broadcast_in_dim.18, f32[1,768,64]{1,2,0:T(8,128)S(1)} %get-tuple-element.68), kind=kOutput, calls=%fused_computation.9 | convolution fusion | flops 907247616 | bytes 5111808 | tf_op jit(solution)/shard_map/bic,bjc->bij/dot_general | solution.py:79
  101.5 1.6 fusion.20
  103.1 12.6 %all-gather.1 = f32[4,192,64]{1,2,0:T(8,128)S(1)} all-gather(f32[1,192,64]{1,2,0:T(8,128)S(1)} %bitcast.53), channel_id=1, replica_groups=mesh['dp'=8,'wshard'=4,'tensor'=4] {'wshard'}, dimensions={0}, use_global_device_ids=true | all-gather | bytes 245760 | tf_op jit(solution)/shard_map/all_gather | solution.py:54
  116.1 4.6 %fusion.3 = f32[2,768,128]{1,2,0:T(8,128)S(1)} fusion(f32[1,768,768]{2,1,0:T(8,128)S(1)} %bitcast.50, f32[1,768,768]{2,1,0:T(8,128)} %param.20, f32[1,768,64]{1,2,0:T(8,128)S(1)} %broadcast_in_dim.19, f32[1,768,64]{1,2,0:T(8,128)S(1)} %get-tuple-element.69, f32[1,768,64]{1,2,0:T(8,128)S(1)} %broadcast_in_dim.18, f32[1,768,64]{1,2,0:T(8,128)S(1)} %get-tuple-element.68), kind=kOutput, calls=%fused_computation.6 | convolution fusion | flops 1813708800 | bytes 6291456 | tf_op jit(solution)/shard_map/bki,bkc->bic/dot_general | solution.py:61
  120.8 4.8 %fusion.2 = f32[2,768,64]{1,2,0:T(8,128)S(1)} fusion(f32[1,768,768]{2,1,0:T(8,128)S(1)} %bitcast.51, f32[1,768,768]{2,1,0:T(8,128)S(1)} %copy-done.3, f32[2,768,128]{1,2,0:T(8,128)S(1)} %fusion.3, f32[2,768,64]{1,2,0:T(8,128)S(1)} %fusion.11), kind=kOutput, calls=%fused_computation.5 | convolution fusion | flops 907345920 | bytes 5898240 | tf_op jit(solution)/shard_map/bik,bkc->bic/dot_general | solution.py:68
  126.3 30.3 %all_gather.14 = bf16[1,768,512]{1,2,0:T(8,128)(2,1)S(1)} all-gather(bf16[1,768,64]{1,2,0:T(8,128)(2,1)S(1)} %get-tuple-element.59), channel_id=1, replica_groups=mesh['dp'=8,'wshard'=4,'tensor'=4] {'dp'}, dimensions={2}, use_global_device_ids=true | all-gather | bytes 884736 | tf_op jit(solution)/shard_map/all_gather | solution.py:76
  157.8 1.6 fusion.26
  159.4 28.8 %all_gather.15 = bf16[192,512]{0,1:T(8,128)(2,1)S(1)} all-gather(bf16[192,64]{0,1:T(8,128)(2,1)S(1)} %get-tuple-element.57), channel_id=1, replica_groups=mesh['dp'=8,'wshard'=4,'tensor'=4] {'dp'}, dimensions={1}, use_global_device_ids=true | all-gather | bytes 221184 | tf_op jit(solution)/shard_map/all_gather | solution.py:77
  189.8 26.9 %all-reduce.2.cloned.1.call-done = f32[2,768,768]{2,1,0:T(8,128)} async-done(((f32[2,768,768]{2,1,0:T(8,128)}), f32[2,768,768]{2,1,0:T(8,128)}) %all-reduce.2.cloned.1.call-update) | async-done | bytes 4718608 | tf_op jit(solution)/shard_map/psum | solution.py:86
  216.7 9.3 %multiply_reduce_fusion = (f32[2]{0:T(128)S(1)}, f32[2,768,768]{2,1,0:T(8,128)S(1)}) fusion(f32[2,768,768]{2,1,0:T(8,128)} %all-reduce.2.cloned.1.call-done, f32[1,768,768]{2,1,0:T(8,128)S(1)} %bitcast.52, f32[1,768,768]{2,1,0:T(8,128)} %param.20), kind=kOutput, calls=%fused_computation.3 | convolution fusion | flops 5439356928 | bytes 14155784 | tf_op jit(solution)/shard_map/bik,bkj->bij/dot_general | solution.py:88
  226.0 2.6 broadcast_multiply_fusion
  228.7 6.1 %copy.47 = f32[2,768,768]{1,2,0:T(8,128)} copy(f32[2,768,768]{2,1,0:T(8,128)} %broadcast_multiply_fusion) | data formatting | bytes 9437184 | tf_op jit(solution)/shard_map/while | solution.py:94
  234.8 85.3 %while.10 = (s32[]{:T(128)}, f32[2,768,768]{1,2,0:T(8,128)}, s32[]{:T(128)}) while((s32[]{:T(128)}, f32[2,768,768]{1,2,0:T(8,128)}, s32[]{:T(128)}) %tuple.35), condition=%wide.region_5.0_spmd, body=%wide.region_4.0_spmd.sunk | while | flops 16313352192 | bytes 80216168 | solution.py:94
  234.8 9.8 %fusion.53 = f32[2,768,768]{2,1,0:T(8,128)S(1)} fusion(f32[2,768,768]{1,2,0:T(8,128)} %get-tuple-element.91), kind=kOutput, calls=%fused_computation.50.clone.1 | convolution fusion | flops 5435817984 | bytes 9437184 | tf_op jit(solution)/shard_map/while/body/eval_jaxpr/bki,bkj->bij/dot_general | solution.py:17
  244.6 7.3 %fusion.54 = f32[2,768,768]{2,1,0:T(8,128)S(1)} fusion(f32[2,768,768]{2,1,0:T(8,128)S(1)} %fusion.53, f32[2,768,768]{1,2,0:T(8,128)S(1)} %copy-done), kind=kOutput, calls=%fused_computation.51.clone.1 | convolution fusion | flops 5435817984 | bytes 14155776 | tf_op jit(solution)/shard_map/while/body/eval_jaxpr/bik,bkj->bij/dot_general | solution.py:21
  251.9 9.1 %fusion.55 = f32[2,768,768]{1,2,0:T(8,128)S(1)} fusion(f32[2,768,768]{2,1,0:T(8,128)S(1)} %fusion.54, f32[2,768,768]{1,2,0:T(8,128)S(1)} %copy-done, f32[2,768,768]{2,1,0:T(8,128)S(1)} %fusion.53), kind=kOutput, calls=%fused_computation.1.clone.1 | convolution fusion | flops 5441716224 | bytes 18874368 | tf_op jit(solution)/shard_map/while/body/eval_jaxpr/bik,bkj->bij/dot_general | solution.py:22
  261.0 2.2 copy-done.1
  263.2 9.8 %fusion.53 = f32[2,768,768]{2,1,0:T(8,128)S(1)} fusion(f32[2,768,768]{1,2,0:T(8,128)} %get-tuple-element.91), kind=kOutput, calls=%fused_computation.50.clone.1 | convolution fusion | flops 5435817984 | bytes 9437184 | tf_op jit(solution)/shard_map/while/body/eval_jaxpr/bki,bkj->bij/dot_general | solution.py:17
  273.0 7.3 %fusion.54 = f32[2,768,768]{2,1,0:T(8,128)S(1)} fusion(f32[2,768,768]{2,1,0:T(8,128)S(1)} %fusion.53, f32[2,768,768]{1,2,0:T(8,128)S(1)} %copy-done), kind=kOutput, calls=%fused_computation.51.clone.1 | convolution fusion | flops 5435817984 | bytes 14155776 | tf_op jit(solution)/shard_map/while/body/eval_jaxpr/bik,bkj->bij/dot_general | solution.py:21
  280.4 9.1 %fusion.55 = f32[2,768,768]{1,2,0:T(8,128)S(1)} fusion(f32[2,768,768]{2,1,0:T(8,128)S(1)} %fusion.54, f32[2,768,768]{1,2,0:T(8,128)S(1)} %copy-done, f32[2,768,768]{2,1,0:T(8,128)S(1)} %fusion.53), kind=kOutput, calls=%fused_computation.1.clone.1 | convolution fusion | flops 5441716224 | bytes 18874368 | tf_op jit(solution)/shard_map/while/body/eval_jaxpr/bik,bkj->bij/dot_general | solution.py:22
  289.5 2.2 copy-done.1
  291.7 9.8 %fusion.53 = f32[2,768,768]{2,1,0:T(8,128)S(1)} fusion(f32[2,768,768]{1,2,0:T(8,128)} %get-tuple-element.91), kind=kOutput, calls=%fused_computation.50.clone.1 | convolution fusion | flops 5435817984 | bytes 9437184 | tf_op jit(solution)/shard_map/while/body/eval_jaxpr/bki,bkj->bij/dot_general | solution.py:17
  301.5 7.3 %fusion.54 = f32[2,768,768]{2,1,0:T(8,128)S(1)} fusion(f32[2,768,768]{2,1,0:T(8,128)S(1)} %fusion.53, f32[2,768,768]{1,2,0:T(8,128)S(1)} %copy-done), kind=kOutput, calls=%fused_computation.51.clone.1 | convolution fusion | flops 5435817984 | bytes 14155776 | tf_op jit(solution)/shard_map/while/body/eval_jaxpr/bik,bkj->bij/dot_general | solution.py:21
  308.8 9.1 %fusion.55 = f32[2,768,768]{1,2,0:T(8,128)S(1)} fusion(f32[2,768,768]{2,1,0:T(8,128)S(1)} %fusion.54, f32[2,768,768]{1,2,0:T(8,128)S(1)} %copy-done, f32[2,768,768]{2,1,0:T(8,128)S(1)} %fusion.53), kind=kOutput, calls=%fused_computation.1.clone.1 | convolution fusion | flops 5441716224 | bytes 18874368 | tf_op jit(solution)/shard_map/while/body/eval_jaxpr/bik,bkj->bij/dot_general | solution.py:22
  317.9 2.2 copy-done.1
  320.1 6.0 %copy.48 = f32[2,768,768]{2,1,0:T(8,128)} copy(f32[2,768,768]{1,2,0:T(8,128)} %get-tuple-element.24) | data formatting | bytes 9437184 | tf_op jit(solution)/shard_map/while | solution.py:94
  326.1 4.9 %slice_bitcast_fusion = (f32[768,768]{1,0:T(8,128)}, f32[1,768,768]{2,1,0:T(8,128)}) fusion(f32[2,768,768]{2,1,0:T(8,128)} %copy.48), kind=kLoop, calls=%fused_computation.7 | loop fusion | bytes 9437184 | tf_op jit(solution)/shard_map/squeeze | solution.py:107
  331.0 1.6 dynamic-slice_bitcast_fusion
  (52 shorter events, 9.5 us)
Async XLA Ops:
  7.2 44.8 %copy-start.12 = (f32[192,64]{0,1:T(8,128)S(1)}, f32[192,64]{0,1:T(8,128)}, u32[]{:S(2)}) copy-start(f32[192,64]{0,1:T(8,128)} %param.22) | copy-start | bytes 147460
  7.2 87.6 %copy-start.8 = (f32[1,768,64]{1,2,0:T(8,128)S(1)}, f32[1,768,64]{1,2,0:T(8,128)}, u32[]{:S(2)}) copy-start(f32[1,768,64]{1,2,0:T(8,128)} %param.17) | copy-start | bytes 589828
  7.2 44.7 %reduce-scatter.5.cloned.1.call-start = ((), (), s32[]{:S(2)}) async-start(), calls=%async_computation.3 | async-start | bytes 589824 | tf_op jit(solution)/shard_map/reduce_scatter | solution.py:46
  9.2 85.6 %reduce-scatter.3.cloned.1.call-start = ((), (), s32[]{:S(2)}) async-start(), calls=%async_computation.2 | async-start | bytes 1769472 | tf_op jit(solution)/shard_map/reduce_scatter | solution.py:45
  11.9 89.5 %copy-start.10 = (f32[24,768]{1,0:T(8,128)S(1)}, f32[24,768]{1,0:T(8,128)}, u32[]{:S(2)}) copy-start(f32[24,768]{1,0:T(8,128)} %param.24) | copy-start | bytes 221188
  11.9 89.5 %copy-start.11 = (f32[1,24,768]{2,1,0:T(8,128)S(1)}, f32[1,24,768]{2,1,0:T(8,128)}, u32[]{:S(2)}) copy-start(f32[1,24,768]{2,1,0:T(8,128)} %param.19) | copy-start | bytes 221188
  12.0 204.7 %all-reduce.2.cloned.1.call-start = ((), (), s32[]{:S(2)}) async-start(), calls=%async_computation.4 | async-start | bytes 9437184 | tf_op jit(solution)/shard_map/psum | solution.py:86
  52.8 50.3 %copy-start.5 = (f32[192,64]{0,1:T(8,128)}, f32[192,64]{0,1:T(8,128)S(1)}, u32[]{:S(2)}) copy-start(f32[192,64]{0,1:T(8,128)S(1)} %get-tuple-element.71) | copy-start | bytes 147460
  95.8 20.3 %copy-start.4 = (f32[1,768,64]{1,2,0:T(8,128)}, f32[1,768,64]{1,2,0:T(8,128)S(1)}, u32[]{:S(2)}) copy-start(f32[1,768,64]{1,2,0:T(8,128)S(1)} %get-tuple-element.69) | copy-start | bytes 589828
  95.8 20.3 %copy-start.2 = (f32[768,768]{1,0:T(8,128)S(1)}, f32[768,768]{1,0:T(8,128)}, u32[]{:S(2)}) copy-start(f32[768,768]{1,0:T(8,128)} %param.25) | copy-start | bytes 7077892
  116.0 4.7 %copy-start.6 = (f32[768,64]{0,1:T(8,128)S(1)}, f32[768,64]{0,1:T(8,128)}, u32[]{:S(2)}) copy-start(f32[768,64]{0,1:T(8,128)} %param.23) | copy-start | bytes 589828
  116.0 4.6 %copy-start.7 = (f32[1,768,64]{1,2,0:T(8,128)S(1)}, f32[1,768,64]{1,2,0:T(8,128)}, u32[]{:S(2)}) copy-start(f32[1,768,64]{1,2,0:T(8,128)} %param.18) | copy-start | bytes 589828
  116.1 4.7 %copy-start.3 = (f32[1,768,768]{2,1,0:T(8,128)S(1)}, f32[1,768,768]{2,1,0:T(8,128)}, u32[]{:S(2)}) copy-start(f32[1,768,768]{2,1,0:T(8,128)} %param.20) | copy-start | bytes 7077892
  120.7 4.9 %copy-start.9 = (f32[1,768,64]{1,2,0:T(8,128)S(1)}, f32[1,768,64]{1,2,0:T(8,128)}, u32[]{:S(2)}) copy-start(f32[1,768,64]{1,2,0:T(8,128)} %param.16) | copy-start | bytes 589828
  234.8 9.8 %copy-start = (f32[2,768,768]{1,2,0:T(8,128)S(1)}, f32[2,768,768]{1,2,0:T(8,128)}, u32[]{:S(2)}) copy-start(f32[2,768,768]{1,2,0:T(8,128)} %get-tuple-element.91) | copy-start | bytes 14155780 | tf_op jit(solution)/shard_map/while
  261.0 2.2 copy-start.1
  263.2 9.8 %copy-start = (f32[2,768,768]{1,2,0:T(8,128)S(1)}, f32[2,768,768]{1,2,0:T(8,128)}, u32[]{:S(2)}) copy-start(f32[2,768,768]{1,2,0:T(8,128)} %get-tuple-element.91) | copy-start | bytes 14155780 | tf_op jit(solution)/shard_map/while
  289.5 2.2 copy-start.1
  291.7 9.8 %copy-start = (f32[2,768,768]{1,2,0:T(8,128)S(1)}, f32[2,768,768]{1,2,0:T(8,128)}, u32[]{:S(2)}) copy-start(f32[2,768,768]{1,2,0:T(8,128)} %get-tuple-element.91) | copy-start | bytes 14155780 | tf_op jit(solution)/shard_map/while
  317.9 2.2 copy-start.1
Sparse Core Ops, SparseCore 0:
  10.9 40.9 reduce-scatter.4
  54.9 39.8 reduce-scatter.2
  103.2 113.3 all-reduce.1

commit v4 on v3

--- a/solution.py
+++ b/solution.py
@@ -85,14 +85,26 @@
     )
     stats_full = lax.psum(placed + 0.05 * partial_stat, ("tensor", "dp"))
     stats_out = lax.dynamic_slice_in_dim(stats_full, row_start, stat_rows, 1)
-    power = jnp.einsum("bik,bkj->bij", stats_full, bases_all, precision=HIGH)
+    tensor_size = lax.axis_size("tensor")
+    core = lax.axis_index("tensor") % 2
+    stat_mine = lax.dynamic_slice_in_dim(stats_full, core, 1, 0)
+    basis_mine = lax.dynamic_slice_in_dim(bases_all, core, 1, 0)
+    power = jnp.einsum("bik,bkj->bij", stat_mine, basis_mine, precision=HIGH)
     square_sum = jnp.sum(power * power, (1, 2))
     current = power * lax.rsqrt(square_sum + 1e-06)[:, None, None]
+
     def ns_iteration(repeat, current):
         return quintic_step(current, local_gram(current))
 
     current = lax.fori_loop(0, NS_ITERS, ns_iteration, current)
-    bases_out = current
+    partner = lax.ppermute(
+        current, "tensor", perm=[(t, t ^ 1) for t in range(tensor_size)]
+    )
+    bases_out = jnp.where(
+        core == 0,
+        jnp.concatenate([current, partner], 0),
+        jnp.concatenate([partner, current], 0),
+    )
     return (
         expert_master_out,
         expert_first_out,

time: 340 us -> 361 us (1.062)
  waiting for transfers between devices: 96 us -> 181 us
  matrix products: 103 us -> 54.1 us
  local copies, waits for them, and re-layouts: 31.1 us -> 14 us
    psum x1, waiting for transfers between devices: 26.9 us -> 111 us  [shards(): stats_full = lax.psum(placed + 0.05 * partial_stat, ('tensor', 'dp'))]
    dot_general x3, matrix products: 29.5 us -> 9.09 us  [local_gram(): return jnp.einsum('bki,bkj->bij', current, current, precision=HIGH)]
    dot_general x3, matrix products: 27.2 us -> 13.1 us  [quintic_step(): jnp.einsum('bik,bkj->bij', first_prod, gram_matrix, precision=HIGH)]
    dot_general x3, matrix products: 22 us -> 9.91 us  [quintic_step(): jnp.einsum('bik,bkj->bij', current, gram_matrix, precision=HIGH)]
    while x2, local copies, waits for them, and re-layouts: 12.1 us -> 3.99 us  [shards(): current = lax.fori_loop(0, NS_ITERS, ns_iteration, current)]
    while x12 -> x0, local copies, waits for them, and re-layouts: 6.53 us -> none
  transfers between devices with their start and end apart: 3 -> 4, of which waited for: 3 -> 3; matrix products, arithmetic and copies ran while one was open for 6% -> 6% of each run, Pallas kernels for 0% -> 0%
where the time goes in v4:
time: 361 us; the launch traced here: 360 us
  waiting for transfers between devices  181 us (50%)
  blocking collectives  83.8 us (23%)
  matrix products  54.1 us (15%)
  between operations  14.7 us (4%)
  local copies, waits for them, and re-layouts  14 us (4%)
  other arithmetic  12.4 us (3%)
    psum x1, waiting for transfers between devices, shards(): stats_full = lax.psum(placed + 0.05 * partial_stat, ('tensor', 'dp'))  111 us
    reduce_scatter x1, waiting for transfers between devices, shards(): lax.psum_scatter(dense_local, 'dp', scatter_dimension=1, tiled=True)  40 us
    all_gather x1, blocking collectives, shards(): lax.all_gather(expert_master_out.astype(jnp.bfloat16), 'dp', axis=2, tile...  30.1 us
    reduce_scatter x1, waiting for transfers between devices, shards(): lax.psum_scatter(expert_local, 'dp', scatter_dimension=2, tiled=True)  29.1 us
    all_gather x1, blocking collectives, shards(): lax.all_gather(dense_master_out.astype(jnp.bfloat16), 'dp', axis=1, tiled...  28.4 us
    dot_general x3, matrix products, quintic_step(): jnp.einsum('bik,bkj->bij', first_prod, gram_matrix, precision=HIGH)  13.1 us
    all_gather x1, blocking collectives, shards(): lax.all_gather(dense_first_out, 'wshard', axis=0, tiled=True)  12.8 us
    all_gather x1, blocking collectives, shards(): lax.all_gather(dense_mean, 'wshard', axis=0, tiled=True)  12.6 us
  transfers between devices with their start and end apart: 4, of which 3 were waited for; matrix products, arithmetic and copies ran while one was open for 6% of the time, Pallas kernels for 0%

profile of v4, /device:TPU:0, one launch (start us, length us, event | category | flops | bytes accessed | tf_op | source)
XLA Modules:
  0.0 359.9 jit_solution(7379867457524554938)
XLA Ops:
  9.2 1.4 copy.36
  10.6 1.3 bitcast_convert_fusion
  12.0 40.0 %reduce-scatter.5.cloned.1.call-done = f32[192,64]{0,1:T(8,128)} async-done(((f32[192,512]{0,1:T(8,128)}), f32[192,64]{0,1:T(8,128)}) %reduce-scatter.5.cloned.1.call-update) | async-done | bytes 49168 | tf_op jit(solution)/shard_map/reduce_scatter | solution.py:46
  52.8 12.6 %all-gather = f32[4,192,64]{1,2,0:T(8,128)S(1)} all-gather(f32[1,192,64]{1,2,0:T(8,128)S(1)} %get-tuple-element.70), channel_id=1, replica_groups=mesh['dp'=8,'wshard'=4,'tensor'=4] {'wshard'}, dimensions={0}, use_global_device_ids=true | all-gather | bytes 245760 | tf_op jit(solution)/shard_map/all_gather | solution.py:53
  65.7 29.1 %reduce-scatter.3.cloned.1.call-done = f32[1,768,64]{1,2,0:T(8,128)} async-done(((f32[1,768,512]{1,2,0:T(8,128)}), f32[1,768,64]{1,2,0:T(8,128)}) %reduce-scatter.3.cloned.1.call-update) | async-done | bytes 196624 | tf_op jit(solution)/shard_map/reduce_scatter | solution.py:45
  95.8 5.7 %broadcast_multiply_fusion = f32[2,768,768]{2,1,0:T(8,128)} fusion(f32[1,768,64]{1,2,0:T(8,128)S(1)} %broadcast_in_dim.18, f32[1,768,64]{1,2,0:T(8,128)S(1)} %get-tuple-element.68), kind=kOutput, calls=%fused_computation.20 | convolution fusion | flops 907247616 | bytes 5111808 | tf_op jit(solution)/shard_map/bic,bjc->bij/dot_general | solution.py:79
  101.5 1.6 fusion.29
  103.1 111.4 %all-reduce.2.cloned.1.call-done = f32[2,768,768]{2,1,0:T(8,128)} async-done(((f32[2,768,768]{2,1,0:T(8,128)}), f32[2,768,768]{2,1,0:T(8,128)}) %all-reduce.2.cloned.1.call-update) | async-done | bytes 4718608 | tf_op jit(solution)/shard_map/psum | solution.py:86
  214.6 6.3 %multiply_reduce_fusion = (f32[]{:T(128)}, f32[768,768]{1,0:T(8,128)S(1)}) fusion(s32[]{:T(128)S(6)} %select_n.29, f32[1,768,768]{2,1,0:T(8,128)} %param.20, f32[1,768,768]{2,1,0:T(8,128)} %bitcast.67, f32[2,768,768]{2,1,0:T(8,128)} %all-reduce.2.cloned.1.call-done), kind=kOutput, calls=%fused_computation.18 | convolution fusion | flops 2719678464 | bytes 9438212 | tf_op jit(solution)/shard_map/bik,bkj->bij/dot_general | solution.py:92
  221.5 1.6 multiply_bitcast_fusion
  223.1 2.0 copy.40
  225.1 32.4 %while.10 = (s32[]{:T(128)}, f32[1,768,768]{1,2,0:T(8,128)S(1)}, s32[]{:T(128)}) while((s32[]{:T(128)}, f32[1,768,768]{1,2,0:T(8,128)S(1)}, s32[]{:T(128)}) %tuple.35), condition=%wide.region_5.6_spmd, body=%wide.region_4.5_spmd.sunk | while | flops 8156676096 | bytes 21233708 | solution.py:99
  225.3 3.0 fusion.55
  228.4 3.3 fusion.56
  231.7 4.4 %fusion.57 = f32[1,768,768]{1,2,0:T(8,128)S(1)} fusion(f32[768,768]{1,0:T(8,128)S(1)} %fusion.56, f32[1,768,768]{1,2,0:T(8,128)S(1)} %get-tuple-element.91, f32[768,768]{1,0:T(8,128)S(1)} %fusion.55), kind=kOutput, calls=%fused_computation.1.clone.1 | convolution fusion | flops 2720858112 | bytes 9437184 | tf_op jit(solution)/shard_map/while/body/eval_jaxpr/bik,bkj->bij/dot_general | solution.py:22
  236.1 3.0 fusion.55
  239.1 3.3 fusion.56
  242.4 4.4 %fusion.57 = f32[1,768,768]{1,2,0:T(8,128)S(1)} fusion(f32[768,768]{1,0:T(8,128)S(1)} %fusion.56, f32[1,768,768]{1,2,0:T(8,128)S(1)} %get-tuple-element.91, f32[768,768]{1,0:T(8,128)S(1)} %fusion.55), kind=kOutput, calls=%fused_computation.1.clone.1 | convolution fusion | flops 2720858112 | bytes 9437184 | tf_op jit(solution)/shard_map/while/body/eval_jaxpr/bik,bkj->bij/dot_general | solution.py:22
  246.8 3.0 fusion.55
  249.9 3.3 fusion.56
  253.2 4.4 %fusion.57 = f32[1,768,768]{1,2,0:T(8,128)S(1)} fusion(f32[768,768]{1,0:T(8,128)S(1)} %fusion.56, f32[1,768,768]{1,2,0:T(8,128)S(1)} %get-tuple-element.91, f32[768,768]{1,0:T(8,128)S(1)} %fusion.55), kind=kOutput, calls=%fused_computation.1.clone.1 | convolution fusion | flops 2720858112 | bytes 9437184 | tf_op jit(solution)/shard_map/while/body/eval_jaxpr/bik,bkj->bij/dot_general | solution.py:22
  257.5 2.0 copy.42
  259.5 12.8 %all-gather.1 = f32[4,192,64]{1,2,0:T(8,128)S(1)} all-gather(f32[1,192,64]{1,2,0:T(8,128)S(1)} %bitcast.70), channel_id=1, replica_groups=mesh['dp'=8,'wshard'=4,'tensor'=4] {'wshard'}, dimensions={0}, use_global_device_ids=true | all-gather | bytes 245760 | tf_op jit(solution)/shard_map/all_gather | solution.py:54
  272.7 5.3 %fusion.6 = f32[2,768,128]{1,2,0:T(8,128)S(1)} fusion(f32[1,768,768]{2,1,0:T(8,128)} %bitcast.68, f32[1,768,768]{2,1,0:T(8,128)} %param.20, f32[1,768,64]{1,2,0:T(8,128)S(1)} %broadcast_in_dim.19, f32[1,768,64]{1,2,0:T(8,128)S(1)} %get-tuple-element.69, f32[1,768,64]{1,2,0:T(8,128)S(1)} %broadcast_in_dim.18, f32[1,768,64]{1,2,0:T(8,128)S(1)} %get-tuple-element.68), kind=kOutput, calls=%fused_computation.11 | convolution fusion | flops 1813708800 | bytes 6291456 | tf_op jit(solution)/shard_map/bki,bkc->bic/dot_general | solution.py:61
  278.1 4.8 %fusion.5 = f32[2,768,64]{1,2,0:T(8,128)S(1)} fusion(f32[1,768,768]{2,1,0:T(8,128)S(1)} %bitcast.69, f32[1,768,768]{2,1,0:T(8,128)S(1)} %copy-done.1, f32[2,768,128]{1,2,0:T(8,128)S(1)} %fusion.6, f32[2,768,64]{1,2,0:T(8,128)S(1)} %fusion.20), kind=kOutput, calls=%fused_computation.10 | convolution fusion | flops 907345920 | bytes 5898240 | tf_op jit(solution)/shard_map/bik,bkc->bic/dot_general | solution.py:68
  283.7 30.1 %all_gather.14 = bf16[1,768,512]{1,2,0:T(8,128)(2,1)S(1)} all-gather(bf16[1,768,64]{1,2,0:T(8,128)(2,1)S(1)} %get-tuple-element.59), channel_id=1, replica_groups=mesh['dp'=8,'wshard'=4,'tensor'=4] {'dp'}, dimensions={2}, use_global_device_ids=true | all-gather | bytes 884736 | tf_op jit(solution)/shard_map/all_gather | solution.py:76
  313.7 1.2 copy.44
  314.9 1.6 fusion.36
  316.5 28.4 %all_gather.15 = bf16[192,512]{0,1:T(8,128)(2,1)S(1)} all-gather(bf16[192,64]{0,1:T(8,128)(2,1)S(1)} %get-tuple-element.57), channel_id=1, replica_groups=mesh['dp'=8,'wshard'=4,'tensor'=4] {'dp'}, dimensions={1}, use_global_device_ids=true | all-gather | bytes 221184 | tf_op jit(solution)/shard_map/all_gather | solution.py:77
  346.5 1.6 dynamic-slice_bitcast_fusion
  348.1 2.8 maximum_select_fusion
  350.9 2.5 slice_bitcast_fusion
  (44 shorter events, 7.1 us)
Async XLA Ops:
  7.2 44.7 %reduce-scatter.5.cloned.1.call-start = ((), (), s32[]{:S(2)}) async-start(), calls=%async_computation.3 | async-start | bytes 589824 | tf_op jit(solution)/shard_map/reduce_scatter | solution.py:46
  9.1 85.7 %reduce-scatter.3.cloned.1.call-start = ((), (), s32[]{:S(2)}) async-start(), calls=%async_computation.2 | async-start | bytes 1769472 | tf_op jit(solution)/shard_map/reduce_scatter | solution.py:45
  10.6 41.3 %copy-start.11 = (f32[192,64]{0,1:T(8,128)S(1)}, f32[192,64]{0,1:T(8,128)}, u32[]{:S(2)}) copy-start(f32[192,64]{0,1:T(8,128)} %param.22) | copy-start | bytes 147460
  10.6 84.2 %copy-start.7 = (f32[1,768,64]{1,2,0:T(8,128)S(1)}, f32[1,768,64]{1,2,0:T(8,128)}, u32[]{:S(2)}) copy-start(f32[1,768,64]{1,2,0:T(8,128)} %param.17) | copy-start | bytes 589828
  11.9 202.6 %all-reduce.2.cloned.1.call-start = ((), (), s32[]{:S(2)}) async-start(), calls=%async_computation.4 | async-start | bytes 9437184 | tf_op jit(solution)/shard_map/psum | solution.py:86
  52.8 206.7 %copy-start.4 = (f32[192,64]{0,1:T(8,128)}, f32[192,64]{0,1:T(8,128)S(1)}, u32[]{:S(2)}) copy-start(f32[192,64]{0,1:T(8,128)S(1)} %get-tuple-element.71) | copy-start | bytes 147460
  95.8 176.9 %copy-start.3 = (f32[1,768,64]{1,2,0:T(8,128)}, f32[1,768,64]{1,2,0:T(8,128)S(1)}, u32[]{:S(2)}) copy-start(f32[1,768,64]{1,2,0:T(8,128)S(1)} %get-tuple-element.69) | copy-start | bytes 589828
  95.8 5.7 %copy-start.9 = (f32[24,768]{1,0:T(8,128)S(1)}, f32[24,768]{1,0:T(8,128)}, u32[]{:S(2)}) copy-start(f32[24,768]{1,0:T(8,128)} %param.24) | copy-start | bytes 221188
  95.8 5.7 %copy-start.10 = (f32[1,24,768]{2,1,0:T(8,128)S(1)}, f32[1,24,768]{2,1,0:T(8,128)}, u32[]{:S(2)}) copy-start(f32[1,24,768]{2,1,0:T(8,128)} %param.19) | copy-start | bytes 221188
  259.5 88.6 %collective-permute-start = (f32[1,768,768]{2,1,0:T(8,128)}, f32[1,768,768]{2,1,0:T(8,128)}, u32[]{:S(2)}, u32[]{:S(2)}) collective-permute-start(f32[1,768,768]{2,1,0:T(8,128)} %copy.42), channel_id=1, source_target_pairs={{0,1},{1,0},{2,3},{3,2},{4,5},{5,4},{6,7},{7,6},{8,9},{9,8},{10,11... | collective-permute-start | bytes 7077896 | tf_op jit(solution)/shard_map/ppermute | solution.py:100
  272.7 5.3 %copy-start.5 = (f32[768,64]{0,1:T(8,128)S(1)}, f32[768,64]{0,1:T(8,128)}, u32[]{:S(2)}) copy-start(f32[768,64]{0,1:T(8,128)} %param.23) | copy-start | bytes 589828
  272.7 5.3 %copy-start.6 = (f32[1,768,64]{1,2,0:T(8,128)S(1)}, f32[1,768,64]{1,2,0:T(8,128)}, u32[]{:S(2)}) copy-start(f32[1,768,64]{1,2,0:T(8,128)} %param.18) | copy-start | bytes 589828
  272.7 5.4 %copy-start = (f32[768,768]{1,0:T(8,128)S(1)}, f32[768,768]{1,0:T(8,128)}, u32[]{:S(2)}) copy-start(f32[768,768]{1,0:T(8,128)} %param.25) | copy-start | bytes 7077892
  272.7 5.4 %copy-start.1 = (f32[1,768,768]{2,1,0:T(8,128)S(1)}, f32[1,768,768]{2,1,0:T(8,128)}, u32[]{:S(2)}) copy-start(f32[1,768,768]{2,1,0:T(8,128)} %param.20) | copy-start | bytes 7077892
  278.1 4.8 %copy-start.8 = (f32[1,768,64]{1,2,0:T(8,128)S(1)}, f32[1,768,64]{1,2,0:T(8,128)}, u32[]{:S(2)}) copy-start(f32[1,768,64]{1,2,0:T(8,128)} %param.16) | copy-start | bytes 589828
  283.7 64.4 %copy-start.2 = (f32[1,768,768]{2,1,0:T(8,128)S(1)}, f32[1,768,768]{2,1,0:T(8,128)}, u32[]{:S(2)}) copy-start(f32[1,768,768]{2,1,0:T(8,128)} %copy.42) | copy-start | bytes 7077892
Sparse Core Ops, SparseCore 0:
  10.9 40.9 reduce-scatter.4
  54.9 39.8 reduce-scatter.2
  103.2 111.2 all-reduce.1

commit v5 on v4

--- a/solution.py
+++ b/solution.py
@@ -84,6 +84,11 @@
         jnp.zeros_like(partial_stat), 0.95 * stats_all, row_start, 1
     )
     stats_full = lax.psum(placed + 0.05 * partial_stat, ("tensor", "dp"))
+    stats_full, expert_weights, dense_weights, expert_master_out, dense_master_out = (
+        lax.optimization_barrier(
+            (stats_full, expert_weights, dense_weights, expert_master_out, dense_master_out)
+        )
+    )
     stats_out = lax.dynamic_slice_in_dim(stats_full, row_start, stat_rows, 1)
     tensor_size = lax.axis_size("tensor")
     core = lax.axis_index("tensor") % 2

time: 361 us -> 279 us (0.77)
  waiting for transfers between devices: 181 us -> 96.7 us
    psum x1, waiting for transfers between devices: 111 us -> 27.6 us  [shards(): stats_full = lax.psum(placed + 0.05 * partial_stat, ('tensor', 'dp'))]
  transfers between devices with their start and end apart: 4 -> 4, of which waited for: 3 -> 3; matrix products, arithmetic and copies ran while one was open for 6% -> 7% of each run, Pallas kernels for 0% -> 0%
where the time goes in v5:
time: 279 us; the launch traced here: 278 us
  waiting for transfers between devices  96.7 us (35%)
  blocking collectives  86 us (31%)
  matrix products  53.4 us (19%)
  local copies, waits for them, and re-layouts  15 us (5%)
  between operations  14.7 us (5%)
  other arithmetic  11.4 us (4%)
    reduce_scatter x1, waiting for transfers between devices, shards(): lax.psum_scatter(dense_local, 'dp', scatter_dimension=1, tiled=True)  40 us
    all_gather x1, blocking collectives, shards(): lax.all_gather(dense_master_out.astype(jnp.bfloat16), 'dp', axis=1, tiled...  30.7 us
    all_gather x1, blocking collectives, shards(): lax.all_gather(expert_master_out.astype(jnp.bfloat16), 'dp', axis=2, tile...  30 us
    reduce_scatter x1, waiting for transfers between devices, shards(): lax.psum_scatter(expert_local, 'dp', scatter_dimension=2, tiled=True)  29.1 us
    psum x1, waiting for transfers between devices, shards(): stats_full = lax.psum(placed + 0.05 * partial_stat, ('tensor', 'dp'))  27.6 us
    dot_general x3, matrix products, quintic_step(): jnp.einsum('bik,bkj->bij', first_prod, gram_matrix, precision=HIGH)  13.1 us
    all_gather x1, blocking collectives, shards(): lax.all_gather(dense_first_out, 'wshard', axis=0, tiled=True)  12.7 us
    all_gather x1, blocking collectives, shards(): lax.all_gather(dense_mean, 'wshard', axis=0, tiled=True)  12.6 us
  transfers between devices with their start and end apart: 4, of which 3 were waited for; matrix products, arithmetic and copies ran while one was open for 7% of the time, Pallas kernels for 0%

profile of v5, /device:TPU:0, one launch (start us, length us, event | category | flops | bytes accessed | tf_op | source)
XLA Modules:
  0.0 277.5 jit_solution(15564665934741274810)
XLA Ops:
  9.2 1.4 copy.36
  10.6 1.3 bitcast_convert_fusion
  12.0 40.0 %reduce-scatter.5.cloned.1.call-done = f32[192,64]{0,1:T(8,128)} async-done(((f32[192,512]{0,1:T(8,128)}), f32[192,64]{0,1:T(8,128)}) %reduce-scatter.5.cloned.1.call-update) | async-done | bytes 49168 | tf_op jit(solution)/shard_map/reduce_scatter | solution.py:46
  52.8 12.6 %all-gather = f32[4,192,64]{1,2,0:T(8,128)S(1)} all-gather(f32[1,192,64]{1,2,0:T(8,128)S(1)} %get-tuple-element.81), channel_id=1, replica_groups=mesh['dp'=8,'wshard'=4,'tensor'=4] {'wshard'}, dimensions={0}, use_global_device_ids=true | all-gather | bytes 245760 | tf_op jit(solution)/shard_map/all_gather | solution.py:53
  65.7 29.1 %reduce-scatter.3.cloned.1.call-done = f32[1,768,64]{1,2,0:T(8,128)} async-done(((f32[1,768,512]{1,2,0:T(8,128)}), f32[1,768,64]{1,2,0:T(8,128)}) %reduce-scatter.3.cloned.1.call-update) | async-done | bytes 196624 | tf_op jit(solution)/shard_map/reduce_scatter | solution.py:45
  95.8 5.7 %broadcast_multiply_fusion = f32[2,768,768]{2,1,0:T(8,128)} fusion(f32[1,768,64]{1,2,0:T(8,128)S(1)} %broadcast_in_dim.17, f32[1,768,64]{1,2,0:T(8,128)S(1)} %get-tuple-element.79), kind=kOutput, calls=%fused_computation.20 | convolution fusion | flops 907247616 | bytes 5111808 | tf_op jit(solution)/shard_map/bic,bjc->bij/dot_general | solution.py:79
  101.5 1.6 fusion.29
  103.2 12.7 %all-gather.1 = f32[4,192,64]{1,2,0:T(8,128)S(1)} all-gather(f32[1,192,64]{1,2,0:T(8,128)S(1)} %bitcast.70), channel_id=1, replica_groups=mesh['dp'=8,'wshard'=4,'tensor'=4] {'wshard'}, dimensions={0}, use_global_device_ids=true | all-gather | bytes 245760 | tf_op jit(solution)/shard_map/all_gather | solution.py:54
  116.3 4.6 %fusion.6 = f32[2,768,128]{1,2,0:T(8,128)S(1)} fusion(f32[1,768,768]{2,1,0:T(8,128)S(1)} %bitcast.68, f32[1,768,768]{2,1,0:T(8,128)} %param.20, f32[1,768,64]{1,2,0:T(8,128)S(1)} %broadcast_in_dim.20, f32[1,768,64]{1,2,0:T(8,128)S(1)} %get-tuple-element.78, f32[1,768,64]{1,2,0:T(8,128)S(1)} %broadcast_in_dim.17, f32[1,768,64]{1,2,0:T(8,128)S(1)} %get-tuple-element.79), kind=kOutput, calls=%fused_computation.11 | convolution fusion | flops 1813708800 | bytes 6291456 | tf_op jit(solution)/shard_map/bki,bkc->bic/dot_general | solution.py:61
  121.0 4.8 %fusion.5 = f32[2,768,64]{1,2,0:T(8,128)S(1)} fusion(f32[1,768,768]{2,1,0:T(8,128)S(1)} %bitcast.69, f32[1,768,768]{2,1,0:T(8,128)S(1)} %copy-done.1, f32[2,768,128]{1,2,0:T(8,128)S(1)} %fusion.6, f32[2,768,64]{1,2,0:T(8,128)S(1)} %fusion.20), kind=kOutput, calls=%fused_computation.10 | convolution fusion | flops 907345920 | bytes 5898240 | tf_op jit(solution)/shard_map/bik,bkc->bic/dot_general | solution.py:68
  127.2 30.7 %all_gather.15 = bf16[192,512]{0,1:T(8,128)(2,1)} all-gather(bf16[192,64]{0,1:T(8,128)(2,1)S(1)} %get-tuple-element.67), channel_id=1, replica_groups=mesh['dp'=8,'wshard'=4,'tensor'=4] {'dp'}, dimensions={1}, use_global_device_ids=true | all-gather | bytes 221184 | tf_op jit(solution)/shard_map/all_gather | solution.py:77
  157.9 30.0 %all_gather.14 = bf16[1,768,512]{1,2,0:T(8,128)(2,1)S(1)} all-gather(bf16[1,768,64]{1,2,0:T(8,128)(2,1)S(1)} %get-tuple-element.69), channel_id=1, replica_groups=mesh['dp'=8,'wshard'=4,'tensor'=4] {'dp'}, dimensions={2}, use_global_device_ids=true | all-gather | bytes 884736 | tf_op jit(solution)/shard_map/all_gather | solution.py:76
  187.9 27.6 %all-reduce.2.cloned.1.call-done = f32[2,768,768]{2,1,0:T(8,128)} async-done(((f32[2,768,768]{2,1,0:T(8,128)}), f32[2,768,768]{2,1,0:T(8,128)}) %all-reduce.2.cloned.1.call-update) | async-done | bytes 4718608 | tf_op jit(solution)/shard_map/psum | solution.py:86
  215.5 6.3 %multiply_reduce_fusion = (f32[]{:T(128)}, f32[768,768]{1,0:T(8,128)S(1)}) fusion(s32[]{:T(128)S(6)} %select_n.30, f32[1,768,768]{2,1,0:T(8,128)} %param.20, f32[1,768,768]{2,1,0:T(8,128)} %bitcast.67, f32[2,768,768]{2,1,0:T(8,128)} %all-reduce.2.cloned.1.call-done), kind=kOutput, calls=%fused_computation.18 | convolution fusion | flops 2719678464 | bytes 9438212 | tf_op jit(solution)/shard_map/bik,bkj->bij/dot_general | solution.py:97
  222.5 1.6 multiply_bitcast_fusion
  224.1 2.0 copy.40
  226.1 32.2 %while.10 = (s32[]{:T(128)}, f32[1,768,768]{1,2,0:T(8,128)S(1)}, s32[]{:T(128)}) while((s32[]{:T(128)}, f32[1,768,768]{1,2,0:T(8,128)S(1)}, s32[]{:T(128)}) %tuple.37), condition=%wide.region_5.6_spmd, body=%wide.region_4.5_spmd.sunk | while | flops 8156676096 | bytes 21233708 | solution.py:104
  226.2 3.0 %fusion.55 = f32[768,768]{1,0:T(8,128)S(1)} fusion(f32[1,768,768]{1,2,0:T(8,128)S(1)} %get-tuple-element.101), kind=kOutput, calls=%fused_computation.4.clone.1 | convolution fusion | flops 2717908992 | bytes 4718592 | tf_op jit(solution)/shard_map/while/body/eval_jaxpr/bki,bkj->bij/dot_general | solution.py:17
  229.2 3.3 %fusion.56 = f32[768,768]{1,0:T(8,128)S(1)} fusion(f32[768,768]{1,0:T(8,128)S(1)} %fusion.55, f32[1,768,768]{1,2,0:T(8,128)S(1)} %get-tuple-element.101), kind=kOutput, calls=%fused_computation.2.clone.1 | convolution fusion | flops 2717908992 | bytes 7077888 | tf_op jit(solution)/shard_map/while/body/eval_jaxpr/bik,bkj->bij/dot_general | solution.py:21
  232.5 4.4 %fusion.57 = f32[1,768,768]{1,2,0:T(8,128)S(1)} fusion(f32[768,768]{1,0:T(8,128)S(1)} %fusion.56, f32[1,768,768]{1,2,0:T(8,128)S(1)} %get-tuple-element.101, f32[768,768]{1,0:T(8,128)S(1)} %fusion.55), kind=kOutput, calls=%fused_computation.1.clone.1 | convolution fusion | flops 2720858112 | bytes 9437184 | tf_op jit(solution)/shard_map/while/body/eval_jaxpr/bik,bkj->bij/dot_general | solution.py:22
  236.9 3.0 %fusion.55 = f32[768,768]{1,0:T(8,128)S(1)} fusion(f32[1,768,768]{1,2,0:T(8,128)S(1)} %get-tuple-element.101), kind=kOutput, calls=%fused_computation.4.clone.1 | convolution fusion | flops 2717908992 | bytes 4718592 | tf_op jit(solution)/shard_map/while/body/eval_jaxpr/bki,bkj->bij/dot_general | solution.py:17
  239.9 3.3 %fusion.56 = f32[768,768]{1,0:T(8,128)S(1)} fusion(f32[768,768]{1,0:T(8,128)S(1)} %fusion.55, f32[1,768,768]{1,2,0:T(8,128)S(1)} %get-tuple-element.101), kind=kOutput, calls=%fused_computation.2.clone.1 | convolution fusion | flops 2717908992 | bytes 7077888 | tf_op jit(solution)/shard_map/while/body/eval_jaxpr/bik,bkj->bij/dot_general | solution.py:21
  243.2 4.4 %fusion.57 = f32[1,768,768]{1,2,0:T(8,128)S(1)} fusion(f32[768,768]{1,0:T(8,128)S(1)} %fusion.56, f32[1,768,768]{1,2,0:T(8,128)S(1)} %get-tuple-element.101, f32[768,768]{1,0:T(8,128)S(1)} %fusion.55), kind=kOutput, calls=%fused_computation.1.clone.1 | convolution fusion | flops 2720858112 | bytes 9437184 | tf_op jit(solution)/shard_map/while/body/eval_jaxpr/bik,bkj->bij/dot_general | solution.py:22
  247.6 3.0 %fusion.55 = f32[768,768]{1,0:T(8,128)S(1)} fusion(f32[1,768,768]{1,2,0:T(8,128)S(1)} %get-tuple-element.101), kind=kOutput, calls=%fused_computation.4.clone.1 | convolution fusion | flops 2717908992 | bytes 4718592 | tf_op jit(solution)/shard_map/while/body/eval_jaxpr/bki,bkj->bij/dot_general | solution.py:17
  250.7 3.3 %fusion.56 = f32[768,768]{1,0:T(8,128)S(1)} fusion(f32[768,768]{1,0:T(8,128)S(1)} %fusion.55, f32[1,768,768]{1,2,0:T(8,128)S(1)} %get-tuple-element.101), kind=kOutput, calls=%fused_computation.2.clone.1 | convolution fusion | flops 2717908992 | bytes 7077888 | tf_op jit(solution)/shard_map/while/body/eval_jaxpr/bik,bkj->bij/dot_general | solution.py:21
  254.0 4.4 %fusion.57 = f32[1,768,768]{1,2,0:T(8,128)S(1)} fusion(f32[768,768]{1,0:T(8,128)S(1)} %fusion.56, f32[1,768,768]{1,2,0:T(8,128)S(1)} %get-tuple-element.101, f32[768,768]{1,0:T(8,128)S(1)} %fusion.55), kind=kOutput, calls=%fused_computation.1.clone.1 | convolution fusion | flops 2720858112 | bytes 9437184 | tf_op jit(solution)/shard_map/while/body/eval_jaxpr/bik,bkj->bij/dot_general | solution.py:22
  258.4 2.0 copy.42
  261.1 1.8 copy.45
  262.9 1.2 copy.44
  264.1 1.6 dynamic-slice_bitcast_fusion
  265.7 2.8 %maximum_select_fusion = f32[2,768,768]{2,1,0:T(8,128)S(1)} fusion(f32[1,768,768]{2,1,0:T(8,128)} %collective-permute-done, f32[1,768,768]{2,1,0:T(8,128)S(1)} %copy-done.2, pred[]{:T(512)S(6)} %eq.5), kind=kLoop, calls=%fused_computation.9 | loop fusion | flops 3538944 | bytes 9437185 | tf_op jit(solution)/shard_map/jit(_where)/select_n | solution.py:108
  268.5 2.5 slice_bitcast_fusion
  (46 shorter events, 6.9 us)
Async XLA Ops:
  7.2 44.7 %reduce-scatter.5.cloned.1.call-start = ((), (), s32[]{:S(2)}) async-start(), calls=%async_computation.3 | async-start | bytes 589824 | tf_op jit(solution)/shard_map/reduce_scatter | solution.py:46
  9.1 85.7 %reduce-scatter.3.cloned.1.call-start = ((), (), s32[]{:S(2)}) async-start(), calls=%async_computation.2 | async-start | bytes 1769472 | tf_op jit(solution)/shard_map/reduce_scatter | solution.py:45
  10.6 41.3 %copy-start.12 = (f32[192,64]{0,1:T(8,128)S(1)}, f32[192,64]{0,1:T(8,128)}, u32[]{:S(2)}) copy-start(f32[192,64]{0,1:T(8,128)} %param.22) | copy-start | bytes 147460
  10.6 84.2 %copy-start.7 = (f32[1,768,64]{1,2,0:T(8,128)S(1)}, f32[1,768,64]{1,2,0:T(8,128)}, u32[]{:S(2)}) copy-start(f32[1,768,64]{1,2,0:T(8,128)} %param.17) | copy-start | bytes 589828
  11.9 203.6 %all-reduce.2.cloned.1.call-start = ((), (), s32[]{:S(2)}) async-start(), calls=%async_computation.4 | async-start | bytes 9437184 | tf_op jit(solution)/shard_map/psum | solution.py:86
  52.8 50.4 %copy-start.4 = (f32[192,64]{0,1:T(8,128)}, f32[192,64]{0,1:T(8,128)S(1)}, u32[]{:S(2)}) copy-start(f32[192,64]{0,1:T(8,128)S(1)} %get-tuple-element.80) | copy-start | bytes 147460
  95.8 20.4 %copy-start.3 = (f32[1,768,64]{1,2,0:T(8,128)}, f32[1,768,64]{1,2,0:T(8,128)S(1)}, u32[]{:S(2)}) copy-start(f32[1,768,64]{1,2,0:T(8,128)S(1)} %get-tuple-element.78) | copy-start | bytes 589828
  95.8 5.7 %copy-start.9 = (f32[24,768]{1,0:T(8,128)S(1)}, f32[24,768]{1,0:T(8,128)}, u32[]{:S(2)}) copy-start(f32[24,768]{1,0:T(8,128)} %param.24) | copy-start | bytes 221188
  95.8 5.7 %copy-start.10 = (f32[1,24,768]{2,1,0:T(8,128)S(1)}, f32[1,24,768]{2,1,0:T(8,128)}, u32[]{:S(2)}) copy-start(f32[1,24,768]{2,1,0:T(8,128)} %param.19) | copy-start | bytes 221188
  103.1 13.1 %copy-start = (f32[768,768]{1,0:T(8,128)S(1)}, f32[768,768]{1,0:T(8,128)}, u32[]{:S(2)}) copy-start(f32[768,768]{1,0:T(8,128)} %param.25) | copy-start | bytes 7077892
  116.2 4.6 %copy-start.5 = (f32[768,64]{0,1:T(8,128)S(1)}, f32[768,64]{0,1:T(8,128)}, u32[]{:S(2)}) copy-start(f32[768,64]{0,1:T(8,128)} %param.23) | copy-start | bytes 589828
  116.2 4.6 %copy-start.6 = (f32[1,768,64]{1,2,0:T(8,128)S(1)}, f32[1,768,64]{1,2,0:T(8,128)}, u32[]{:S(2)}) copy-start(f32[1,768,64]{1,2,0:T(8,128)} %param.18) | copy-start | bytes 589828
  116.2 4.7 %copy-start.1 = (f32[1,768,768]{2,1,0:T(8,128)S(1)}, f32[1,768,768]{2,1,0:T(8,128)}, u32[]{:S(2)}) copy-start(f32[1,768,768]{2,1,0:T(8,128)} %param.20) | copy-start | bytes 7077892
  120.9 4.8 %copy-start.8 = (f32[1,768,64]{1,2,0:T(8,128)S(1)}, f32[1,768,64]{1,2,0:T(8,128)}, u32[]{:S(2)}) copy-start(f32[1,768,64]{1,2,0:T(8,128)} %param.16) | copy-start | bytes 589828
  120.9 5.5 %copy-start.11 = (f32[192,64]{0,1:T(8,128)S(1)}, f32[192,64]{0,1:T(8,128)}, u32[]{:S(2)}) copy-start(f32[192,64]{0,1:T(8,128)} %param.21) | copy-start | bytes 147460
  260.3 5.3 %copy-start.2 = (f32[1,768,768]{2,1,0:T(8,128)S(1)}, f32[1,768,768]{2,1,0:T(8,128)}, u32[]{:S(2)}) copy-start(f32[1,768,768]{2,1,0:T(8,128)} %copy.42) | copy-start | bytes 7077892
  260.3 5.3 %collective-permute-start = (f32[1,768,768]{2,1,0:T(8,128)}, f32[1,768,768]{2,1,0:T(8,128)}, u32[]{:S(2)}, u32[]{:S(2)}) collective-permute-start(f32[1,768,768]{2,1,0:T(8,128)} %copy.42), channel_id=1, source_target_pairs={{0,1},{1,0},{2,3},{3,2},{4,5},{5,4},{6,7},{7,6},{8,9},{9,8},{10,11... | collective-permute-start | bytes 7077896 | tf_op jit(solution)/shard_map/ppermute | solution.py:105
Sparse Core Ops, SparseCore 0:
  10.9 40.9 reduce-scatter.4
  54.9 39.8 reduce-scatter.2
  103.3 112.2 all-reduce.1

commit v6 on v5

--- a/solution.py
+++ b/solution.py
@@ -41,10 +41,11 @@
     experts_here = expert_grads.shape[1]
     expert_local = expert_grads.reshape(expert_grads.shape[1:]).astype(jnp.float32)
     dense_local = dense_grads.reshape(dense_grads.shape[1:]).astype(jnp.float32)
-    expert_sum, dense_sum = (
-        lax.psum_scatter(expert_local, "dp", scatter_dimension=2, tiled=True),
-        lax.psum_scatter(dense_local, "dp", scatter_dimension=1, tiled=True),
-    )
+    expert_rows = expert_local.shape[1]
+    joined = jnp.concatenate([expert_local[0], dense_local], 0)
+    joined_sum = lax.psum_scatter(joined, "dp", scatter_dimension=1, tiled=True)
+    expert_sum = joined_sum[None, :expert_rows]
+    dense_sum = joined_sum[expert_rows:]
     expert_mean = expert_sum / replicas
     dense_mean = dense_sum / replicas
     expert_first_out = 0.9 * expert_first + 0.1 * expert_mean

time: 279 us -> 255 us (0.914)
  waiting for transfers between devices: 96.7 us -> 72.2 us
    reduce_scatter x2 -> x1, waiting for transfers between devices: 69 us -> 45.8 us  [shards(): joined_sum = lax.psum_scatter(joined, 'dp', scatter_dimension=1, tiled=True)]
  transfers between devices with their start and end apart: 4 -> 3, of which waited for: 3 -> 2; matrix products, arithmetic and copies ran while one was open for 7% -> 7% of each run, Pallas kernels for 0% -> 0%
where the time goes in v6:
time: 255 us; the launch traced here: 253 us
  blocking collectives  85.4 us (33%)
  waiting for transfers between devices  72.2 us (28%)
  matrix products  53.5 us (21%)
  local copies, waits for them, and re-layouts  15 us (6%)
  between operations  15 us (6%)
  other arithmetic  11.8 us (5%)
    reduce_scatter x1, waiting for transfers between devices, shards(): joined_sum = lax.psum_scatter(joined, 'dp', scatter_dimension=1, tiled=True)  45.8 us
    all_gather x1, blocking collectives, shards(): lax.all_gather(dense_master_out.astype(jnp.bfloat16), 'dp', axis=1, tiled...  30.6 us
    all_gather x1, blocking collectives, shards(): lax.all_gather(expert_master_out.astype(jnp.bfloat16), 'dp', axis=2, tile...  29.8 us
    psum x1, waiting for transfers between devices, shards(): stats_full = lax.psum(placed + 0.05 * partial_stat, ('tensor', 'dp'))  26.4 us
    dot_general x3, matrix products, quintic_step(): jnp.einsum('bik,bkj->bij', first_prod, gram_matrix, precision=HIGH)  13.1 us
    all_gather x1, blocking collectives, shards(): lax.all_gather(dense_mean, 'wshard', axis=0, tiled=True)  12.6 us
    all_gather x1, blocking collectives, shards(): lax.all_gather(dense_first_out, 'wshard', axis=0, tiled=True)  12.4 us
    dot_general x3, matrix products, quintic_step(): jnp.einsum('bik,bkj->bij', current, gram_matrix, precision=HIGH)  9.91 us
  transfers between devices with their start and end apart: 3, of which 2 were waited for; matrix products, arithmetic and copies ran while one was open for 7% of the time, Pallas kernels for 0%

profile of v6, /device:TPU:0, one launch (start us, length us, event | category | flops | bytes accessed | tf_op | source)
XLA Modules:
  0.0 253.1 jit_solution(9452417011461819555)
XLA Ops:
  7.2 1.1 copy.47
  8.3 1.4 copy.46
  9.7 1.6 maximum_convert_fusion
  11.4 45.8 %reduce-scatter.2.cloned.1.call-done = f32[960,64]{0,1:T(8,128)} async-done(((f32[960,512]{0,1:T(8,128)}), f32[960,64]{0,1:T(8,128)}) %reduce-scatter.2.cloned.1.call-update) | async-done | bytes 245776 | tf_op jit(solution)/shard_map/reduce_scatter | solution.py:46
  58.0 12.6 %all-gather = f32[4,192,64]{1,2,0:T(8,128)S(1)} all-gather(f32[1,192,64]{1,2,0:T(8,128)S(1)} %get-tuple-element.93), channel_id=1, replica_groups=mesh['dp'=8,'wshard'=4,'tensor'=4] {'wshard'}, dimensions={0}, use_global_device_ids=true | all-gather | bytes 245760 | tf_op jit(solution)/shard_map/all_gather | solution.py:54
  71.9 5.7 %broadcast_multiply_fusion = f32[2,768,768]{2,1,0:T(8,128)} fusion(f32[1,768,64]{1,2,0:T(8,128)S(1)} %broadcast_in_dim.18, f32[1,768,64]{1,2,0:T(8,128)S(1)} %multiply_bitcast_fusion.1), kind=kOutput, calls=%fused_computation.20 | convolution fusion | flops 907247616 | bytes 5111808 | tf_op jit(solution)/shard_map/bic,bjc->bij/dot_general | solution.py:80
  77.6 1.6 fusion.29
  79.3 12.4 %all-gather.1 = f32[4,192,64]{1,2,0:T(8,128)S(1)} all-gather(f32[1,192,64]{1,2,0:T(8,128)S(1)} %bitcast.72), channel_id=1, replica_groups=mesh['dp'=8,'wshard'=4,'tensor'=4] {'wshard'}, dimensions={0}, use_global_device_ids=true | all-gather | bytes 245760 | tf_op jit(solution)/shard_map/all_gather | solution.py:55
  93.0 4.6 %fusion.6 = f32[2,768,128]{1,2,0:T(8,128)S(1)} fusion(f32[1,768,768]{2,1,0:T(8,128)S(1)} %bitcast.68, f32[1,768,768]{2,1,0:T(8,128)} %param.20, f32[1,768,64]{1,2,0:T(8,128)S(1)} %broadcast_in_dim.21, f32[1,768,64]{1,2,0:T(8,128)S(1)} %bitcast_add_fusion.1, f32[1,768,64]{1,2,0:T(8,128)S(1)} %broadcast_in_dim.18, f32[1,768,64]{1,2,0:T(8,128)S(1)} %multiply_bitcast_fusion.1), kind=kOutput, calls=%fused_computation.11 | convolution fusion | flops 1813708800 | bytes 6291456 | tf_op jit(solution)/shard_map/bki,bkc->bic/dot_general | solution.py:62
  97.8 4.8 %fusion.5 = f32[2,768,64]{1,2,0:T(8,128)S(1)} fusion(f32[1,768,768]{2,1,0:T(8,128)S(1)} %bitcast.69, f32[1,768,768]{2,1,0:T(8,128)S(1)} %copy-done.1, f32[2,768,128]{1,2,0:T(8,128)S(1)} %fusion.6, f32[2,768,64]{1,2,0:T(8,128)S(1)} %fusion.20), kind=kOutput, calls=%fused_computation.10 | convolution fusion | flops 907345920 | bytes 5898240 | tf_op jit(solution)/shard_map/bik,bkc->bic/dot_general | solution.py:69
  104.0 30.6 %all_gather.15 = bf16[192,512]{0,1:T(8,128)(2,1)} all-gather(bf16[192,64]{0,1:T(8,128)(2,1)S(1)} %get-tuple-element.81), channel_id=1, replica_groups=mesh['dp'=8,'wshard'=4,'tensor'=4] {'dp'}, dimensions={1}, use_global_device_ids=true | all-gather | bytes 221184 | tf_op jit(solution)/shard_map/all_gather | solution.py:78
  134.6 29.8 %all_gather.14 = bf16[1,768,512]{1,2,0:T(8,128)(2,1)S(1)} all-gather(bf16[1,768,64]{1,2,0:T(8,128)(2,1)S(1)} %get-tuple-element.83), channel_id=1, replica_groups=mesh['dp'=8,'wshard'=4,'tensor'=4] {'dp'}, dimensions={2}, use_global_device_ids=true | all-gather | bytes 884736 | tf_op jit(solution)/shard_map/all_gather | solution.py:77
  164.4 26.4 %all-reduce.2.cloned.1.call-done = f32[2,768,768]{2,1,0:T(8,128)} async-done(((f32[2,768,768]{2,1,0:T(8,128)}), f32[2,768,768]{2,1,0:T(8,128)}) %all-reduce.2.cloned.1.call-update) | async-done | bytes 4718608 | tf_op jit(solution)/shard_map/psum | solution.py:87
  190.8 6.3 %multiply_reduce_fusion = (f32[]{:T(128)}, f32[768,768]{1,0:T(8,128)S(1)}) fusion(s32[]{:T(128)S(6)} %select_n.30, f32[1,768,768]{2,1,0:T(8,128)} %param.20, f32[1,768,768]{2,1,0:T(8,128)} %bitcast.67, f32[2,768,768]{2,1,0:T(8,128)} %all-reduce.2.cloned.1.call-done), kind=kOutput, calls=%fused_computation.18 | convolution fusion | flops 2719678464 | bytes 9438212 | tf_op jit(solution)/shard_map/bik,bkj->bij/dot_general | solution.py:98
  197.8 1.6 multiply_bitcast_fusion
  199.4 2.0 copy.50
  201.4 32.2 %while.10 = (s32[]{:T(128)}, f32[1,768,768]{1,2,0:T(8,128)S(1)}, s32[]{:T(128)}) while((s32[]{:T(128)}, f32[1,768,768]{1,2,0:T(8,128)S(1)}, s32[]{:T(128)}) %tuple.38), condition=%wide.region_4.5_spmd, body=%wide.region_3.4_spmd.sunk | while | flops 8156676096 | bytes 21233708 | solution.py:105
  201.5 3.0 %fusion.55 = f32[768,768]{1,0:T(8,128)S(1)} fusion(f32[1,768,768]{1,2,0:T(8,128)S(1)} %get-tuple-element.113), kind=kOutput, calls=%fused_computation.4.clone.1 | convolution fusion | flops 2717908992 | bytes 4718592 | tf_op jit(solution)/shard_map/while/body/eval_jaxpr/bki,bkj->bij/dot_general | solution.py:17
  204.5 3.3 %fusion.56 = f32[768,768]{1,0:T(8,128)S(1)} fusion(f32[768,768]{1,0:T(8,128)S(1)} %fusion.55, f32[1,768,768]{1,2,0:T(8,128)S(1)} %get-tuple-element.113), kind=kOutput, calls=%fused_computation.2.clone.1 | convolution fusion | flops 2717908992 | bytes 7077888 | tf_op jit(solution)/shard_map/while/body/eval_jaxpr/bik,bkj->bij/dot_general | solution.py:21
  207.8 4.4 %fusion.57 = f32[1,768,768]{1,2,0:T(8,128)S(1)} fusion(f32[768,768]{1,0:T(8,128)S(1)} %fusion.56, f32[1,768,768]{1,2,0:T(8,128)S(1)} %get-tuple-element.113, f32[768,768]{1,0:T(8,128)S(1)} %fusion.55), kind=kOutput, calls=%fused_computation.1.clone.1 | convolution fusion | flops 2720858112 | bytes 9437184 | tf_op jit(solution)/shard_map/while/body/eval_jaxpr/bik,bkj->bij/dot_general | solution.py:22
  212.2 3.0 %fusion.55 = f32[768,768]{1,0:T(8,128)S(1)} fusion(f32[1,768,768]{1,2,0:T(8,128)S(1)} %get-tuple-element.113), kind=kOutput, calls=%fused_computation.4.clone.1 | convolution fusion | flops 2717908992 | bytes 4718592 | tf_op jit(solution)/shard_map/while/body/eval_jaxpr/bki,bkj->bij/dot_general | solution.py:17
  215.2 3.3 %fusion.56 = f32[768,768]{1,0:T(8,128)S(1)} fusion(f32[768,768]{1,0:T(8,128)S(1)} %fusion.55, f32[1,768,768]{1,2,0:T(8,128)S(1)} %get-tuple-element.113), kind=kOutput, calls=%fused_computation.2.clone.1 | convolution fusion | flops 2717908992 | bytes 7077888 | tf_op jit(solution)/shard_map/while/body/eval_jaxpr/bik,bkj->bij/dot_general | solution.py:21
  218.5 4.4 %fusion.57 = f32[1,768,768]{1,2,0:T(8,128)S(1)} fusion(f32[768,768]{1,0:T(8,128)S(1)} %fusion.56, f32[1,768,768]{1,2,0:T(8,128)S(1)} %get-tuple-element.113, f32[768,768]{1,0:T(8,128)S(1)} %fusion.55), kind=kOutput, calls=%fused_computation.1.clone.1 | convolution fusion | flops 2720858112 | bytes 9437184 | tf_op jit(solution)/shard_map/while/body/eval_jaxpr/bik,bkj->bij/dot_general | solution.py:22
  222.9 3.0 %fusion.55 = f32[768,768]{1,0:T(8,128)S(1)} fusion(f32[1,768,768]{1,2,0:T(8,128)S(1)} %get-tuple-element.113), kind=kOutput, calls=%fused_computation.4.clone.1 | convolution fusion | flops 2717908992 | bytes 4718592 | tf_op jit(solution)/shard_map/while/body/eval_jaxpr/bki,bkj->bij/dot_general | solution.py:17
  226.0 3.3 %fusion.56 = f32[768,768]{1,0:T(8,128)S(1)} fusion(f32[768,768]{1,0:T(8,128)S(1)} %fusion.55, f32[1,768,768]{1,2,0:T(8,128)S(1)} %get-tuple-element.113), kind=kOutput, calls=%fused_computation.2.clone.1 | convolution fusion | flops 2717908992 | bytes 7077888 | tf_op jit(solution)/shard_map/while/body/eval_jaxpr/bik,bkj->bij/dot_general | solution.py:21
  229.3 4.4 %fusion.57 = f32[1,768,768]{1,2,0:T(8,128)S(1)} fusion(f32[768,768]{1,0:T(8,128)S(1)} %fusion.56, f32[1,768,768]{1,2,0:T(8,128)S(1)} %get-tuple-element.113, f32[768,768]{1,0:T(8,128)S(1)} %fusion.55), kind=kOutput, calls=%fused_computation.1.clone.1 | convolution fusion | flops 2720858112 | bytes 9437184 | tf_op jit(solution)/shard_map/while/body/eval_jaxpr/bik,bkj->bij/dot_general | solution.py:22
  233.7 2.0 copy.52
  236.4 1.8 copy.55
  238.2 1.2 copy.54
  239.4 1.6 dynamic-slice_bitcast_fusion
  241.0 2.8 %maximum_select_fusion = f32[2,768,768]{2,1,0:T(8,128)S(1)} fusion(f32[1,768,768]{2,1,0:T(8,128)} %collective-permute-done, f32[1,768,768]{2,1,0:T(8,128)S(1)} %copy-done.2, pred[]{:T(512)S(6)} %eq.5), kind=kLoop, calls=%fused_computation.9 | loop fusion | flops 3538944 | bytes 9437185 | tf_op jit(solution)/shard_map/jit(_where)/select_n | solution.py:109
  243.8 2.5 slice_bitcast_fusion
  (43 shorter events, 5.9 us)
Async XLA Ops:
  7.2 50.0 %reduce-scatter.2.cloned.1.call-start = ((), (), s32[]{:S(2)}) async-start(), calls=%async_computation.1 | async-start | bytes 2359296 | tf_op jit(solution)/shard_map/reduce_scatter | solution.py:46
  9.7 47.4 %copy-start.12 = (f32[192,64]{0,1:T(8,128)S(1)}, f32[192,64]{0,1:T(8,128)}, u32[]{:S(2)}) copy-start(f32[192,64]{0,1:T(8,128)} %param.22) | copy-start | bytes 147460
  11.3 179.5 %all-reduce.2.cloned.1.call-start = ((), (), s32[]{:S(2)}) async-start(), calls=%async_computation.2 | async-start | bytes 9437184 | tf_op jit(solution)/shard_map/psum | solution.py:87
  58.0 21.2 %copy-start.5 = (f32[192,64]{0,1:T(8,128)}, f32[192,64]{0,1:T(8,128)S(1)}, u32[]{:S(2)}) copy-start(f32[192,64]{0,1:T(8,128)S(1)} %get-tuple-element.92) | copy-start | bytes 147460
  71.9 5.7 %copy-start.9 = (f32[24,768]{1,0:T(8,128)S(1)}, f32[24,768]{1,0:T(8,128)}, u32[]{:S(2)}) copy-start(f32[24,768]{1,0:T(8,128)} %param.24) | copy-start | bytes 221188
  71.9 5.7 %copy-start.10 = (f32[1,24,768]{2,1,0:T(8,128)S(1)}, f32[1,24,768]{2,1,0:T(8,128)}, u32[]{:S(2)}) copy-start(f32[1,24,768]{2,1,0:T(8,128)} %param.19) | copy-start | bytes 221188
  79.2 12.8 %copy-start.3 = (f32[960,64]{0,1:T(8,128)S(1)}, f32[960,64]{0,1:T(8,128)}, u32[]{:S(2)}) copy-start(f32[960,64]{0,1:T(8,128)} %reduce-scatter.2.cloned.1.call-done) | copy-start | bytes 737284
  79.2 13.8 %copy-start = (f32[768,768]{1,0:T(8,128)S(1)}, f32[768,768]{1,0:T(8,128)}, u32[]{:S(2)}) copy-start(f32[768,768]{1,0:T(8,128)} %param.25) | copy-start | bytes 7077892
  93.0 4.7 %copy-start.4 = (f32[1,768,64]{1,2,0:T(8,128)}, f32[1,768,64]{1,2,0:T(8,128)S(1)}, u32[]{:S(2)}) copy-start(f32[1,768,64]{1,2,0:T(8,128)S(1)} %bitcast_add_fusion.1) | copy-start | bytes 589828
  93.0 4.7 %copy-start.6 = (f32[768,64]{0,1:T(8,128)S(1)}, f32[768,64]{0,1:T(8,128)}, u32[]{:S(2)}) copy-start(f32[768,64]{0,1:T(8,128)} %param.23) | copy-start | bytes 589828
  93.0 4.7 %copy-start.7 = (f32[1,768,64]{1,2,0:T(8,128)S(1)}, f32[1,768,64]{1,2,0:T(8,128)}, u32[]{:S(2)}) copy-start(f32[1,768,64]{1,2,0:T(8,128)} %param.18) | copy-start | bytes 589828
  93.0 4.7 %copy-start.1 = (f32[1,768,768]{2,1,0:T(8,128)S(1)}, f32[1,768,768]{2,1,0:T(8,128)}, u32[]{:S(2)}) copy-start(f32[1,768,768]{2,1,0:T(8,128)} %param.20) | copy-start | bytes 7077892
  97.8 4.8 %copy-start.8 = (f32[1,768,64]{1,2,0:T(8,128)S(1)}, f32[1,768,64]{1,2,0:T(8,128)}, u32[]{:S(2)}) copy-start(f32[1,768,64]{1,2,0:T(8,128)} %param.16) | copy-start | bytes 589828
  97.8 5.5 %copy-start.11 = (f32[192,64]{0,1:T(8,128)S(1)}, f32[192,64]{0,1:T(8,128)}, u32[]{:S(2)}) copy-start(f32[192,64]{0,1:T(8,128)} %param.21) | copy-start | bytes 147460
  235.6 5.3 %copy-start.2 = (f32[1,768,768]{2,1,0:T(8,128)S(1)}, f32[1,768,768]{2,1,0:T(8,128)}, u32[]{:S(2)}) copy-start(f32[1,768,768]{2,1,0:T(8,128)} %copy.52) | copy-start | bytes 7077892
  235.6 5.3 %collective-permute-start = (f32[1,768,768]{2,1,0:T(8,128)}, f32[1,768,768]{2,1,0:T(8,128)}, u32[]{:S(2)}, u32[]{:S(2)}) collective-permute-start(f32[1,768,768]{2,1,0:T(8,128)} %copy.52), channel_id=1, source_target_pairs={{0,1},{1,0},{2,3},{3,2},{4,5},{5,4},{6,7},{7,6},{8,9},{9,8},{10,11... | collective-permute-start | bytes 7077896 | tf_op jit(solution)/shard_map/ppermute | solution.py:106
Sparse Core Ops, SparseCore 0:
  11.4 45.6 reduce-scatter.1
  79.3 111.4 all-reduce.1

commit v7 on v6

--- a/solution.py
+++ b/solution.py
@@ -39,11 +39,14 @@
 ):
     replicas = lax.axis_size("dp")
     experts_here = expert_grads.shape[1]
-    expert_local = expert_grads.reshape(expert_grads.shape[1:]).astype(jnp.float32)
-    dense_local = dense_grads.reshape(dense_grads.shape[1:]).astype(jnp.float32)
-    expert_rows = expert_local.shape[1]
-    joined = jnp.concatenate([expert_local[0], dense_local], 0)
-    joined_sum = lax.psum_scatter(joined, "dp", scatter_dimension=1, tiled=True)
+    expert_local = expert_grads.reshape(expert_grads.shape[2:])
+    dense_local = dense_grads.reshape(dense_grads.shape[1:])
+    expert_rows = expert_local.shape[0]
+    joined = jnp.concatenate([expert_local, dense_local], 0)
+    owned = joined.shape[1] // replicas
+    joined = joined.reshape(joined.shape[0], replicas, owned).transpose(1, 0, 2)
+    received = lax.all_to_all(joined, "dp", 0, 0, tiled=True)
+    joined_sum = jnp.sum(received.astype(jnp.float32), 0)
     expert_sum = joined_sum[None, :expert_rows]
     dense_sum = joined_sum[expert_rows:]
     expert_mean = expert_sum / replicas

time: 255 us -> 230 us (0.902)
  waiting for transfers between devices: 72.2 us -> 42.5 us
  starting transfers between devices: 0.08 us -> 6.52 us
    reduce_scatter x1 -> x0, waiting for transfers between devices: 45.8 us -> none  [shards(): joined_sum = lax.psum_scatter(joined, 'dp', scatter_dimension=1, tiled=True)]
    all_to_all x0 -> x1, waiting for transfers between devices: none -> 14.7 us  [shards(): received = lax.all_to_all(joined, 'dp', 0, 0, tiled=True)]
    all_to_all x0 -> x1, starting transfers between devices: none -> 6.48 us  [shards(): received = lax.all_to_all(joined, 'dp', 0, 0, tiled=True)]
    unnamed x30 -> x28, local copies, waits for them, and re-layouts: 5.53 us -> 5.52 us
  transfers between devices with their start and end apart: 3 -> 3, of which waited for: 2 -> 2; matrix products, arithmetic and copies ran while one was open for 7% -> 8% of each run, Pallas kernels for 0% -> 0%
where the time goes in v7:
time: 230 us; the launch traced here: 228 us
  blocking collectives  85.5 us (37%)
  matrix products  53.4 us (23%)
  waiting for transfers between devices  42.5 us (18%)
  local copies, waits for them, and re-layouts  15 us (7%)
  between operations  15 us (7%)
  other arithmetic  9.78 us (4%)
  starting transfers between devices  6.52 us (3%)
    all_gather x1, blocking collectives, shards(): lax.all_gather(dense_master_out.astype(jnp.bfloat16), 'dp', axis=1, tiled...  30.7 us
    all_gather x1, blocking collectives, shards(): lax.all_gather(expert_master_out.astype(jnp.bfloat16), 'dp', axis=2, tile...  29.7 us
    psum x1, waiting for transfers between devices, shards(): stats_full = lax.psum(placed + 0.05 * partial_stat, ('tensor', 'dp'))  27.8 us
    all_to_all x1, waiting for transfers between devices, shards(): received = lax.all_to_all(joined, 'dp', 0, 0, tiled=True)  14.7 us
    dot_general x3, matrix products, quintic_step(): jnp.einsum('bik,bkj->bij', first_prod, gram_matrix, precision=HIGH)  13.1 us
    all_gather x1, blocking collectives, shards(): lax.all_gather(dense_mean, 'wshard', axis=0, tiled=True)  12.8 us
    all_gather x1, blocking collectives, shards(): lax.all_gather(dense_first_out, 'wshard', axis=0, tiled=True)  12.4 us
    dot_general x3, matrix products, quintic_step(): jnp.einsum('bik,bkj->bij', current, gram_matrix, precision=HIGH)  9.91 us
  transfers between devices with their start and end apart: 3, of which 2 were waited for; matrix products, arithmetic and copies ran while one was open for 8% of the time, Pallas kernels for 0%

profile of v7, /device:TPU:0, one launch (start us, length us, event | category | flops | bytes accessed | tf_op | source)
XLA Modules:
  0.0 227.9 jit_solution(2094385989861738282)
XLA Ops:
  8.2 1.4 copy.44
  9.7 1.1 maximum_bitcast_fusion
  10.8 6.5 %all-to-all-start = ((bf16[8,960,64]{1,2,0:T(8,128)(2,1)}), bf16[8,960,64]{1,2,0:T(8,128)(2,1)S(1)}, u32[]{:S(2)}, u32[]{:S(2)}) async-start(bf16[8,960,64]{1,2,0:T(8,128)(2,1)} %maximum_bitcast_fusion), calls=%async_computation | async-start | bytes 2097152 | tf_op jit(solution)/shard_map/all_to_all | solution.py:48
  17.3 14.7 %all-to-all-done = bf16[8,960,64]{1,2,0:T(8,128)(2,1)S(1)} async-done(((bf16[8,960,64]{1,2,0:T(8,128)(2,1)}), bf16[8,960,64]{1,2,0:T(8,128)(2,1)S(1)}, u32[]{:S(2)}, u32[]{:S(2)}) %all-to-all-start) | async-done | bytes 983072 | tf_op jit(solution)/shard_map/all_to_all | solution.py:48
  32.3 12.8 %all-gather = f32[4,192,64]{1,2,0:T(8,128)S(1)} all-gather(f32[1,192,64]{1,2,0:T(8,128)S(1)} %get-tuple-element.93), channel_id=1, replica_groups=mesh['dp'=8,'wshard'=4,'tensor'=4] {'wshard'}, dimensions={0}, use_global_device_ids=true | all-gather | bytes 245760 | tf_op jit(solution)/shard_map/all_gather | solution.py:57
  45.5 5.6 %broadcast_multiply_fusion = f32[2,768,768]{2,1,0:T(8,128)} fusion(f32[1,768,64]{1,2,0:T(8,128)S(1)} %broadcast_in_dim.18, f32[1,768,64]{1,2,0:T(8,128)S(1)} %multiply_bitcast_fusion.1), kind=kOutput, calls=%fused_computation.20 | convolution fusion | flops 907247616 | bytes 5111808 | tf_op jit(solution)/shard_map/bic,bjc->bij/dot_general | solution.py:83
  51.1 1.6 fusion.29
  52.8 12.4 %all-gather.1 = f32[4,192,64]{1,2,0:T(8,128)S(1)} all-gather(f32[1,192,64]{1,2,0:T(8,128)S(1)} %bitcast.74), channel_id=1, replica_groups=mesh['dp'=8,'wshard'=4,'tensor'=4] {'wshard'}, dimensions={0}, use_global_device_ids=true | all-gather | bytes 245760 | tf_op jit(solution)/shard_map/all_gather | solution.py:58
  66.5 4.6 %fusion.6 = f32[2,768,128]{1,2,0:T(8,128)S(1)} fusion(f32[1,768,768]{2,1,0:T(8,128)S(1)} %bitcast.70, f32[1,768,768]{2,1,0:T(8,128)} %param.20, f32[1,768,64]{1,2,0:T(8,128)S(1)} %broadcast_in_dim.21, f32[1,768,64]{1,2,0:T(8,128)S(1)} %bitcast_add_fusion.1, f32[1,768,64]{1,2,0:T(8,128)S(1)} %broadcast_in_dim.18, f32[1,768,64]{1,2,0:T(8,128)S(1)} %multiply_bitcast_fusion.1), kind=kOutput, calls=%fused_computation.11 | convolution fusion | flops 1813708800 | bytes 6291456 | tf_op jit(solution)/shard_map/bki,bkc->bic/dot_general | solution.py:65
  71.2 4.8 %fusion.5 = f32[2,768,64]{1,2,0:T(8,128)S(1)} fusion(f32[1,768,768]{2,1,0:T(8,128)S(1)} %bitcast.71, f32[1,768,768]{2,1,0:T(8,128)S(1)} %copy-done.1, f32[2,768,128]{1,2,0:T(8,128)S(1)} %fusion.6, f32[2,768,64]{1,2,0:T(8,128)S(1)} %fusion.20), kind=kOutput, calls=%fused_computation.10 | convolution fusion | flops 907345920 | bytes 5898240 | tf_op jit(solution)/shard_map/bik,bkc->bic/dot_general | solution.py:72
  77.5 30.7 %all_gather.15 = bf16[192,512]{0,1:T(8,128)(2,1)} all-gather(bf16[192,64]{0,1:T(8,128)(2,1)S(1)} %get-tuple-element.81), channel_id=1, replica_groups=mesh['dp'=8,'wshard'=4,'tensor'=4] {'dp'}, dimensions={1}, use_global_device_ids=true | all-gather | bytes 221184 | tf_op jit(solution)/shard_map/all_gather | solution.py:81
  108.1 29.7 %all_gather.14 = bf16[1,768,512]{1,2,0:T(8,128)(2,1)S(1)} all-gather(bf16[1,768,64]{1,2,0:T(8,128)(2,1)S(1)} %get-tuple-element.83), channel_id=1, replica_groups=mesh['dp'=8,'wshard'=4,'tensor'=4] {'dp'}, dimensions={2}, use_global_device_ids=true | all-gather | bytes 884736 | tf_op jit(solution)/shard_map/all_gather | solution.py:80
  137.8 27.8 %all-reduce.2.cloned.1.call-done = f32[2,768,768]{2,1,0:T(8,128)} async-done(((f32[2,768,768]{2,1,0:T(8,128)}), f32[2,768,768]{2,1,0:T(8,128)}) %all-reduce.2.cloned.1.call-update) | async-done | bytes 4718608 | tf_op jit(solution)/shard_map/psum | solution.py:90
  165.6 6.3 %multiply_reduce_fusion = (f32[]{:T(128)}, f32[768,768]{1,0:T(8,128)S(1)}) fusion(s32[]{:T(128)S(6)} %select_n.30, f32[1,768,768]{2,1,0:T(8,128)} %param.20, f32[1,768,768]{2,1,0:T(8,128)} %bitcast.69, f32[2,768,768]{2,1,0:T(8,128)} %all-reduce.2.cloned.1.call-done), kind=kOutput, calls=%fused_computation.18 | convolution fusion | flops 2719678464 | bytes 9438212 | tf_op jit(solution)/shard_map/bik,bkj->bij/dot_general | solution.py:101
  172.6 1.6 multiply_bitcast_fusion
  174.2 2.0 copy.48
  176.2 32.2 %while.10 = (s32[]{:T(128)}, f32[1,768,768]{1,2,0:T(8,128)S(1)}, s32[]{:T(128)}) while((s32[]{:T(128)}, f32[1,768,768]{1,2,0:T(8,128)S(1)}, s32[]{:T(128)}) %tuple.38), condition=%wide.region_4.5_spmd, body=%wide.region_3.4_spmd.sunk | while | flops 8156676096 | bytes 21233708 | solution.py:108
  176.2 3.0 %fusion.55 = f32[768,768]{1,0:T(8,128)S(1)} fusion(f32[1,768,768]{1,2,0:T(8,128)S(1)} %get-tuple-element.113), kind=kOutput, calls=%fused_computation.4.clone.1 | convolution fusion | flops 2717908992 | bytes 4718592 | tf_op jit(solution)/shard_map/while/body/eval_jaxpr/bki,bkj->bij/dot_general | solution.py:17
  179.3 3.3 %fusion.56 = f32[768,768]{1,0:T(8,128)S(1)} fusion(f32[768,768]{1,0:T(8,128)S(1)} %fusion.55, f32[1,768,768]{1,2,0:T(8,128)S(1)} %get-tuple-element.113), kind=kOutput, calls=%fused_computation.2.clone.1 | convolution fusion | flops 2717908992 | bytes 7077888 | tf_op jit(solution)/shard_map/while/body/eval_jaxpr/bik,bkj->bij/dot_general | solution.py:21
  182.6 4.4 %fusion.57 = f32[1,768,768]{1,2,0:T(8,128)S(1)} fusion(f32[768,768]{1,0:T(8,128)S(1)} %fusion.56, f32[1,768,768]{1,2,0:T(8,128)S(1)} %get-tuple-element.113, f32[768,768]{1,0:T(8,128)S(1)} %fusion.55), kind=kOutput, calls=%fused_computation.1.clone.1 | convolution fusion | flops 2720858112 | bytes 9437184 | tf_op jit(solution)/shard_map/while/body/eval_jaxpr/bik,bkj->bij/dot_general | solution.py:22
  187.0 3.0 %fusion.55 = f32[768,768]{1,0:T(8,128)S(1)} fusion(f32[1,768,768]{1,2,0:T(8,128)S(1)} %get-tuple-element.113), kind=kOutput, calls=%fused_computation.4.clone.1 | convolution fusion | flops 2717908992 | bytes 4718592 | tf_op jit(solution)/shard_map/while/body/eval_jaxpr/bki,bkj->bij/dot_general | solution.py:17
  190.0 3.3 %fusion.56 = f32[768,768]{1,0:T(8,128)S(1)} fusion(f32[768,768]{1,0:T(8,128)S(1)} %fusion.55, f32[1,768,768]{1,2,0:T(8,128)S(1)} %get-tuple-element.113), kind=kOutput, calls=%fused_computation.2.clone.1 | convolution fusion | flops 2717908992 | bytes 7077888 | tf_op jit(solution)/shard_map/while/body/eval_jaxpr/bik,bkj->bij/dot_general | solution.py:21
  193.3 4.4 %fusion.57 = f32[1,768,768]{1,2,0:T(8,128)S(1)} fusion(f32[768,768]{1,0:T(8,128)S(1)} %fusion.56, f32[1,768,768]{1,2,0:T(8,128)S(1)} %get-tuple-element.113, f32[768,768]{1,0:T(8,128)S(1)} %fusion.55), kind=kOutput, calls=%fused_computation.1.clone.1 | convolution fusion | flops 2720858112 | bytes 9437184 | tf_op jit(solution)/shard_map/while/body/eval_jaxpr/bik,bkj->bij/dot_general | solution.py:22
  197.7 3.0 %fusion.55 = f32[768,768]{1,0:T(8,128)S(1)} fusion(f32[1,768,768]{1,2,0:T(8,128)S(1)} %get-tuple-element.113), kind=kOutput, calls=%fused_computation.4.clone.1 | convolution fusion | flops 2717908992 | bytes 4718592 | tf_op jit(solution)/shard_map/while/body/eval_jaxpr/bki,bkj->bij/dot_general | solution.py:17
  200.7 3.3 %fusion.56 = f32[768,768]{1,0:T(8,128)S(1)} fusion(f32[768,768]{1,0:T(8,128)S(1)} %fusion.55, f32[1,768,768]{1,2,0:T(8,128)S(1)} %get-tuple-element.113), kind=kOutput, calls=%fused_computation.2.clone.1 | convolution fusion | flops 2717908992 | bytes 7077888 | tf_op jit(solution)/shard_map/while/body/eval_jaxpr/bik,bkj->bij/dot_general | solution.py:21
  204.1 4.4 %fusion.57 = f32[1,768,768]{1,2,0:T(8,128)S(1)} fusion(f32[768,768]{1,0:T(8,128)S(1)} %fusion.56, f32[1,768,768]{1,2,0:T(8,128)S(1)} %get-tuple-element.113, f32[768,768]{1,0:T(8,128)S(1)} %fusion.55), kind=kOutput, calls=%fused_computation.1.clone.1 | convolution fusion | flops 2720858112 | bytes 9437184 | tf_op jit(solution)/shard_map/while/body/eval_jaxpr/bik,bkj->bij/dot_general | solution.py:22
  208.4 2.0 copy.50
  211.2 1.8 copy.53
  213.0 1.2 copy.52
  214.1 1.6 dynamic-slice_bitcast_fusion
  215.7 2.8 %maximum_select_fusion = f32[2,768,768]{2,1,0:T(8,128)S(1)} fusion(f32[1,768,768]{2,1,0:T(8,128)} %collective-permute-done, f32[1,768,768]{2,1,0:T(8,128)S(1)} %copy-done.2, pred[]{:T(512)S(6)} %eq.5), kind=kLoop, calls=%fused_computation.9 | loop fusion | flops 3538944 | bytes 9437185 | tf_op jit(solution)/shard_map/jit(_where)/select_n | solution.py:112
  218.6 2.5 %slice_bitcast_fusion = (f32[768,768]{1,0:T(8,128)}, f32[1,768,768]{2,1,0:T(8,128)}) fusion(f32[2,768,768]{2,1,0:T(8,128)S(1)} %maximum_select_fusion), kind=kLoop, calls=%fused_computation.15 | loop fusion | bytes 9437184 | tf_op jit(solution)/shard_map/squeeze | solution.py:128
  (41 shorter events, 5.3 us)
Async XLA Ops:
  10.8 21.5 %copy-start.11 = (f32[192,64]{0,1:T(8,128)S(1)}, f32[192,64]{0,1:T(8,128)}, u32[]{:S(2)}) copy-start(f32[192,64]{0,1:T(8,128)} %param.22) | copy-start | bytes 147460
  10.8 21.3 %all-to-all-start = ((bf16[8,960,64]{1,2,0:T(8,128)(2,1)}), bf16[8,960,64]{1,2,0:T(8,128)(2,1)S(1)}, u32[]{:S(2)}, u32[]{:S(2)}) async-start(bf16[8,960,64]{1,2,0:T(8,128)(2,1)} %maximum_bitcast_fusion), calls=%async_computation | async-start | bytes 2097152 | tf_op jit(solution)/shard_map/all_to_all | solution.py:48
  17.3 148.4 %all-reduce.2.cloned.1.call-start = ((), (), s32[]{:S(2)}) async-start(), calls=%async_computation.1 | async-start | bytes 9437184 | tf_op jit(solution)/shard_map/psum | solution.py:90
  32.3 20.5 %copy-start.4 = (f32[192,64]{0,1:T(8,128)}, f32[192,64]{0,1:T(8,128)S(1)}, u32[]{:S(2)}) copy-start(f32[192,64]{0,1:T(8,128)S(1)} %get-tuple-element.92) | copy-start | bytes 147460
  45.4 5.7 %copy-start.8 = (f32[24,768]{1,0:T(8,128)S(1)}, f32[24,768]{1,0:T(8,128)}, u32[]{:S(2)}) copy-start(f32[24,768]{1,0:T(8,128)} %param.24) | copy-start | bytes 221188
  45.5 5.7 %copy-start.9 = (f32[1,24,768]{2,1,0:T(8,128)S(1)}, f32[1,24,768]{2,1,0:T(8,128)}, u32[]{:S(2)}) copy-start(f32[1,24,768]{2,1,0:T(8,128)} %param.19) | copy-start | bytes 221188
  52.7 13.8 %copy-start = (f32[768,768]{1,0:T(8,128)S(1)}, f32[768,768]{1,0:T(8,128)}, u32[]{:S(2)}) copy-start(f32[768,768]{1,0:T(8,128)} %param.25) | copy-start | bytes 7077892
  66.5 4.6 %copy-start.3 = (f32[1,768,64]{1,2,0:T(8,128)}, f32[1,768,64]{1,2,0:T(8,128)S(1)}, u32[]{:S(2)}) copy-start(f32[1,768,64]{1,2,0:T(8,128)S(1)} %bitcast_add_fusion.1) | copy-start | bytes 589828
  66.5 4.6 %copy-start.5 = (f32[768,64]{0,1:T(8,128)S(1)}, f32[768,64]{0,1:T(8,128)}, u32[]{:S(2)}) copy-start(f32[768,64]{0,1:T(8,128)} %param.23) | copy-start | bytes 589828
  66.5 4.6 %copy-start.6 = (f32[1,768,64]{1,2,0:T(8,128)S(1)}, f32[1,768,64]{1,2,0:T(8,128)}, u32[]{:S(2)}) copy-start(f32[1,768,64]{1,2,0:T(8,128)} %param.18) | copy-start | bytes 589828
  66.5 4.7 %copy-start.1 = (f32[1,768,768]{2,1,0:T(8,128)S(1)}, f32[1,768,768]{2,1,0:T(8,128)}, u32[]{:S(2)}) copy-start(f32[1,768,768]{2,1,0:T(8,128)} %param.20) | copy-start | bytes 7077892
  71.2 4.8 %copy-start.7 = (f32[1,768,64]{1,2,0:T(8,128)S(1)}, f32[1,768,64]{1,2,0:T(8,128)}, u32[]{:S(2)}) copy-start(f32[1,768,64]{1,2,0:T(8,128)} %param.16) | copy-start | bytes 589828
  71.2 5.5 %copy-start.10 = (f32[192,64]{0,1:T(8,128)S(1)}, f32[192,64]{0,1:T(8,128)}, u32[]{:S(2)}) copy-start(f32[192,64]{0,1:T(8,128)} %param.21) | copy-start | bytes 147460
  210.4 5.3 %copy-start.2 = (f32[1,768,768]{2,1,0:T(8,128)S(1)}, f32[1,768,768]{2,1,0:T(8,128)}, u32[]{:S(2)}) copy-start(f32[1,768,768]{2,1,0:T(8,128)} %copy.50) | copy-start | bytes 7077892
  210.4 5.3 %collective-permute-start = (f32[1,768,768]{2,1,0:T(8,128)}, f32[1,768,768]{2,1,0:T(8,128)}, u32[]{:S(2)}, u32[]{:S(2)}) collective-permute-start(f32[1,768,768]{2,1,0:T(8,128)} %copy.50), channel_id=1, source_target_pairs={{0,1},{1,0},{2,3},{3,2},{4,5},{5,4},{6,7},{7,6},{8,9},{9,8},{10,11... | collective-permute-start | bytes 7077896 | tf_op jit(solution)/shard_map/ppermute | solution.py:109
Sparse Core Ops, SparseCore 0:
  52.9 112.7 all-reduce.1

commit v8 on v7

--- a/solution.py
+++ b/solution.py
@@ -21,6 +21,25 @@
     first_prod = jnp.einsum("bik,bkj->bij", current, gram_matrix, precision=HIGH)
     second_prod = jnp.einsum("bik,bkj->bij", first_prod, gram_matrix, precision=HIGH)
     return linear_coef * current + cubic_coef * first_prod + quintic_coef * second_prod
+
+
+def symmetric_psum(full, axes):
+    size = full.shape[-1]
+    block = 128 if size % 128 == 0 else size
+    count = size // block
+    strips = [full[:, i * block : (i + 1) * block, i * block :] for i in range(count)]
+    summed = lax.psum(jnp.concatenate(strips, 2), axes)
+    rows = []
+    offset = 0
+    for i in range(count):
+        width = size - i * block
+        strip = summed[:, :, offset : offset + width]
+        offset += width
+        rows.append(jnp.pad(strip, ((0, 0), (0, 0), (i * block, 0))))
+    upper = jnp.concatenate(rows, 1)
+    block_index = jnp.arange(size) // block
+    strict = block_index[:, None] < block_index[None, :]
+    return upper + jnp.swapaxes(jnp.where(strict, upper, 0.0), 1, 2)
 
 
 def shards(
@@ -87,7 +106,7 @@
     placed = lax.dynamic_update_slice_in_dim(
         jnp.zeros_like(partial_stat), 0.95 * stats_all, row_start, 1
     )
-    stats_full = lax.psum(placed + 0.05 * partial_stat, ("tensor", "dp"))
+    stats_full = symmetric_psum(placed + 0.05 * partial_stat, ("tensor", "dp"))
     stats_full, expert_weights, dense_weights, expert_master_out, dense_master_out = (
         lax.optimization_barrier(
             (stats_full, expert_weights, dense_weights, expert_master_out, dense_master_out)

time: 230 us -> 243 us (1.057)
  local copies, waits for them, and re-layouts: 15 us -> 33.6 us
  waiting for transfers between devices: 42.5 us -> 36.3 us
  other arithmetic: 9.78 us -> 14 us
  matrix products: 53.4 us -> 49.6 us
    unnamed x28 -> x46, local copies, waits for them, and re-layouts: 5.52 us -> 16.4 us
    concatenate x0 -> x3, local copies, waits for them, and re-layouts: none -> 7.75 us  [the longest x2 7.09 us: symmetric_psum(): upper = jnp.concatenate(rows, 1)]
    psum x1, waiting for transfers between devices: 27.8 us -> 22.8 us  [symmetric_psum(): summed = lax.psum(jnp.concatenate(strips, 2), axes)]
    add x1 -> x2, other arithmetic: 1.59 us -> 4.62 us  [the longest x1 4.58 us: symmetric_psum(): return upper + jnp.swapaxes(jnp.where(strict, upper, 0.0), 1, 2)]
where the time goes in v8:
time: 243 us; the launch traced here: 241 us
  blocking collectives  85.5 us (35%)
  matrix products  49.6 us (20%)
  waiting for transfers between devices  36.3 us (15%)
  local copies, waits for them, and re-layouts  33.6 us (14%)
  between operations  15.1 us (6%)
  other arithmetic  14 us (6%)
  starting transfers between devices  6.52 us (3%)
    all_gather x1, blocking collectives, shards(): lax.all_gather(dense_master_out.astype(jnp.bfloat16), 'dp', axis=1, tiled...  30.6 us
    all_gather x1, blocking collectives, shards(): lax.all_gather(expert_master_out.astype(jnp.bfloat16), 'dp', axis=2, tile...  29.7 us
    psum x1, waiting for transfers between devices, symmetric_psum(): summed = lax.psum(jnp.concatenate(strips, 2), axes)  22.8 us
    unnamed x46, local copies, waits for them, and re-layouts  16.4 us
    all_to_all x1, waiting for transfers between devices, shards(): received = lax.all_to_all(joined, 'dp', 0, 0, tiled=True)  13.5 us
    dot_general x3, matrix products, quintic_step(): jnp.einsum('bik,bkj->bij', first_prod, gram_matrix, precision=HIGH)  13.1 us
    all_gather x1, blocking collectives, shards(): lax.all_gather(dense_mean, 'wshard', axis=0, tiled=True)  12.8 us
    all_gather x1, blocking collectives, shards(): lax.all_gather(dense_first_out, 'wshard', axis=0, tiled=True)  12.4 us
  transfers between devices with their start and end apart: 3, of which 2 were waited for; matrix products, arithmetic and copies ran while one was open for 8% of the time, Pallas kernels for 0%

profile of v8, /device:TPU:0, one launch (start us, length us, event | category | flops | bytes accessed | tf_op | source)
XLA Modules:
  0.0 241.0 jit_solution(14994183330858346767)
XLA Ops:
  8.2 1.4 copy.46
  10.8 6.5 %all-to-all-start = ((bf16[8,960,64]{1,2,0:T(8,128)(2,1)}), bf16[8,960,64]{1,2,0:T(8,128)(2,1)S(1)}, u32[]{:S(2)}, u32[]{:S(2)}) async-start(bf16[8,960,64]{1,2,0:T(8,128)(2,1)} %maximum_bitcast_fusion), calls=%async_computation | async-start | bytes 2097152 | tf_op jit(solution)/shard_map/all_to_all | solution.py:67
  18.5 13.5 %all-to-all-done = bf16[8,960,64]{1,2,0:T(8,128)(2,1)S(1)} async-done(((bf16[8,960,64]{1,2,0:T(8,128)(2,1)}), bf16[8,960,64]{1,2,0:T(8,128)(2,1)S(1)}, u32[]{:S(2)}, u32[]{:S(2)}) %all-to-all-start) | async-done | bytes 983072 | tf_op jit(solution)/shard_map/all_to_all | solution.py:67
  32.3 12.8 %all-gather = f32[4,192,64]{1,2,0:T(8,128)S(1)} all-gather(f32[1,192,64]{1,2,0:T(8,128)S(1)} %get-tuple-element.93), channel_id=1, replica_groups=mesh['dp'=8,'wshard'=4,'tensor'=4] {'wshard'}, dimensions={0}, use_global_device_ids=true | all-gather | bytes 245760 | tf_op jit(solution)/shard_map/all_gather | solution.py:76
  45.5 4.2 %broadcast_multiply_fusion = f32[2,768,768]{2,1,0:T(8,128)S(1)} fusion(f32[1,768,64]{1,2,0:T(8,128)S(1)} %broadcast_in_dim.28, f32[1,768,64]{1,2,0:T(8,128)S(1)} %multiply_bitcast_fusion.1), kind=kOutput, calls=%fused_computation.21 | convolution fusion | flops 907247616 | bytes 5111808 | tf_op jit(solution)/shard_map/bic,bjc->bij/dot_general | solution.py:102
  54.8 12.4 %all-gather.1 = f32[4,192,64]{1,2,0:T(8,128)S(1)} all-gather(f32[1,192,64]{1,2,0:T(8,128)S(1)} %bitcast.76), channel_id=1, replica_groups=mesh['dp'=8,'wshard'=4,'tensor'=4] {'wshard'}, dimensions={0}, use_global_device_ids=true | all-gather | bytes 245760 | tf_op jit(solution)/shard_map/all_gather | solution.py:77
  68.6 4.6 %fusion.6 = f32[2,768,128]{1,2,0:T(8,128)S(1)} fusion(f32[1,768,768]{2,1,0:T(8,128)S(1)} %bitcast.71, f32[1,768,768]{2,1,0:T(8,128)} %param.20, f32[1,768,64]{1,2,0:T(8,128)S(1)} %broadcast_in_dim.33, f32[1,768,64]{1,2,0:T(8,128)S(1)} %bitcast_add_fusion.2, f32[1,768,64]{1,2,0:T(8,128)S(1)} %broadcast_in_dim.28, f32[1,768,64]{1,2,0:T(8,128)S(1)} %multiply_bitcast_fusion.1), kind=kOutput, calls=%fused_computation.12 | convolution fusion | flops 1813708800 | bytes 6291456 | tf_op jit(solution)/shard_map/bki,bkc->bic/dot_general | solution.py:84
  73.4 4.8 %fusion.5 = f32[2,768,64]{1,2,0:T(8,128)S(1)} fusion(f32[1,768,768]{2,1,0:T(8,128)S(1)} %bitcast.72, f32[1,768,768]{2,1,0:T(8,128)S(1)} %copy-done.3, f32[2,768,128]{1,2,0:T(8,128)S(1)} %fusion.6, f32[2,768,64]{1,2,0:T(8,128)S(1)} %fusion.20), kind=kOutput, calls=%fused_computation.11 | convolution fusion | flops 907345920 | bytes 5898240 | tf_op jit(solution)/shard_map/bik,bkc->bic/dot_general | solution.py:91
  79.6 30.6 %all_gather.15 = bf16[192,512]{0,1:T(8,128)(2,1)} all-gather(bf16[192,64]{0,1:T(8,128)(2,1)S(1)} %get-tuple-element.81), channel_id=1, replica_groups=mesh['dp'=8,'wshard'=4,'tensor'=4] {'dp'}, dimensions={1}, use_global_device_ids=true | all-gather | bytes 221184 | tf_op jit(solution)/shard_map/all_gather | solution.py:100
  110.2 29.7 %all_gather.14 = bf16[1,768,512]{1,2,0:T(8,128)(2,1)S(1)} all-gather(bf16[1,768,64]{1,2,0:T(8,128)(2,1)S(1)} %get-tuple-element.83), channel_id=1, replica_groups=mesh['dp'=8,'wshard'=4,'tensor'=4] {'dp'}, dimensions={2}, use_global_device_ids=true | all-gather | bytes 884736 | tf_op jit(solution)/shard_map/all_gather | solution.py:99
  139.9 22.8 %all-reduce.7.cloned.1.call-done = f32[2,128,2688]{2,1,0:T(8,128)} async-done(((f32[2,128,2688]{2,1,0:T(8,128)}), f32[2,128,2688]{2,1,0:T(8,128)}) %all-reduce.7.cloned.1.call-update) | async-done | bytes 2752528 | tf_op jit(solution)/shard_map/psum | solution.py:31
  162.7 2.2 slice_dynamic-update-slice_fusion
  169.6 6.1 %copy.49 = f32[2,768,768]{1,2,0:T(8,128)} copy(f32[2,768,768]{2,1,0:T(8,128)} %pad_dynamic-update-slice_fusion) | data formatting | bytes 9437184 | tf_op jit(solution)/shard_map/concatenate | solution.py:39
  175.8 4.6 %bitcast_add_fusion.1 = f32[2,768,768]{2,1,0:T(8,128)S(1)} fusion(f32[2,768,768]{2,1,0:T(8,128)} %pad_dynamic-update-slice_fusion, f32[2,768,768]{1,2,0:T(8,128)} %copy.49, pred[768,768]{0,1:T(8,128)(4,1)S(1)} %copy-done.6), kind=kLoop, calls=%fused_computation.10 | loop fusion | flops 2359296 | bytes 14745600 | tf_op jit(solution)/shard_map/add | solution.py:42
  180.9 3.9 %multiply_reduce_fusion = (f32[]{:T(128)}, f32[768,768]{1,0:T(8,128)S(1)}) fusion(s32[]{:T(128)S(6)} %select_n.49, f32[1,768,768]{2,1,0:T(8,128)S(1)} %copy-done.4, f32[1,768,768]{2,1,0:T(8,128)S(1)} %bitcast.73, f32[2,768,768]{2,1,0:T(8,128)S(1)} %bitcast_add_fusion.1), kind=kOutput, calls=%fused_computation.19 | convolution fusion | flops 2719678464 | bytes 9438212 | tf_op jit(solution)/shard_map/bik,bkj->bij/dot_general | solution.py:120
  185.6 1.6 multiply_bitcast_fusion
  187.1 2.0 copy.51
  189.2 32.5 %while.10 = (s32[]{:T(128)}, f32[1,768,768]{1,2,0:T(8,128)S(1)}, s32[]{:T(128)}) while((s32[]{:T(128)}, f32[1,768,768]{1,2,0:T(8,128)S(1)}, s32[]{:T(128)}) %tuple.38), condition=%wide.region_4.5_spmd, body=%wide.region_3.4_spmd.sunk | while | flops 8156676096 | bytes 21233708 | solution.py:127
  189.4 3.0 %fusion.58 = f32[768,768]{1,0:T(8,128)S(1)} fusion(f32[1,768,768]{1,2,0:T(8,128)S(1)} %get-tuple-element.113), kind=kOutput, calls=%fused_computation.4.clone.1 | convolution fusion | flops 2717908992 | bytes 4718592 | tf_op jit(solution)/shard_map/while/body/eval_jaxpr/bki,bkj->bij/dot_general | solution.py:17
  192.5 3.3 %fusion.59 = f32[768,768]{1,0:T(8,128)S(1)} fusion(f32[768,768]{1,0:T(8,128)S(1)} %fusion.58, f32[1,768,768]{1,2,0:T(8,128)S(1)} %get-tuple-element.113), kind=kOutput, calls=%fused_computation.2.clone.1 | convolution fusion | flops 2717908992 | bytes 7077888 | tf_op jit(solution)/shard_map/while/body/eval_jaxpr/bik,bkj->bij/dot_general | solution.py:21
  195.8 4.4 %fusion.60 = f32[1,768,768]{1,2,0:T(8,128)S(1)} fusion(f32[768,768]{1,0:T(8,128)S(1)} %fusion.59, f32[1,768,768]{1,2,0:T(8,128)S(1)} %get-tuple-element.113, f32[768,768]{1,0:T(8,128)S(1)} %fusion.58), kind=kOutput, calls=%fused_computation.1.clone.1 | convolution fusion | flops 2720858112 | bytes 9437184 | tf_op jit(solution)/shard_map/while/body/eval_jaxpr/bik,bkj->bij/dot_general | solution.py:22
  200.2 3.0 %fusion.58 = f32[768,768]{1,0:T(8,128)S(1)} fusion(f32[1,768,768]{1,2,0:T(8,128)S(1)} %get-tuple-element.113), kind=kOutput, calls=%fused_computation.4.clone.1 | convolution fusion | flops 2717908992 | bytes 4718592 | tf_op jit(solution)/shard_map/while/body/eval_jaxpr/bki,bkj->bij/dot_general | solution.py:17
  203.2 3.3 %fusion.59 = f32[768,768]{1,0:T(8,128)S(1)} fusion(f32[768,768]{1,0:T(8,128)S(1)} %fusion.58, f32[1,768,768]{1,2,0:T(8,128)S(1)} %get-tuple-element.113), kind=kOutput, calls=%fused_computation.2.clone.1 | convolution fusion | flops 2717908992 | bytes 7077888 | tf_op jit(solution)/shard_map/while/body/eval_jaxpr/bik,bkj->bij/dot_general | solution.py:21
  206.5 4.4 %fusion.60 = f32[1,768,768]{1,2,0:T(8,128)S(1)} fusion(f32[768,768]{1,0:T(8,128)S(1)} %fusion.59, f32[1,768,768]{1,2,0:T(8,128)S(1)} %get-tuple-element.113, f32[768,768]{1,0:T(8,128)S(1)} %fusion.58), kind=kOutput, calls=%fused_computation.1.clone.1 | convolution fusion | flops 2720858112 | bytes 9437184 | tf_op jit(solution)/shard_map/while/body/eval_jaxpr/bik,bkj->bij/dot_general | solution.py:22
  210.9 3.0 %fusion.58 = f32[768,768]{1,0:T(8,128)S(1)} fusion(f32[1,768,768]{1,2,0:T(8,128)S(1)} %get-tuple-element.113), kind=kOutput, calls=%fused_computation.4.clone.1 | convolution fusion | flops 2717908992 | bytes 4718592 | tf_op jit(solution)/shard_map/while/body/eval_jaxpr/bki,bkj->bij/dot_general | solution.py:17
  213.9 3.3 %fusion.59 = f32[768,768]{1,0:T(8,128)S(1)} fusion(f32[768,768]{1,0:T(8,128)S(1)} %fusion.58, f32[1,768,768]{1,2,0:T(8,128)S(1)} %get-tuple-element.113), kind=kOutput, calls=%fused_computation.2.clone.1 | convolution fusion | flops 2717908992 | bytes 7077888 | tf_op jit(solution)/shard_map/while/body/eval_jaxpr/bik,bkj->bij/dot_general | solution.py:21
  217.3 4.4 %fusion.60 = f32[1,768,768]{1,2,0:T(8,128)S(1)} fusion(f32[768,768]{1,0:T(8,128)S(1)} %fusion.59, f32[1,768,768]{1,2,0:T(8,128)S(1)} %get-tuple-element.113, f32[768,768]{1,0:T(8,128)S(1)} %fusion.58), kind=kOutput, calls=%fused_computation.1.clone.1 | convolution fusion | flops 2720858112 | bytes 9437184 | tf_op jit(solution)/shard_map/while/body/eval_jaxpr/bik,bkj->bij/dot_general | solution.py:22
  221.6 2.0 copy.53
  225.5 1.8 copy.56
  227.3 1.6 dynamic-slice_bitcast_fusion
  228.9 2.8 %maximum_select_fusion = f32[2,768,768]{2,1,0:T(8,128)S(1)} fusion(f32[1,768,768]{2,1,0:T(8,128)} %collective-permute-done, f32[1,768,768]{2,1,0:T(8,128)S(1)} %copy-done.5, pred[]{:T(512)S(6)} %eq.5), kind=kLoop, calls=%fused_computation.9 | loop fusion | flops 3538944 | bytes 9437185 | tf_op jit(solution)/shard_map/jit(_where)/select_n | solution.py:131
  231.7 2.5 %slice_bitcast_fusion = (f32[768,768]{1,0:T(8,128)}, f32[1,768,768]{2,1,0:T(8,128)}) fusion(f32[2,768,768]{2,1,0:T(8,128)S(1)} %maximum_select_fusion), kind=kLoop, calls=%fused_computation.16 | loop fusion | bytes 9437184 | tf_op jit(solution)/shard_map/squeeze | solution.py:147
  (75 shorter events, 19.2 us)
Async XLA Ops:
  10.8 21.5 %copy-start.15 = (f32[192,64]{0,1:T(8,128)S(1)}, f32[192,64]{0,1:T(8,128)}, u32[]{:S(2)}) copy-start(f32[192,64]{0,1:T(8,128)} %param.22) | copy-start | bytes 147460
  10.8 21.3 %all-to-all-start = ((bf16[8,960,64]{1,2,0:T(8,128)(2,1)}), bf16[8,960,64]{1,2,0:T(8,128)(2,1)S(1)}, u32[]{:S(2)}, u32[]{:S(2)}) async-start(bf16[8,960,64]{1,2,0:T(8,128)(2,1)} %maximum_bitcast_fusion), calls=%async_computation | async-start | bytes 2097152 | tf_op jit(solution)/shard_map/all_to_all | solution.py:67
  17.3 145.4 %all-reduce.7.cloned.1.call-start = ((), (), s32[]{:S(2)}) async-start(), calls=%async_computation.1 | async-start | bytes 5505024 | tf_op jit(solution)/shard_map/psum | solution.py:31
  32.3 22.5 %copy-start.8 = (f32[192,64]{0,1:T(8,128)}, f32[192,64]{0,1:T(8,128)S(1)}, u32[]{:S(2)}) copy-start(f32[192,64]{0,1:T(8,128)S(1)} %get-tuple-element.92) | copy-start | bytes 147460
  45.3 4.4 %copy-start.12 = (f32[24,768]{1,0:T(8,128)S(1)}, f32[24,768]{1,0:T(8,128)}, u32[]{:S(2)}) copy-start(f32[24,768]{1,0:T(8,128)} %param.24) | copy-start | bytes 221188
  45.3 4.4 %copy-start.13 = (f32[1,24,768]{2,1,0:T(8,128)S(1)}, f32[1,24,768]{2,1,0:T(8,128)}, u32[]{:S(2)}) copy-start(f32[1,24,768]{2,1,0:T(8,128)} %param.19) | copy-start | bytes 221188
  53.4 15.2 %copy-start.1 = (f32[768,768]{1,0:T(8,128)S(1)}, f32[768,768]{1,0:T(8,128)}, u32[]{:S(2)}) copy-start(f32[768,768]{1,0:T(8,128)} %param.25) | copy-start | bytes 7077892
  68.6 4.6 %copy-start.7 = (f32[1,768,64]{1,2,0:T(8,128)}, f32[1,768,64]{1,2,0:T(8,128)S(1)}, u32[]{:S(2)}) copy-start(f32[1,768,64]{1,2,0:T(8,128)S(1)} %bitcast_add_fusion.2) | copy-start | bytes 589828
  68.6 4.6 %copy-start.9 = (f32[768,64]{0,1:T(8,128)S(1)}, f32[768,64]{0,1:T(8,128)}, u32[]{:S(2)}) copy-start(f32[768,64]{0,1:T(8,128)} %param.23) | copy-start | bytes 589828
  68.6 4.6 %copy-start.10 = (f32[1,768,64]{1,2,0:T(8,128)S(1)}, f32[1,768,64]{1,2,0:T(8,128)}, u32[]{:S(2)}) copy-start(f32[1,768,64]{1,2,0:T(8,128)} %param.18) | copy-start | bytes 589828
  68.6 4.7 %copy-start.3 = (f32[1,768,768]{2,1,0:T(8,128)S(1)}, f32[1,768,768]{2,1,0:T(8,128)}, u32[]{:S(2)}) copy-start(f32[1,768,768]{2,1,0:T(8,128)} %param.20) | copy-start | bytes 7077892
  73.3 4.8 %copy-start.11 = (f32[1,768,64]{1,2,0:T(8,128)S(1)}, f32[1,768,64]{1,2,0:T(8,128)}, u32[]{:S(2)}) copy-start(f32[1,768,64]{1,2,0:T(8,128)} %param.16) | copy-start | bytes 589828
  73.3 5.5 %copy-start.14 = (f32[192,64]{0,1:T(8,128)S(1)}, f32[192,64]{0,1:T(8,128)}, u32[]{:S(2)}) copy-start(f32[192,64]{0,1:T(8,128)} %param.21) | copy-start | bytes 147460
  162.7 2.2 slice-start
  162.7 3.2 %slice-start.1 = ((f32[2,128,2688]{2,1,0:T(8,128)}), f32[2,128,512]{2,1,0:T(8,128)S(1)}, s32[]{:S(2)}) async-start(f32[2,128,2688]{2,1,0:T(8,128)} %all-reduce.7.cloned.1.call-done), calls=%async_computation.3 | async-start | bytes 1048576 | tf_op jit(solution)/shard_map/slice | solution.py:36
  164.9 1.9 slice-start.2
  165.9 1.9 slice-start.3
  165.9 2.8 %slice-start.4 = ((f32[2,128,2688]{2,1,0:T(8,128)}), f32[2,128,128]{2,1,0:T(8,128)S(1)}, s32[]{:S(2)}) async-start(f32[2,128,2688]{2,1,0:T(8,128)} %all-reduce.7.cloned.1.call-done), calls=%async_computation.6 | async-start | bytes 262144 | tf_op jit(solution)/shard_map/slice | solution.py:36
  169.6 6.1 %copy-start.6 = (pred[768,768]{0,1:T(8,128)(4,1)S(1)}, pred[768,768]{0,1:T(8,128)(4,1)}, u32[]{:S(2)}) copy-start(pred[768,768]{0,1:T(8,128)(4,1)} %broadcast_compare_fusion) | copy-start | bytes 1769476
  175.8 4.6 %copy-start.2 = (f32[768,768]{1,0:T(8,128)S(1)}, f32[768,768]{1,0:T(8,128)}, u32[]{:S(2)}) copy-start(f32[768,768]{1,0:T(8,128)} %param.25) | copy-start | bytes 7077892
  175.8 5.1 %copy-start.4 = (f32[1,768,768]{2,1,0:T(8,128)S(1)}, f32[1,768,768]{2,1,0:T(8,128)}, u32[]{:S(2)}) copy-start(f32[1,768,768]{2,1,0:T(8,128)} %param.20) | copy-start | bytes 7077892
  180.4 4.5 %copy-start = (f32[2,768,768]{2,1,0:T(8,128)}, f32[2,768,768]{2,1,0:T(8,128)S(1)}, u32[]{:S(2)}) copy-start(f32[2,768,768]{2,1,0:T(8,128)S(1)} %bitcast_add_fusion.1) | copy-start | bytes 14155780
  223.6 5.3 %copy-start.5 = (f32[1,768,768]{2,1,0:T(8,128)S(1)}, f32[1,768,768]{2,1,0:T(8,128)}, u32[]{:S(2)}) copy-start(f32[1,768,768]{2,1,0:T(8,128)} %copy.53) | copy-start | bytes 7077892
  223.6 5.3 %collective-permute-start = (f32[1,768,768]{2,1,0:T(8,128)}, f32[1,768,768]{2,1,0:T(8,128)}, u32[]{:S(2)}, u32[]{:S(2)}) collective-permute-start(f32[1,768,768]{2,1,0:T(8,128)} %copy.53), channel_id=1, source_target_pairs={{0,1},{1,0},{2,3},{3,2},{4,5},{5,4},{6,7},{7,6},{8,9},{9,8},{10,11... | collective-permute-start | bytes 7077896 | tf_op jit(solution)/shard_map/ppermute | solution.py:128
Sparse Core Ops, SparseCore 0:
  54.9 107.7 all-reduce.6

commit v9 on v7

--- a/solution.py
+++ b/solution.py
@@ -87,7 +87,7 @@
     placed = lax.dynamic_update_slice_in_dim(
         jnp.zeros_like(partial_stat), 0.95 * stats_all, row_start, 1
     )
-    stats_full = lax.psum(placed + 0.05 * partial_stat, ("tensor", "dp"))
+    stats_full = lax.psum(lax.psum(placed + 0.05 * partial_stat, "dp"), "tensor")
     stats_full, expert_weights, dense_weights, expert_master_out, dense_master_out = (
         lax.optimization_barrier(
             (stats_full, expert_weights, dense_weights, expert_master_out, dense_master_out)

time: 230 us -> 340 us (1.48)
  waiting for transfers between devices: 42.5 us -> 149 us
  blocking collectives: 85.5 us -> 89.5 us
    psum x1 -> x2, waiting for transfers between devices: 27.8 us -> 135 us  [the longest x1 115 us: shards(): lax.psum(placed + 0.05 * partial_stat, 'dp')]
  transfers between devices with their start and end apart: 3 -> 4, of which waited for: 2 -> 3; matrix products, arithmetic and copies ran while one was open for 8% -> 5% of each run, Pallas kernels for 0% -> 0%
where the time goes in v9:
time: 340 us; the launch traced here: 339 us
  waiting for transfers between devices  149 us (44%)
  blocking collectives  89.5 us (26%)
  matrix products  53.3 us (16%)
  between operations  15 us (4%)
  local copies, waits for them, and re-layouts  14.9 us (4%)
  other arithmetic  9.77 us (3%)
  starting transfers between devices  6.99 us (2%)
    psum x1, waiting for transfers between devices, shards(): lax.psum(placed + 0.05 * partial_stat, 'dp')  115 us
    all_gather x1, blocking collectives, shards(): lax.all_gather(expert_master_out.astype(jnp.bfloat16), 'dp', axis=2, tile...  32.2 us
    all_gather x1, blocking collectives, shards(): lax.all_gather(dense_master_out.astype(jnp.bfloat16), 'dp', axis=1, tiled...  31.7 us
    psum x1, waiting for transfers between devices, shards(): lax.psum(lax.psum(placed + 0.05 * partial_stat, 'dp'), 'tensor')  20 us
    all_to_all x1, waiting for transfers between devices, shards(): received = lax.all_to_all(joined, 'dp', 0, 0, tiled=True)  14.7 us
    dot_general x3, matrix products, quintic_step(): jnp.einsum('bik,bkj->bij', first_prod, gram_matrix, precision=HIGH)  13.1 us
    all_gather x1, blocking collectives, shards(): lax.all_gather(dense_mean, 'wshard', axis=0, tiled=True)  12.8 us
    all_gather x1, blocking collectives, shards(): lax.all_gather(dense_first_out, 'wshard', axis=0, tiled=True)  12.7 us
  transfers between devices with their start and end apart: 4, of which 3 were waited for; matrix products, arithmetic and copies ran while one was open for 5% of the time, Pallas kernels for 0%

profile of v9, /device:TPU:0, one launch (start us, length us, event | category | flops | bytes accessed | tf_op | source)
XLA Modules:
  0.0 339.1 jit_solution(14700776913197168125)
XLA Ops:
  8.2 1.4 copy.44
  10.8 6.5 %all-to-all-start = ((bf16[8,960,64]{1,2,0:T(8,128)(2,1)}), bf16[8,960,64]{1,2,0:T(8,128)(2,1)S(1)}, u32[]{:S(2)}, u32[]{:S(2)}) async-start(bf16[8,960,64]{1,2,0:T(8,128)(2,1)} %maximum_bitcast_fusion), calls=%async_computation | async-start | bytes 2097152 | tf_op jit(solution)/shard_map/all_to_all | solution.py:48
  17.3 14.7 %all-to-all-done = bf16[8,960,64]{1,2,0:T(8,128)(2,1)S(1)} async-done(((bf16[8,960,64]{1,2,0:T(8,128)(2,1)}), bf16[8,960,64]{1,2,0:T(8,128)(2,1)S(1)}, u32[]{:S(2)}, u32[]{:S(2)}) %all-to-all-start) | async-done | bytes 983072 | tf_op jit(solution)/shard_map/all_to_all | solution.py:48
  32.3 12.8 %all-gather = f32[4,192,64]{1,2,0:T(8,128)S(1)} all-gather(f32[1,192,64]{1,2,0:T(8,128)S(1)} %get-tuple-element.93), channel_id=1, replica_groups=mesh['dp'=8,'wshard'=4,'tensor'=4] {'wshard'}, dimensions={0}, use_global_device_ids=true | all-gather | bytes 245760 | tf_op jit(solution)/shard_map/all_gather | solution.py:57
  45.5 5.6 %broadcast_multiply_fusion = f32[2,768,768]{2,1,0:T(8,128)} fusion(f32[1,768,64]{1,2,0:T(8,128)S(1)} %broadcast_in_dim.18, f32[1,768,64]{1,2,0:T(8,128)S(1)} %multiply_bitcast_fusion.1), kind=kOutput, calls=%fused_computation.20 | convolution fusion | flops 907247616 | bytes 5111808 | tf_op jit(solution)/shard_map/bic,bjc->bij/dot_general | solution.py:83
  51.1 1.6 fusion.29
  52.7 114.7 %all-reduce.3.cloned.1.call-done = f32[2,768,768]{2,1,0:T(8,128)} async-done(((f32[2,768,768]{2,1,0:T(8,128)}), f32[2,768,768]{2,1,0:T(8,128)}) %all-reduce.3.cloned.1.call-update) | async-done | bytes 4718608 | tf_op jit(solution)/shard_map/psum | solution.py:90
  167.5 12.7 %all-gather.1 = f32[4,192,64]{1,2,0:T(8,128)S(1)} all-gather(f32[1,192,64]{1,2,0:T(8,128)S(1)} %bitcast.74), channel_id=1, replica_groups=mesh['dp'=8,'wshard'=4,'tensor'=4] {'wshard'}, dimensions={0}, use_global_device_ids=true | all-gather | bytes 245760 | tf_op jit(solution)/shard_map/all_gather | solution.py:58
  181.6 4.6 %fusion.6 = f32[2,768,128]{1,2,0:T(8,128)S(1)} fusion(f32[1,768,768]{2,1,0:T(8,128)S(1)} %bitcast.70, f32[1,768,768]{2,1,0:T(8,128)} %param.20, f32[1,768,64]{1,2,0:T(8,128)S(1)} %broadcast_in_dim.21, f32[1,768,64]{1,2,0:T(8,128)S(1)} %bitcast_add_fusion.1, f32[1,768,64]{1,2,0:T(8,128)S(1)} %broadcast_in_dim.18, f32[1,768,64]{1,2,0:T(8,128)S(1)} %multiply_bitcast_fusion.1), kind=kOutput, calls=%fused_computation.11 | convolution fusion | flops 1813708800 | bytes 6291456 | tf_op jit(solution)/shard_map/bki,bkc->bic/dot_general | solution.py:65
  186.3 4.8 %fusion.5 = f32[2,768,64]{1,2,0:T(8,128)S(1)} fusion(f32[1,768,768]{2,1,0:T(8,128)S(1)} %bitcast.71, f32[1,768,768]{2,1,0:T(8,128)S(1)} %copy-done.1, f32[2,768,128]{1,2,0:T(8,128)S(1)} %fusion.6, f32[2,768,64]{1,2,0:T(8,128)S(1)} %fusion.20), kind=kOutput, calls=%fused_computation.10 | convolution fusion | flops 907345920 | bytes 5898240 | tf_op jit(solution)/shard_map/bik,bkc->bic/dot_general | solution.py:72
  192.5 31.7 %all_gather.15 = bf16[192,512]{0,1:T(8,128)(2,1)} all-gather(bf16[192,64]{0,1:T(8,128)(2,1)S(1)} %get-tuple-element.81), channel_id=1, replica_groups=mesh['dp'=8,'wshard'=4,'tensor'=4] {'dp'}, dimensions={1}, use_global_device_ids=true | all-gather | bytes 221184 | tf_op jit(solution)/shard_map/all_gather | solution.py:81
  224.2 32.2 %all_gather.14 = bf16[1,768,512]{1,2,0:T(8,128)(2,1)S(1)} all-gather(bf16[1,768,64]{1,2,0:T(8,128)(2,1)S(1)} %get-tuple-element.83), channel_id=1, replica_groups=mesh['dp'=8,'wshard'=4,'tensor'=4] {'dp'}, dimensions={2}, use_global_device_ids=true | all-gather | bytes 884736 | tf_op jit(solution)/shard_map/all_gather | solution.py:80
  256.5 20.0 %all-reduce.5.cloned.1.call-done = f32[2,768,768]{2,1,0:T(8,128)} async-done(((f32[2,768,768]{2,1,0:T(8,128)}), f32[2,768,768]{2,1,0:T(8,128)}) %all-reduce.5.cloned.1.call-update) | async-done | bytes 4718608 | tf_op jit(solution)/shard_map/psum | solution.py:90
  276.4 6.3 %multiply_reduce_fusion = (f32[]{:T(128)}, f32[768,768]{1,0:T(8,128)S(1)}) fusion(s32[]{:T(128)S(6)} %select_n.30, f32[1,768,768]{2,1,0:T(8,128)} %param.20, f32[1,768,768]{2,1,0:T(8,128)} %bitcast.69, f32[2,768,768]{2,1,0:T(8,128)} %all-reduce.5.cloned.1.call-done), kind=kOutput, calls=%fused_computation.18 | convolution fusion | flops 2719678464 | bytes 9438212 | tf_op jit(solution)/shard_map/bik,bkj->bij/dot_general | solution.py:101
  283.4 1.6 multiply_bitcast_fusion
  285.0 2.0 copy.48
  287.0 32.2 %while.10 = (s32[]{:T(128)}, f32[1,768,768]{1,2,0:T(8,128)S(1)}, s32[]{:T(128)}) while((s32[]{:T(128)}, f32[1,768,768]{1,2,0:T(8,128)S(1)}, s32[]{:T(128)}) %tuple.38), condition=%wide.region_5.6_spmd, body=%wide.region_4.5_spmd.sunk | while | flops 8156676096 | bytes 21233708 | solution.py:108
  287.0 3.0 fusion.55
  290.1 3.3 fusion.56
  293.4 4.4 %fusion.57 = f32[1,768,768]{1,2,0:T(8,128)S(1)} fusion(f32[768,768]{1,0:T(8,128)S(1)} %fusion.56, f32[1,768,768]{1,2,0:T(8,128)S(1)} %get-tuple-element.113, f32[768,768]{1,0:T(8,128)S(1)} %fusion.55), kind=kOutput, calls=%fused_computation.1.clone.1 | convolution fusion | flops 2720858112 | bytes 9437184 | tf_op jit(solution)/shard_map/while/body/eval_jaxpr/bik,bkj->bij/dot_general | solution.py:22
  297.8 3.0 fusion.55
  300.8 3.3 fusion.56
  304.1 4.4 %fusion.57 = f32[1,768,768]{1,2,0:T(8,128)S(1)} fusion(f32[768,768]{1,0:T(8,128)S(1)} %fusion.56, f32[1,768,768]{1,2,0:T(8,128)S(1)} %get-tuple-element.113, f32[768,768]{1,0:T(8,128)S(1)} %fusion.55), kind=kOutput, calls=%fused_computation.1.clone.1 | convolution fusion | flops 2720858112 | bytes 9437184 | tf_op jit(solution)/shard_map/while/body/eval_jaxpr/bik,bkj->bij/dot_general | solution.py:22
  308.5 3.0 fusion.55
  311.6 3.3 fusion.56
  314.9 4.4 %fusion.57 = f32[1,768,768]{1,2,0:T(8,128)S(1)} fusion(f32[768,768]{1,0:T(8,128)S(1)} %fusion.56, f32[1,768,768]{1,2,0:T(8,128)S(1)} %get-tuple-element.113, f32[768,768]{1,0:T(8,128)S(1)} %fusion.55), kind=kOutput, calls=%fused_computation.1.clone.1 | convolution fusion | flops 2720858112 | bytes 9437184 | tf_op jit(solution)/shard_map/while/body/eval_jaxpr/bik,bkj->bij/dot_general | solution.py:22
  319.3 2.0 copy.50
  322.4 1.8 copy.53
  324.2 1.2 copy.52
  325.3 1.6 dynamic-slice_bitcast_fusion
  326.9 2.8 maximum_select_fusion
  329.7 2.5 slice_bitcast_fusion
  (44 shorter events, 6.9 us)
Async XLA Ops:
  10.8 21.5 %copy-start.11 = (f32[192,64]{0,1:T(8,128)S(1)}, f32[192,64]{0,1:T(8,128)}, u32[]{:S(2)}) copy-start(f32[192,64]{0,1:T(8,128)} %param.22) | copy-start | bytes 147460
  10.8 21.3 %all-to-all-start = ((bf16[8,960,64]{1,2,0:T(8,128)(2,1)}), bf16[8,960,64]{1,2,0:T(8,128)(2,1)S(1)}, u32[]{:S(2)}, u32[]{:S(2)}) async-start(bf16[8,960,64]{1,2,0:T(8,128)(2,1)} %maximum_bitcast_fusion), calls=%async_computation | async-start | bytes 2097152 | tf_op jit(solution)/shard_map/all_to_all | solution.py:48
  17.3 150.2 %all-reduce.3.cloned.1.call-start = ((), (), s32[]{:S(2)}) async-start(), calls=%async_computation.1 | async-start | bytes 9437184 | tf_op jit(solution)/shard_map/psum | solution.py:90
  32.3 135.2 %copy-start.4 = (f32[192,64]{0,1:T(8,128)}, f32[192,64]{0,1:T(8,128)S(1)}, u32[]{:S(2)}) copy-start(f32[192,64]{0,1:T(8,128)S(1)} %get-tuple-element.92) | copy-start | bytes 147460
  45.4 5.6 %copy-start.8 = (f32[24,768]{1,0:T(8,128)S(1)}, f32[24,768]{1,0:T(8,128)}, u32[]{:S(2)}) copy-start(f32[24,768]{1,0:T(8,128)} %param.24) | copy-start | bytes 221188
  45.5 5.6 %copy-start.9 = (f32[1,24,768]{2,1,0:T(8,128)S(1)}, f32[1,24,768]{2,1,0:T(8,128)}, u32[]{:S(2)}) copy-start(f32[1,24,768]{2,1,0:T(8,128)} %param.19) | copy-start | bytes 221188
  52.7 223.8 %all-reduce.5.cloned.1.call-start = ((), (), s32[]{:S(2)}) async-start(), calls=%async_computation.2 | async-start | bytes 9437184 | tf_op jit(solution)/shard_map/psum | solution.py:90
  167.4 14.1 %copy-start = (f32[768,768]{1,0:T(8,128)S(1)}, f32[768,768]{1,0:T(8,128)}, u32[]{:S(2)}) copy-start(f32[768,768]{1,0:T(8,128)} %param.25) | copy-start | bytes 7077892
  181.5 4.6 %copy-start.3 = (f32[1,768,64]{1,2,0:T(8,128)}, f32[1,768,64]{1,2,0:T(8,128)S(1)}, u32[]{:S(2)}) copy-start(f32[1,768,64]{1,2,0:T(8,128)S(1)} %bitcast_add_fusion.1) | copy-start | bytes 589828
  181.6 4.6 %copy-start.5 = (f32[768,64]{0,1:T(8,128)S(1)}, f32[768,64]{0,1:T(8,128)}, u32[]{:S(2)}) copy-start(f32[768,64]{0,1:T(8,128)} %param.23) | copy-start | bytes 589828
  181.6 4.6 %copy-start.6 = (f32[1,768,64]{1,2,0:T(8,128)S(1)}, f32[1,768,64]{1,2,0:T(8,128)}, u32[]{:S(2)}) copy-start(f32[1,768,64]{1,2,0:T(8,128)} %param.18) | copy-start | bytes 589828
  181.6 4.7 %copy-start.1 = (f32[1,768,768]{2,1,0:T(8,128)S(1)}, f32[1,768,768]{2,1,0:T(8,128)}, u32[]{:S(2)}) copy-start(f32[1,768,768]{2,1,0:T(8,128)} %param.20) | copy-start | bytes 7077892
  186.3 4.8 %copy-start.7 = (f32[1,768,64]{1,2,0:T(8,128)S(1)}, f32[1,768,64]{1,2,0:T(8,128)}, u32[]{:S(2)}) copy-start(f32[1,768,64]{1,2,0:T(8,128)} %param.16) | copy-start | bytes 589828
  186.3 5.5 %copy-start.10 = (f32[192,64]{0,1:T(8,128)S(1)}, f32[192,64]{0,1:T(8,128)}, u32[]{:S(2)}) copy-start(f32[192,64]{0,1:T(8,128)} %param.21) | copy-start | bytes 147460
  321.2 5.7 %copy-start.2 = (f32[1,768,768]{2,1,0:T(8,128)S(1)}, f32[1,768,768]{2,1,0:T(8,128)}, u32[]{:S(2)}) copy-start(f32[1,768,768]{2,1,0:T(8,128)} %copy.50) | copy-start | bytes 7077892
  321.2 5.7 %collective-permute-start = (f32[1,768,768]{2,1,0:T(8,128)}, f32[1,768,768]{2,1,0:T(8,128)}, u32[]{:S(2)}, u32[]{:S(2)}) collective-permute-start(f32[1,768,768]{2,1,0:T(8,128)} %copy.50), channel_id=1, source_target_pairs={{0,1},{1,0},{2,3},{3,2},{4,5},{5,4},{6,7},{7,6},{8,9},{9,8},{10,11... | collective-permute-start | bytes 7077896 | tf_op jit(solution)/shard_map/ppermute | solution.py:109
Sparse Core Ops, SparseCore 0:
  52.8 114.5 all-reduce.2
  170.0 106.4 all-reduce.4

commit v10 on v7

--- a/solution.py
+++ b/solution.py
@@ -14,12 +14,12 @@
 
 
 def local_gram(current):
-    return jnp.einsum("bki,bkj->bij", current, current, precision=HIGH)
+    return jnp.einsum("bik,bjk->bij", current, current, precision=HIGH)
 
 
 def quintic_step(current, gram_matrix):
-    first_prod = jnp.einsum("bik,bkj->bij", current, gram_matrix, precision=HIGH)
-    second_prod = jnp.einsum("bik,bkj->bij", first_prod, gram_matrix, precision=HIGH)
+    first_prod = jnp.einsum("bik,bkj->bij", gram_matrix, current, precision=HIGH)
+    second_prod = jnp.einsum("bik,bkj->bij", gram_matrix, first_prod, precision=HIGH)
     return linear_coef * current + cubic_coef * first_prod + quintic_coef * second_prod
 
 
@@ -109,23 +109,20 @@
     partner = lax.ppermute(
         current, "tensor", perm=[(t, t ^ 1) for t in range(tensor_size)]
     )
-    bases_out = jnp.where(
-        core == 0,
-        jnp.concatenate([current, partner], 0),
-        jnp.concatenate([partner, current], 0),
-    )
+    expert_basis_out = jnp.where(core == 0, current, partner)
+    dense_basis_out = jnp.where(core == 0, partner, current)[0]
     return (
         expert_master_out,
         expert_first_out,
         seconds_out[:experts_here],
         stats_out[:experts_here],
-        bases_out[:experts_here],
+        expert_basis_out,
         expert_weights,
         dense_master_out,
         dense_first_out,
         seconds_out[experts_here],
         stats_out[experts_here],
-        bases_out[experts_here],
+        dense_basis_out,
         dense_weights,
     )
 

time: 230 us -> 224 us (0.974)
  local copies, waits for them, and re-layouts: 15 us -> 8.47 us
    squeeze x0 -> x1, other arithmetic: none -> 4.15 us  [shards(): dense_basis_out = jnp.where(core == 0, partner, current)[0]]
    while x2 -> x0, local copies, waits for them, and re-layouts: 3.99 us -> none  [shards(): current = lax.fori_loop(0, NS_ITERS, ns_iteration, current)]
    select_n x1 -> x0, other arithmetic: 2.83 us -> none  [shards(): jnp.where(core == 0, jnp.concatenate([current, partner], 0), jnp.concaten...]
    squeeze x1 -> x0, local copies, waits for them, and re-layouts: 2.49 us -> none  [shards(): bases_out[experts_here]]
    unnamed x28 -> x26, local copies, waits for them, and re-layouts: 5.52 us -> 5.44 us
where the time goes in v10:
time: 224 us; the launch traced here: 222 us
  blocking collectives  85.6 us (38%)
  matrix products  52.7 us (24%)
  waiting for transfers between devices  42.5 us (19%)
  between operations  15 us (7%)
  other arithmetic  11.4 us (5%)
  local copies, waits for them, and re-layouts  8.47 us (4%)
  starting transfers between devices  6.61 us (3%)
    all_gather x1, blocking collectives, shards(): lax.all_gather(dense_master_out.astype(jnp.bfloat16), 'dp', axis=1, tiled...  30.7 us
    all_gather x1, blocking collectives, shards(): lax.all_gather(expert_master_out.astype(jnp.bfloat16), 'dp', axis=2, tile...  29.8 us
    psum x1, waiting for transfers between devices, shards(): stats_full = lax.psum(placed + 0.05 * partial_stat, ('tensor', 'dp'))  27.7 us
    all_to_all x1, waiting for transfers between devices, shards(): received = lax.all_to_all(joined, 'dp', 0, 0, tiled=True)  14.7 us
    all_gather x1, blocking collectives, shards(): lax.all_gather(dense_mean, 'wshard', axis=0, tiled=True)  12.8 us
    all_gather x1, blocking collectives, shards(): lax.all_gather(dense_first_out, 'wshard', axis=0, tiled=True)  12.4 us
    dot_general x3, matrix products, quintic_step(): jnp.einsum('bik,bkj->bij', gram_matrix, first_prod, precision=HIGH)  12.1 us
    dot_general x3, matrix products, quintic_step(): jnp.einsum('bik,bkj->bij', gram_matrix, current, precision=HIGH)  9.11 us
  transfers between devices with their start and end apart: 3, of which 2 were waited for; matrix products, arithmetic and copies ran while one was open for 8% of the time, Pallas kernels for 0%

profile of v10, /device:TPU:0, one launch (start us, length us, event | category | flops | bytes accessed | tf_op | source)
XLA Modules:
  0.0 222.4 jit_solution(10380669940565131510)
XLA Ops:
  7.2 1.1 copy.34
  8.2 1.4 copy.33
  9.7 1.1 maximum_bitcast_fusion
  10.8 6.5 %all-to-all-start = ((bf16[8,960,64]{1,2,0:T(8,128)(2,1)}), bf16[8,960,64]{1,2,0:T(8,128)(2,1)S(1)}, u32[]{:S(2)}, u32[]{:S(2)}) async-start(bf16[8,960,64]{1,2,0:T(8,128)(2,1)} %maximum_bitcast_fusion), calls=%async_computation | async-start | bytes 2097152 | tf_op jit(solution)/shard_map/all_to_all | solution.py:48
  17.3 14.7 %all-to-all-done = bf16[8,960,64]{1,2,0:T(8,128)(2,1)S(1)} async-done(((bf16[8,960,64]{1,2,0:T(8,128)(2,1)}), bf16[8,960,64]{1,2,0:T(8,128)(2,1)S(1)}, u32[]{:S(2)}, u32[]{:S(2)}) %all-to-all-start) | async-done | bytes 983072 | tf_op jit(solution)/shard_map/all_to_all | solution.py:48
  32.3 12.8 %all-gather = f32[4,192,64]{1,2,0:T(8,128)S(1)} all-gather(f32[1,192,64]{1,2,0:T(8,128)S(1)} %get-tuple-element.87), channel_id=1, replica_groups=mesh['dp'=8,'wshard'=4,'tensor'=4] {'wshard'}, dimensions={0}, use_global_device_ids=true | all-gather | bytes 245760 | tf_op jit(solution)/shard_map/all_gather | solution.py:57
  45.5 5.7 %broadcast_multiply_fusion = f32[2,768,768]{2,1,0:T(8,128)} fusion(f32[1,768,64]{1,2,0:T(8,128)S(1)} %broadcast_in_dim.18, f32[1,768,64]{1,2,0:T(8,128)S(1)} %multiply_bitcast_fusion.1), kind=kOutput, calls=%fused_computation.19 | convolution fusion | flops 907247616 | bytes 5111808 | tf_op jit(solution)/shard_map/bic,bjc->bij/dot_general | solution.py:83
  51.1 1.6 fusion.28
  52.8 12.4 %all-gather.1 = f32[4,192,64]{1,2,0:T(8,128)S(1)} all-gather(f32[1,192,64]{1,2,0:T(8,128)S(1)} %bitcast.72), channel_id=1, replica_groups=mesh['dp'=8,'wshard'=4,'tensor'=4] {'wshard'}, dimensions={0}, use_global_device_ids=true | all-gather | bytes 245760 | tf_op jit(solution)/shard_map/all_gather | solution.py:58
  65.5 1.0 bitcast_add_fusion.2
  66.6 4.6 %fusion.5 = f32[2,768,128]{1,2,0:T(8,128)S(1)} fusion(f32[1,768,768]{2,1,0:T(8,128)S(1)} %bitcast.67, f32[1,768,768]{2,1,0:T(8,128)} %param.20, f32[1,768,64]{1,2,0:T(8,128)S(1)} %broadcast_in_dim.21, f32[1,768,64]{1,2,0:T(8,128)S(1)} %bitcast_add_fusion.2, f32[1,768,64]{1,2,0:T(8,128)S(1)} %broadcast_in_dim.18, f32[1,768,64]{1,2,0:T(8,128)S(1)} %multiply_bitcast_fusion.1), kind=kOutput, calls=%fused_computation.10 | convolution fusion | flops 1813708800 | bytes 6291456 | tf_op jit(solution)/shard_map/bki,bkc->bic/dot_general | solution.py:65
  71.3 4.8 %fusion.4 = f32[2,768,64]{1,2,0:T(8,128)S(1)} fusion(f32[1,768,768]{2,1,0:T(8,128)S(1)} %bitcast.68, f32[1,768,768]{2,1,0:T(8,128)S(1)} %copy-done.1, f32[2,768,128]{1,2,0:T(8,128)S(1)} %fusion.5, f32[2,768,64]{1,2,0:T(8,128)S(1)} %fusion.19), kind=kOutput, calls=%fused_computation.9 | convolution fusion | flops 907345920 | bytes 5898240 | tf_op jit(solution)/shard_map/bik,bkc->bic/dot_general | solution.py:72
  77.5 30.7 %all_gather.15 = bf16[192,512]{0,1:T(8,128)(2,1)} all-gather(bf16[192,64]{0,1:T(8,128)(2,1)S(1)} %get-tuple-element.75), channel_id=1, replica_groups=mesh['dp'=8,'wshard'=4,'tensor'=4] {'dp'}, dimensions={1}, use_global_device_ids=true | all-gather | bytes 221184 | tf_op jit(solution)/shard_map/all_gather | solution.py:81
  108.1 29.8 %all_gather.14 = bf16[1,768,512]{1,2,0:T(8,128)(2,1)S(1)} all-gather(bf16[1,768,64]{1,2,0:T(8,128)(2,1)S(1)} %get-tuple-element.77), channel_id=1, replica_groups=mesh['dp'=8,'wshard'=4,'tensor'=4] {'dp'}, dimensions={2}, use_global_device_ids=true | all-gather | bytes 884736 | tf_op jit(solution)/shard_map/all_gather | solution.py:80
  137.9 27.7 %all-reduce.2.cloned.1.call-done = f32[2,768,768]{2,1,0:T(8,128)} async-done(((f32[2,768,768]{2,1,0:T(8,128)}), f32[2,768,768]{2,1,0:T(8,128)}) %all-reduce.2.cloned.1.call-update) | async-done | bytes 4718608 | tf_op jit(solution)/shard_map/psum | solution.py:90
  165.6 7.5 %multiply_reduce_fusion = (f32[]{:T(128)}, f32[768,768]{1,0:T(8,128)}) fusion(s32[]{:T(128)S(6)} %select_n.34, f32[1,768,768]{2,1,0:T(8,128)} %param.20, f32[1,768,768]{2,1,0:T(8,128)S(1)} %bitcast.69, f32[2,768,768]{2,1,0:T(8,128)} %all-reduce.2.cloned.1.call-done), kind=kOutput, calls=%fused_computation.17 | convolution fusion | flops 2719678464 | bytes 9438212 | tf_op jit(solution)/shard_map/bik,bkj->bij/dot_general | solution.py:101
  173.8 1.8 multiply_bitcast_fusion
  175.6 30.4 %while.10 = (s32[]{:T(128)}, f32[1,768,768]{2,1,0:T(8,128)S(1)}, s32[]{:T(128)}) while((s32[]{:T(128)}, f32[1,768,768]{2,1,0:T(8,128)S(1)}, s32[]{:T(128)}) %tuple.35), condition=%wide.region_4.5_spmd, body=%wide.region_3.4_spmd.sunk | while | flops 8156676096 | bytes 21233708 | solution.py:108
  175.6 3.0 %fusion.53 = f32[768,768]{1,0:T(8,128)S(1)} fusion(f32[1,768,768]{2,1,0:T(8,128)S(1)} %get-tuple-element.107), kind=kOutput, calls=%fused_computation.4.clone.1 | convolution fusion | flops 2717908992 | bytes 4718592 | tf_op jit(solution)/shard_map/while/body/eval_jaxpr/bik,bjk->bij/dot_general | solution.py:17
  178.7 3.0 %fusion.54 = f32[768,768]{1,0:T(8,128)S(1)} fusion(f32[768,768]{1,0:T(8,128)S(1)} %fusion.53, f32[1,768,768]{2,1,0:T(8,128)S(1)} %get-tuple-element.107), kind=kOutput, calls=%fused_computation.2.clone.1 | convolution fusion | flops 2717908992 | bytes 7077888 | tf_op jit(solution)/shard_map/while/body/eval_jaxpr/bik,bkj->bij/dot_general | solution.py:21
  181.7 4.0 %bitcast_add_fusion.4 = f32[1,768,768]{2,1,0:T(8,128)S(1)} fusion(f32[768,768]{1,0:T(8,128)S(1)} %fusion.54, f32[1,768,768]{2,1,0:T(8,128)S(1)} %get-tuple-element.107, f32[768,768]{1,0:T(8,128)S(1)} %fusion.53), kind=kOutput, calls=%fused_computation.clone.1 | convolution fusion | flops 2720858112 | bytes 9437184 | tf_op jit(solution)/shard_map/while/body/eval_jaxpr/bik,bkj->bij/dot_general | solution.py:22
  185.8 3.0 %fusion.53 = f32[768,768]{1,0:T(8,128)S(1)} fusion(f32[1,768,768]{2,1,0:T(8,128)S(1)} %get-tuple-element.107), kind=kOutput, calls=%fused_computation.4.clone.1 | convolution fusion | flops 2717908992 | bytes 4718592 | tf_op jit(solution)/shard_map/while/body/eval_jaxpr/bik,bjk->bij/dot_general | solution.py:17
  188.8 3.0 %fusion.54 = f32[768,768]{1,0:T(8,128)S(1)} fusion(f32[768,768]{1,0:T(8,128)S(1)} %fusion.53, f32[1,768,768]{2,1,0:T(8,128)S(1)} %get-tuple-element.107), kind=kOutput, calls=%fused_computation.2.clone.1 | convolution fusion | flops 2717908992 | bytes 7077888 | tf_op jit(solution)/shard_map/while/body/eval_jaxpr/bik,bkj->bij/dot_general | solution.py:21
  191.8 4.0 %bitcast_add_fusion.4 = f32[1,768,768]{2,1,0:T(8,128)S(1)} fusion(f32[768,768]{1,0:T(8,128)S(1)} %fusion.54, f32[1,768,768]{2,1,0:T(8,128)S(1)} %get-tuple-element.107, f32[768,768]{1,0:T(8,128)S(1)} %fusion.53), kind=kOutput, calls=%fused_computation.clone.1 | convolution fusion | flops 2720858112 | bytes 9437184 | tf_op jit(solution)/shard_map/while/body/eval_jaxpr/bik,bkj->bij/dot_general | solution.py:22
  195.9 3.0 %fusion.53 = f32[768,768]{1,0:T(8,128)S(1)} fusion(f32[1,768,768]{2,1,0:T(8,128)S(1)} %get-tuple-element.107), kind=kOutput, calls=%fused_computation.4.clone.1 | convolution fusion | flops 2717908992 | bytes 4718592 | tf_op jit(solution)/shard_map/while/body/eval_jaxpr/bik,bjk->bij/dot_general | solution.py:17
  198.9 3.0 %fusion.54 = f32[768,768]{1,0:T(8,128)S(1)} fusion(f32[768,768]{1,0:T(8,128)S(1)} %fusion.53, f32[1,768,768]{2,1,0:T(8,128)S(1)} %get-tuple-element.107), kind=kOutput, calls=%fused_computation.2.clone.1 | convolution fusion | flops 2717908992 | bytes 7077888 | tf_op jit(solution)/shard_map/while/body/eval_jaxpr/bik,bkj->bij/dot_general | solution.py:21
  202.0 4.0 %bitcast_add_fusion.4 = f32[1,768,768]{2,1,0:T(8,128)S(1)} fusion(f32[768,768]{1,0:T(8,128)S(1)} %fusion.54, f32[1,768,768]{2,1,0:T(8,128)S(1)} %get-tuple-element.107, f32[768,768]{1,0:T(8,128)S(1)} %fusion.53), kind=kOutput, calls=%fused_computation.clone.1 | convolution fusion | flops 2720858112 | bytes 9437184 | tf_op jit(solution)/shard_map/while/body/eval_jaxpr/bik,bkj->bij/dot_general | solution.py:22
  206.1 0.8 slice_bitcast_fusion
  206.9 1.8 copy.38
  208.6 1.2 copy.37
  209.8 1.6 dynamic-slice_bitcast_fusion
  211.4 4.2 %select_bitcast_fusion = (f32[768,768]{1,0:T(8,128)}, f32[1,768,768]{2,1,0:T(8,128)}) fusion(f32[1,768,768]{2,1,0:T(8,128)} %collective-permute-done, f32[1,768,768]{2,1,0:T(8,128)S(1)} %get-tuple-element.31, pred[]{:T(512)S(6)} %eq.6), kind=kLoop, calls=%fused_computation.15 | loop fusion | flops 1179648 | bytes 9437185 | tf_op jit(solution)/shard_map/squeeze | solution.py:113
  (36 shorter events, 2.6 us)
Async XLA Ops:
  10.8 21.5 %copy-start.10 = (f32[192,64]{0,1:T(8,128)S(1)}, f32[192,64]{0,1:T(8,128)}, u32[]{:S(2)}) copy-start(f32[192,64]{0,1:T(8,128)} %param.22) | copy-start | bytes 147460
  10.8 21.3 %all-to-all-start = ((bf16[8,960,64]{1,2,0:T(8,128)(2,1)}), bf16[8,960,64]{1,2,0:T(8,128)(2,1)S(1)}, u32[]{:S(2)}, u32[]{:S(2)}) async-start(bf16[8,960,64]{1,2,0:T(8,128)(2,1)} %maximum_bitcast_fusion), calls=%async_computation | async-start | bytes 2097152 | tf_op jit(solution)/shard_map/all_to_all | solution.py:48
  17.3 148.4 %all-reduce.2.cloned.1.call-start = ((), (), s32[]{:S(2)}) async-start(), calls=%async_computation.1 | async-start | bytes 9437184 | tf_op jit(solution)/shard_map/psum | solution.py:90
  32.3 20.5 %copy-start.3 = (f32[192,64]{0,1:T(8,128)}, f32[192,64]{0,1:T(8,128)S(1)}, u32[]{:S(2)}) copy-start(f32[192,64]{0,1:T(8,128)S(1)} %get-tuple-element.86) | copy-start | bytes 147460
  45.4 5.7 %copy-start.7 = (f32[24,768]{1,0:T(8,128)S(1)}, f32[24,768]{1,0:T(8,128)}, u32[]{:S(2)}) copy-start(f32[24,768]{1,0:T(8,128)} %param.24) | copy-start | bytes 221188
  45.5 5.7 %copy-start.8 = (f32[1,24,768]{2,1,0:T(8,128)S(1)}, f32[1,24,768]{2,1,0:T(8,128)}, u32[]{:S(2)}) copy-start(f32[1,24,768]{2,1,0:T(8,128)} %param.19) | copy-start | bytes 221188
  52.7 13.8 %copy-start = (f32[768,768]{1,0:T(8,128)S(1)}, f32[768,768]{1,0:T(8,128)}, u32[]{:S(2)}) copy-start(f32[768,768]{1,0:T(8,128)} %param.25) | copy-start | bytes 7077892
  66.5 4.6 %copy-start.2 = (f32[1,768,64]{1,2,0:T(8,128)}, f32[1,768,64]{1,2,0:T(8,128)S(1)}, u32[]{:S(2)}) copy-start(f32[1,768,64]{1,2,0:T(8,128)S(1)} %bitcast_add_fusion.2) | copy-start | bytes 589828
  66.5 4.6 %copy-start.4 = (f32[768,64]{0,1:T(8,128)S(1)}, f32[768,64]{0,1:T(8,128)}, u32[]{:S(2)}) copy-start(f32[768,64]{0,1:T(8,128)} %param.23) | copy-start | bytes 589828
  66.5 4.6 %copy-start.5 = (f32[1,768,64]{1,2,0:T(8,128)S(1)}, f32[1,768,64]{1,2,0:T(8,128)}, u32[]{:S(2)}) copy-start(f32[1,768,64]{1,2,0:T(8,128)} %param.18) | copy-start | bytes 589828
  66.5 4.7 %copy-start.1 = (f32[1,768,768]{2,1,0:T(8,128)S(1)}, f32[1,768,768]{2,1,0:T(8,128)}, u32[]{:S(2)}) copy-start(f32[1,768,768]{2,1,0:T(8,128)} %param.20) | copy-start | bytes 7077892
  71.2 4.8 %copy-start.6 = (f32[1,768,64]{1,2,0:T(8,128)S(1)}, f32[1,768,64]{1,2,0:T(8,128)}, u32[]{:S(2)}) copy-start(f32[1,768,64]{1,2,0:T(8,128)} %param.16) | copy-start | bytes 589828
  71.3 5.5 %copy-start.9 = (f32[192,64]{0,1:T(8,128)S(1)}, f32[192,64]{0,1:T(8,128)}, u32[]{:S(2)}) copy-start(f32[192,64]{0,1:T(8,128)} %param.21) | copy-start | bytes 147460
  206.0 5.4 %collective-permute-start = (f32[1,768,768]{2,1,0:T(8,128)S(1)}, f32[1,768,768]{2,1,0:T(8,128)}, u32[]{:S(2)}, u32[]{:S(2)}) collective-permute-start(f32[1,768,768]{2,1,0:T(8,128)S(1)} %get-tuple-element.31), channel_id=1, source_target_pairs={{0,1},{1,0},{2,3},{3,2},{4,5},{5,4},{6,7},{7,6},{8,9},{9,8},{10,11... | collective-permute-start | bytes 7077896 | tf_op jit(solution)/shard_map/ppermute | solution.py:109
Sparse Core Ops, SparseCore 0:
  52.9 112.6 all-reduce.1

commit v11 on v10

--- a/solution.py
+++ b/solution.py
@@ -21,6 +21,19 @@
     first_prod = jnp.einsum("bik,bkj->bij", gram_matrix, current, precision=HIGH)
     second_prod = jnp.einsum("bik,bkj->bij", gram_matrix, first_prod, precision=HIGH)
     return linear_coef * current + cubic_coef * first_prod + quintic_coef * second_prod
+
+
+def gather_rows(block, axis):
+    size = lax.axis_size(axis)
+    here = lax.axis_index(axis)
+    rows = block.shape[0]
+    full = jnp.zeros((size * rows,) + block.shape[1:], block.dtype)
+    full = lax.dynamic_update_slice_in_dim(full, block, here * rows, 0)
+    for shift in range(1, size):
+        moved = lax.ppermute(block, axis, perm=[(i, (i + shift) % size) for i in range(size)])
+        source = (here - shift) % size
+        full = lax.dynamic_update_slice_in_dim(full, moved, source * rows, 0)
+    return full
 
 
 def shards(
@@ -53,10 +66,8 @@
     dense_mean = dense_sum / replicas
     expert_first_out = 0.9 * expert_first + 0.1 * expert_mean
     dense_first_out = 0.9 * dense_first + 0.1 * dense_mean
-    dense_grad_full, dense_first_full = (
-        lax.all_gather(dense_mean, "wshard", axis=0, tiled=True),
-        lax.all_gather(dense_first_out, "wshard", axis=0, tiled=True),
-    )
+    dense_grad_full = gather_rows(dense_mean, "wshard")
+    dense_first_full = lax.all_gather(dense_first_out, "wshard", axis=0, tiled=True)
     grads_all = jnp.concatenate([expert_mean, dense_grad_full[None]], 0)
     firsts_all = jnp.concatenate([expert_first_out, dense_first_full[None]], 0)
     bases_all = jnp.concatenate([expert_basis, dense_basis[None]], 0)
@@ -80,7 +91,13 @@
         lax.all_gather(expert_master_out.astype(jnp.bfloat16), "dp", axis=2, tiled=True),
         lax.all_gather(dense_master_out.astype(jnp.bfloat16), "dp", axis=1, tiled=True),
     )
-    partial_stat = jnp.einsum("bic,bjc->bij", grads_all, grads_all, precision=HIGHEST)
+    partial_stat = jnp.concatenate(
+        [
+            jnp.einsum("bic,bjc->bij", expert_mean, expert_mean, precision=HIGHEST),
+            jnp.einsum("ic,jc->ij", dense_grad_full, dense_grad_full, precision=HIGHEST)[None],
+        ],
+        0,
+    )
     stats_all = jnp.concatenate([expert_stat, dense_stat[None]], 0)
     stat_rows = stats_all.shape[1]
     row_start = lax.axis_index(("tensor", "dp")) * stat_rows

time: 224 us -> 220 us (0.982)
  blocking collectives: 85.6 us -> 73.2 us
  starting transfers between devices: 6.61 us -> 11.2 us
    all_gather x1 -> x0, blocking collectives: 12.8 us -> none  [shards(): lax.all_gather(dense_mean, 'wshard', axis=0, tiled=True)]
    ppermute x0 -> x3, starting transfers between devices: none -> 4.68 us  [gather_rows(): lax.ppermute(block, axis, perm=[(i, (i + shift) % size) for i in range(si...]
    mul x0 -> x1, other arithmetic: none -> 2.6 us  [shards(): stats_full = lax.psum(placed + 0.05 * partial_stat, ('tensor', 'dp'))]
    dynamic_update_slice x0 -> x4, local copies, waits for them, and re-layouts: none -> 2.57 us  [the longest x3 1.91 us: gather_rows(): full = lax.dynamic_update_slice_in_dim(full, moved, source * rows, 0)]
    dot_general x1 -> x2, matrix products: 5.65 us -> 4.1 us  [the longest x1 2.05 us: shards(): jnp.einsum('bic,bjc->bij', expert_mean, expert_mean, precision=HIGHEST)]
    unnamed x26 -> x28, local copies, waits for them, and re-layouts: 5.44 us -> 5.45 us
  transfers between devices with their start and end apart: 3 -> 6, of which waited for: 2 -> 3; matrix products, arithmetic and copies ran while one was open for 8% -> 9% of each run, Pallas kernels for 0% -> 0%
where the time goes in v11:
time: 220 us; the launch traced here: 218 us
  blocking collectives  73.2 us (33%)
  matrix products  51.2 us (23%)
  waiting for transfers between devices  43.6 us (20%)
  between operations  15.1 us (7%)
  other arithmetic  13 us (6%)
  starting transfers between devices  11.2 us (5%)
  local copies, waits for them, and re-layouts  10.7 us (5%)
    all_gather x1, blocking collectives, shards(): lax.all_gather(dense_master_out.astype(jnp.bfloat16), 'dp', axis=1, tiled...  30.6 us
    all_gather x1, blocking collectives, shards(): lax.all_gather(expert_master_out.astype(jnp.bfloat16), 'dp', axis=2, tile...  30 us
    psum x1, waiting for transfers between devices, shards(): stats_full = lax.psum(placed + 0.05 * partial_stat, ('tensor', 'dp'))  26.8 us
    all_to_all x1, waiting for transfers between devices, shards(): received = lax.all_to_all(joined, 'dp', 0, 0, tiled=True)  14.7 us
    all_gather x1, blocking collectives, shards(): lax.all_gather(dense_first_out, 'wshard', axis=0, tiled=True)  12.6 us
    dot_general x3, matrix products, quintic_step(): jnp.einsum('bik,bkj->bij', gram_matrix, first_prod, precision=HIGH)  12.1 us
    dot_general x3, matrix products, quintic_step(): jnp.einsum('bik,bkj->bij', gram_matrix, current, precision=HIGH)  9.11 us
    dot_general x3, matrix products, local_gram(): return jnp.einsum('bik,bjk->bij', current, current, precision=HIGH)  9.09 us
  transfers between devices with their start and end apart: 6, of which 3 were waited for; matrix products, arithmetic and copies ran while one was open for 9% of the time, Pallas kernels for 0%

profile of v11, /device:TPU:0, one launch (start us, length us, event | category | flops | bytes accessed | tf_op | source)
XLA Modules:
  0.0 218.3 jit_solution(8690092316559669434)
XLA Ops:
  8.2 1.4 copy.32
  9.7 1.1 maximum_bitcast_fusion
  10.8 6.4 %all-to-all-start = ((bf16[8,960,64]{1,2,0:T(8,128)(2,1)}), bf16[8,960,64]{1,2,0:T(8,128)(2,1)S(1)}, u32[]{:S(2)}, u32[]{:S(2)}) async-start(bf16[8,960,64]{1,2,0:T(8,128)(2,1)} %maximum_bitcast_fusion), calls=%async_computation | async-start | bytes 2097152 | tf_op jit(solution)/shard_map/all_to_all | solution.py:61
  17.3 14.7 %all-to-all-done = bf16[8,960,64]{1,2,0:T(8,128)(2,1)S(1)} async-done(((bf16[8,960,64]{1,2,0:T(8,128)(2,1)}), bf16[8,960,64]{1,2,0:T(8,128)(2,1)S(1)}, u32[]{:S(2)}, u32[]{:S(2)}) %all-to-all-start) | async-done | bytes 983072 | tf_op jit(solution)/shard_map/all_to_all | solution.py:61
  32.2 3.1 %collective-permute-start.2 = (f32[192,64]{0,1:T(8,128)S(1)}, f32[192,64]{0,1:T(8,128)S(1)}, u32[]{:S(2)}, u32[]{:S(2)}) collective-permute-start(f32[192,64]{0,1:T(8,128)S(1)} %get-tuple-element.87), channel_id=1, source_target_pairs={{0,12},{4,0},{8,4},{12,8},{1,13},{5,1},{9,5},{13,9},{2,14},{6,2},{... | collective-permute-start | bytes 147464 | tf_op jit(solution)/shard_map/ppermute | solution.py:33
  36.9 2.1 convolution_bitcast_fusion.1
  39.6 2.1 collective-permute-done
  43.7 2.0 convolution_bitcast_fusion
  45.8 2.6 %maximum_multiply_fusion = f32[2,768,768]{2,1,0:T(8,128)} fusion(f32[1,768,768]{2,1,0:T(8,128)S(1)} %convolution_bitcast_fusion, f32[1,768,768]{2,1,0:T(8,128)S(1)} %convolution_bitcast_fusion.1), kind=kLoop, calls=%fused_computation.9 | loop fusion | flops 2359296 | bytes 9437184 | tf_op jit(solution)/shard_map/mul | solution.py:107
  48.4 1.6 fusion.26
  50.0 12.6 %all-gather = f32[4,192,64]{1,2,0:T(8,128)S(1)} all-gather(f32[1,192,64]{1,2,0:T(8,128)S(1)} %bitcast.76), channel_id=1, replica_groups=mesh['dp'=8,'wshard'=4,'tensor'=4] {'wshard'}, dimensions={0}, use_global_device_ids=true | all-gather | bytes 245760 | tf_op jit(solution)/shard_map/all_gather | solution.py:70
  63.1 4.6 %fusion.5 = f32[2,768,128]{1,2,0:T(8,128)S(1)} fusion(f32[1,768,768]{2,1,0:T(8,128)S(1)} %bitcast.70, f32[1,768,768]{2,1,0:T(8,128)} %param.20, f32[1,768,64]{1,2,0:T(8,128)S(1)} %broadcast_in_dim.29, f32[1,768,64]{1,2,0:T(8,128)S(1)} %bitcast_add_fusion.2, f32[1,768,64]{1,2,0:T(8,128)S(1)} %bitcast.73, f32[1,768,64]{1,2,0:T(8,128)S(1)} %fusion.24), kind=kOutput, calls=%fused_computation.11 | convolution fusion | flops 1813708800 | bytes 6291456 | tf_op jit(solution)/shard_map/bki,bkc->bic/dot_general | solution.py:76
  67.8 4.8 %fusion.4 = f32[2,768,64]{1,2,0:T(8,128)S(1)} fusion(f32[1,768,768]{2,1,0:T(8,128)S(1)} %bitcast.71, f32[1,768,768]{2,1,0:T(8,128)S(1)} %copy-done.1, f32[2,768,128]{1,2,0:T(8,128)S(1)} %fusion.5, f32[2,768,64]{1,2,0:T(8,128)S(1)} %fusion.19), kind=kOutput, calls=%fused_computation.10 | convolution fusion | flops 907345920 | bytes 5898240 | tf_op jit(solution)/shard_map/bik,bkc->bic/dot_general | solution.py:83
  74.0 30.6 %all_gather.11 = bf16[192,512]{0,1:T(8,128)(2,1)} all-gather(bf16[192,64]{0,1:T(8,128)(2,1)S(1)} %get-tuple-element.75), channel_id=1, replica_groups=mesh['dp'=8,'wshard'=4,'tensor'=4] {'dp'}, dimensions={1}, use_global_device_ids=true | all-gather | bytes 221184 | tf_op jit(solution)/shard_map/all_gather | solution.py:92
  104.6 30.0 %all_gather.10 = bf16[1,768,512]{1,2,0:T(8,128)(2,1)S(1)} all-gather(bf16[1,768,64]{1,2,0:T(8,128)(2,1)S(1)} %get-tuple-element.77), channel_id=1, replica_groups=mesh['dp'=8,'wshard'=4,'tensor'=4] {'dp'}, dimensions={2}, use_global_device_ids=true | all-gather | bytes 884736 | tf_op jit(solution)/shard_map/all_gather | solution.py:91
  134.6 26.8 %all-reduce.2.cloned.1.call-done = f32[2,768,768]{2,1,0:T(8,128)} async-done(((f32[2,768,768]{2,1,0:T(8,128)}), f32[2,768,768]{2,1,0:T(8,128)}) %all-reduce.2.cloned.1.call-update) | async-done | bytes 4718608 | tf_op jit(solution)/shard_map/psum | solution.py:107
  161.4 7.5 %multiply_reduce_fusion = (f32[]{:T(128)}, f32[768,768]{1,0:T(8,128)}) fusion(s32[]{:T(128)S(6)} %select_n.62, f32[1,768,768]{2,1,0:T(8,128)} %param.20, f32[1,768,768]{2,1,0:T(8,128)S(1)} %bitcast.72, f32[2,768,768]{2,1,0:T(8,128)} %all-reduce.2.cloned.1.call-done), kind=kOutput, calls=%fused_computation.18 | convolution fusion | flops 2719678464 | bytes 9438212 | tf_op jit(solution)/shard_map/bik,bkj->bij/dot_general | solution.py:118
  169.6 1.8 multiply_bitcast_fusion
  171.4 30.6 %while.10 = (s32[]{:T(128)}, f32[1,768,768]{2,1,0:T(8,128)S(1)}, s32[]{:T(128)}) while((s32[]{:T(128)}, f32[1,768,768]{2,1,0:T(8,128)S(1)}, s32[]{:T(128)}) %tuple.35), condition=%wide.region_4.5_spmd, body=%wide.region_3.4_spmd.sunk | while | flops 8156676096 | bytes 21233708 | solution.py:125
  171.6 3.0 %fusion.54 = f32[768,768]{1,0:T(8,128)S(1)} fusion(f32[1,768,768]{2,1,0:T(8,128)S(1)} %get-tuple-element.107), kind=kOutput, calls=%fused_computation.4.clone.1 | convolution fusion | flops 2717908992 | bytes 4718592 | tf_op jit(solution)/shard_map/while/body/eval_jaxpr/bik,bjk->bij/dot_general | solution.py:17
  174.7 3.0 %fusion.55 = f32[768,768]{1,0:T(8,128)S(1)} fusion(f32[768,768]{1,0:T(8,128)S(1)} %fusion.54, f32[1,768,768]{2,1,0:T(8,128)S(1)} %get-tuple-element.107), kind=kOutput, calls=%fused_computation.2.clone.1 | convolution fusion | flops 2717908992 | bytes 7077888 | tf_op jit(solution)/shard_map/while/body/eval_jaxpr/bik,bkj->bij/dot_general | solution.py:21
  177.7 4.0 %bitcast_add_fusion.4 = f32[1,768,768]{2,1,0:T(8,128)S(1)} fusion(f32[768,768]{1,0:T(8,128)S(1)} %fusion.55, f32[1,768,768]{2,1,0:T(8,128)S(1)} %get-tuple-element.107, f32[768,768]{1,0:T(8,128)S(1)} %fusion.54), kind=kOutput, calls=%fused_computation.clone.1 | convolution fusion | flops 2720858112 | bytes 9437184 | tf_op jit(solution)/shard_map/while/body/eval_jaxpr/bik,bkj->bij/dot_general | solution.py:22
  181.7 3.0 %fusion.54 = f32[768,768]{1,0:T(8,128)S(1)} fusion(f32[1,768,768]{2,1,0:T(8,128)S(1)} %get-tuple-element.107), kind=kOutput, calls=%fused_computation.4.clone.1 | convolution fusion | flops 2717908992 | bytes 4718592 | tf_op jit(solution)/shard_map/while/body/eval_jaxpr/bik,bjk->bij/dot_general | solution.py:17
  184.8 3.0 %fusion.55 = f32[768,768]{1,0:T(8,128)S(1)} fusion(f32[768,768]{1,0:T(8,128)S(1)} %fusion.54, f32[1,768,768]{2,1,0:T(8,128)S(1)} %get-tuple-element.107), kind=kOutput, calls=%fused_computation.2.clone.1 | convolution fusion | flops 2717908992 | bytes 7077888 | tf_op jit(solution)/shard_map/while/body/eval_jaxpr/bik,bkj->bij/dot_general | solution.py:21
  187.8 4.0 %bitcast_add_fusion.4 = f32[1,768,768]{2,1,0:T(8,128)S(1)} fusion(f32[768,768]{1,0:T(8,128)S(1)} %fusion.55, f32[1,768,768]{2,1,0:T(8,128)S(1)} %get-tuple-element.107, f32[768,768]{1,0:T(8,128)S(1)} %fusion.54), kind=kOutput, calls=%fused_computation.clone.1 | convolution fusion | flops 2720858112 | bytes 9437184 | tf_op jit(solution)/shard_map/while/body/eval_jaxpr/bik,bkj->bij/dot_general | solution.py:22
  191.9 3.0 %fusion.54 = f32[768,768]{1,0:T(8,128)S(1)} fusion(f32[1,768,768]{2,1,0:T(8,128)S(1)} %get-tuple-element.107), kind=kOutput, calls=%fused_computation.4.clone.1 | convolution fusion | flops 2717908992 | bytes 4718592 | tf_op jit(solution)/shard_map/while/body/eval_jaxpr/bik,bjk->bij/dot_general | solution.py:17
  194.9 3.0 %fusion.55 = f32[768,768]{1,0:T(8,128)S(1)} fusion(f32[768,768]{1,0:T(8,128)S(1)} %fusion.54, f32[1,768,768]{2,1,0:T(8,128)S(1)} %get-tuple-element.107), kind=kOutput, calls=%fused_computation.2.clone.1 | convolution fusion | flops 2717908992 | bytes 7077888 | tf_op jit(solution)/shard_map/while/body/eval_jaxpr/bik,bkj->bij/dot_general | solution.py:21
  197.9 4.0 %bitcast_add_fusion.4 = f32[1,768,768]{2,1,0:T(8,128)S(1)} fusion(f32[768,768]{1,0:T(8,128)S(1)} %fusion.55, f32[1,768,768]{2,1,0:T(8,128)S(1)} %get-tuple-element.107, f32[768,768]{1,0:T(8,128)S(1)} %fusion.54), kind=kOutput, calls=%fused_computation.clone.1 | convolution fusion | flops 2720858112 | bytes 9437184 | tf_op jit(solution)/shard_map/while/body/eval_jaxpr/bik,bkj->bij/dot_general | solution.py:22
  202.9 1.8 copy.36
  204.6 1.2 copy.35
  205.8 1.6 dynamic-slice_bitcast_fusion
  207.4 4.2 %select_bitcast_fusion = (f32[768,768]{1,0:T(8,128)}, f32[1,768,768]{2,1,0:T(8,128)}) fusion(f32[1,768,768]{2,1,0:T(8,128)} %collective-permute-done.3, f32[1,768,768]{2,1,0:T(8,128)S(1)} %get-tuple-element.31, pred[]{:T(512)S(6)} %eq.9), kind=kLoop, calls=%fused_computation.16 | loop fusion | flops 1179648 | bytes 9437185 | tf_op jit(solution)/shard_map/squeeze | solution.py:130
  (48 shorter events, 8.3 us)
Async XLA Ops:
  9.7 22.5 %copy-start.11 = (f32[192,64]{0,1:T(8,128)S(1)}, f32[192,64]{0,1:T(8,128)}, u32[]{:S(2)}) copy-start(f32[192,64]{0,1:T(8,128)} %param.22) | copy-start | bytes 147460
  10.8 21.2 %all-to-all-start = ((bf16[8,960,64]{1,2,0:T(8,128)(2,1)}), bf16[8,960,64]{1,2,0:T(8,128)(2,1)S(1)}, u32[]{:S(2)}, u32[]{:S(2)}) async-start(bf16[8,960,64]{1,2,0:T(8,128)(2,1)} %maximum_bitcast_fusion), calls=%async_computation | async-start | bytes 2097152 | tf_op jit(solution)/shard_map/all_to_all | solution.py:61
  17.1 144.2 %all-reduce.2.cloned.1.call-start = ((), (), s32[]{:S(2)}) async-start(), calls=%async_computation.1 | async-start | bytes 9437184 | tf_op jit(solution)/shard_map/psum | solution.py:107
  32.2 17.9 %copy-start.3 = (f32[192,64]{0,1:T(8,128)}, f32[192,64]{0,1:T(8,128)S(1)}, u32[]{:S(2)}) copy-start(f32[192,64]{0,1:T(8,128)S(1)} %get-tuple-element.86) | copy-start | bytes 147460
  32.2 10.7 %collective-permute-start.2 = (f32[192,64]{0,1:T(8,128)S(1)}, f32[192,64]{0,1:T(8,128)S(1)}, u32[]{:S(2)}, u32[]{:S(2)}) collective-permute-start(f32[192,64]{0,1:T(8,128)S(1)} %get-tuple-element.87), channel_id=1, source_target_pairs={{0,12},{4,0},{8,4},{12,8},{1,13},{5,1},{9,5},{13,9},{2,14},{6,2},{... | collective-permute-start | bytes 147464 | tf_op jit(solution)/shard_map/ppermute | solution.py:33
  35.2 7.0 %collective-permute-start.1 = (f32[192,64]{0,1:T(8,128)S(1)}, f32[192,64]{0,1:T(8,128)S(1)}, u32[]{:S(2)}, u32[]{:S(2)}) collective-permute-start(f32[192,64]{0,1:T(8,128)S(1)} %get-tuple-element.87), channel_id=1, source_target_pairs={{0,8},{4,12},{8,0},{12,4},{1,9},{5,13},{9,1},{13,5},{2,10},{6,14},... | collective-permute-start | bytes 147464 | tf_op jit(solution)/shard_map/ppermute | solution.py:33
  35.9 5.8 %collective-permute-start = (f32[192,64]{0,1:T(8,128)S(1)}, f32[192,64]{0,1:T(8,128)S(1)}, u32[]{:S(2)}, u32[]{:S(2)}) collective-permute-start(f32[192,64]{0,1:T(8,128)S(1)} %get-tuple-element.87), channel_id=1, source_target_pairs={{0,4},{4,8},{8,12},{12,0},{1,5},{5,9},{9,13},{13,1},{2,6},{6,10},{... | collective-permute-start | bytes 147464 | tf_op jit(solution)/shard_map/ppermute | solution.py:33
  45.7 2.6 %copy-start.8 = (f32[24,768]{1,0:T(8,128)S(1)}, f32[24,768]{1,0:T(8,128)}, u32[]{:S(2)}) copy-start(f32[24,768]{1,0:T(8,128)} %param.24) | copy-start | bytes 221188
  45.7 2.6 %copy-start.9 = (f32[1,24,768]{2,1,0:T(8,128)S(1)}, f32[1,24,768]{2,1,0:T(8,128)}, u32[]{:S(2)}) copy-start(f32[1,24,768]{2,1,0:T(8,128)} %param.19) | copy-start | bytes 221188
  50.0 13.0 %copy-start.6 = (f32[1,768,64]{1,2,0:T(8,128)S(1)}, f32[1,768,64]{1,2,0:T(8,128)}, u32[]{:S(2)}) copy-start(f32[1,768,64]{1,2,0:T(8,128)} %param.17) | copy-start | bytes 589828
  50.0 13.1 %copy-start = (f32[768,768]{1,0:T(8,128)S(1)}, f32[768,768]{1,0:T(8,128)}, u32[]{:S(2)}) copy-start(f32[768,768]{1,0:T(8,128)} %param.25) | copy-start | bytes 7077892
  63.0 4.6 %copy-start.2 = (f32[1,768,64]{1,2,0:T(8,128)}, f32[1,768,64]{1,2,0:T(8,128)S(1)}, u32[]{:S(2)}) copy-start(f32[1,768,64]{1,2,0:T(8,128)S(1)} %bitcast_add_fusion.2) | copy-start | bytes 589828
  63.0 4.6 %copy-start.4 = (f32[768,64]{0,1:T(8,128)S(1)}, f32[768,64]{0,1:T(8,128)}, u32[]{:S(2)}) copy-start(f32[768,64]{0,1:T(8,128)} %param.23) | copy-start | bytes 589828
  63.1 4.6 %copy-start.5 = (f32[1,768,64]{1,2,0:T(8,128)S(1)}, f32[1,768,64]{1,2,0:T(8,128)}, u32[]{:S(2)}) copy-start(f32[1,768,64]{1,2,0:T(8,128)} %param.18) | copy-start | bytes 589828
  63.1 4.7 %copy-start.1 = (f32[1,768,768]{2,1,0:T(8,128)S(1)}, f32[1,768,768]{2,1,0:T(8,128)}, u32[]{:S(2)}) copy-start(f32[1,768,768]{2,1,0:T(8,128)} %param.20) | copy-start | bytes 7077892
  67.8 4.8 %copy-start.7 = (f32[1,768,64]{1,2,0:T(8,128)S(1)}, f32[1,768,64]{1,2,0:T(8,128)}, u32[]{:S(2)}) copy-start(f32[1,768,64]{1,2,0:T(8,128)} %param.16) | copy-start | bytes 589828
  67.8 5.5 %copy-start.10 = (f32[192,64]{0,1:T(8,128)S(1)}, f32[192,64]{0,1:T(8,128)}, u32[]{:S(2)}) copy-start(f32[192,64]{0,1:T(8,128)} %param.21) | copy-start | bytes 147460
  202.0 5.4 %collective-permute-start.3 = (f32[1,768,768]{2,1,0:T(8,128)S(1)}, f32[1,768,768]{2,1,0:T(8,128)}, u32[]{:S(2)}, u32[]{:S(2)}) collective-permute-start(f32[1,768,768]{2,1,0:T(8,128)S(1)} %get-tuple-element.31), channel_id=1, source_target_pairs={{0,1},{1,0},{2,3},{3,2},{4,5},{5,4},{6,7},{7,6},{8,9},{9,8},{10,11... | collective-permute-start | bytes 7077896 | tf_op jit(solution)/shard_map/ppermute | solution.py:126
Sparse Core Ops, SparseCore 0:
  50.1 111.2 all-reduce.1

commit v12 on v11

--- a/solution.py
+++ b/solution.py
@@ -115,7 +115,9 @@
     core = lax.axis_index("tensor") % 2
     stat_mine = lax.dynamic_slice_in_dim(stats_full, core, 1, 0)
     basis_mine = lax.dynamic_slice_in_dim(bases_all, core, 1, 0)
-    power = jnp.einsum("bik,bkj->bij", stat_mine, basis_mine, precision=HIGH)
+    power = lax.optimization_barrier(
+        jnp.einsum("bik,bkj->bij", stat_mine, basis_mine, precision=HIGH)
+    )
     square_sum = jnp.sum(power * power, (1, 2))
     current = power * lax.rsqrt(square_sum + 1e-06)[:, None, None]
 

time: 220 us -> 221 us (level)
    unnamed x28 -> x30, local copies, waits for them, and re-layouts: 5.45 us -> 6.85 us
where the time goes in v12:
time: 221 us; the launch traced here: 219 us
  blocking collectives  73.2 us (33%)
  matrix products  49.2 us (22%)
  waiting for transfers between devices  43.6 us (20%)
  between operations  15.2 us (7%)
  other arithmetic  14.2 us (6%)
  local copies, waits for them, and re-layouts  12.1 us (5%)
  starting transfers between devices  11.2 us (5%)
    all_gather x1, blocking collectives, shards(): lax.all_gather(dense_master_out.astype(jnp.bfloat16), 'dp', axis=1, tiled...  30.6 us
    all_gather x1, blocking collectives, shards(): lax.all_gather(expert_master_out.astype(jnp.bfloat16), 'dp', axis=2, tile...  30 us
    psum x1, waiting for transfers between devices, shards(): stats_full = lax.psum(placed + 0.05 * partial_stat, ('tensor', 'dp'))  26.8 us
    all_to_all x1, waiting for transfers between devices, shards(): received = lax.all_to_all(joined, 'dp', 0, 0, tiled=True)  14.7 us
    all_gather x1, blocking collectives, shards(): lax.all_gather(dense_first_out, 'wshard', axis=0, tiled=True)  12.6 us
    dot_general x3, matrix products, quintic_step(): jnp.einsum('bik,bkj->bij', gram_matrix, first_prod, precision=HIGH)  12.1 us
    dot_general x3, matrix products, quintic_step(): jnp.einsum('bik,bkj->bij', gram_matrix, current, precision=HIGH)  9.11 us
    dot_general x3, matrix products, local_gram(): return jnp.einsum('bik,bjk->bij', current, current, precision=HIGH)  9.09 us
  transfers between devices with their start and end apart: 6, of which 3 were waited for; matrix products, arithmetic and copies ran while one was open for 9% of the time, Pallas kernels for 0%

profile of v12, /device:TPU:0, one launch (start us, length us, event | category | flops | bytes accessed | tf_op | source)
XLA Modules:
  0.0 219.0 jit_solution(9039440925823726742)
XLA Ops:
  8.2 1.4 copy.32
  10.8 6.4 %all-to-all-start = ((bf16[8,960,64]{1,2,0:T(8,128)(2,1)}), bf16[8,960,64]{1,2,0:T(8,128)(2,1)S(1)}, u32[]{:S(2)}, u32[]{:S(2)}) async-start(bf16[8,960,64]{1,2,0:T(8,128)(2,1)} %maximum_bitcast_fusion), calls=%async_computation | async-start | bytes 2097152 | tf_op jit(solution)/shard_map/all_to_all | solution.py:61
  17.3 14.7 %all-to-all-done = bf16[8,960,64]{1,2,0:T(8,128)(2,1)S(1)} async-done(((bf16[8,960,64]{1,2,0:T(8,128)(2,1)}), bf16[8,960,64]{1,2,0:T(8,128)(2,1)S(1)}, u32[]{:S(2)}, u32[]{:S(2)}) %all-to-all-start) | async-done | bytes 983072 | tf_op jit(solution)/shard_map/all_to_all | solution.py:61
  32.2 3.1 %collective-permute-start.2 = (f32[192,64]{0,1:T(8,128)S(1)}, f32[192,64]{0,1:T(8,128)S(1)}, u32[]{:S(2)}, u32[]{:S(2)}) collective-permute-start(f32[192,64]{0,1:T(8,128)S(1)} %get-tuple-element.87), channel_id=1, source_target_pairs={{0,12},{4,0},{8,4},{12,8},{1,13},{5,1},{9,5},{13,9},{2,14},{6,2},{... | collective-permute-start | bytes 147464 | tf_op jit(solution)/shard_map/ppermute | solution.py:33
  36.9 2.1 convolution_bitcast_fusion.1
  39.6 2.1 collective-permute-done
  43.7 2.0 convolution_bitcast_fusion
  45.8 2.6 %maximum_multiply_fusion = f32[2,768,768]{2,1,0:T(8,128)} fusion(f32[1,768,768]{2,1,0:T(8,128)S(1)} %convolution_bitcast_fusion, f32[1,768,768]{2,1,0:T(8,128)S(1)} %convolution_bitcast_fusion.1), kind=kLoop, calls=%fused_computation.9 | loop fusion | flops 2359296 | bytes 9437184 | tf_op jit(solution)/shard_map/mul | solution.py:107
  48.4 1.6 fusion.31
  50.0 12.6 %all-gather = f32[4,192,64]{1,2,0:T(8,128)S(1)} all-gather(f32[1,192,64]{1,2,0:T(8,128)S(1)} %bitcast.76), channel_id=1, replica_groups=mesh['dp'=8,'wshard'=4,'tensor'=4] {'wshard'}, dimensions={0}, use_global_device_ids=true | all-gather | bytes 245760 | tf_op jit(solution)/shard_map/all_gather | solution.py:70
  63.1 4.6 %fusion.5 = f32[2,768,128]{1,2,0:T(8,128)S(1)} fusion(f32[1,768,768]{2,1,0:T(8,128)S(1)} %bitcast.70, f32[1,768,768]{2,1,0:T(8,128)} %param.20, f32[1,768,64]{1,2,0:T(8,128)S(1)} %broadcast_in_dim.29, f32[1,768,64]{1,2,0:T(8,128)S(1)} %bitcast_add_fusion.2, f32[1,768,64]{1,2,0:T(8,128)S(1)} %bitcast.73, f32[1,768,64]{1,2,0:T(8,128)S(1)} %fusion.29), kind=kOutput, calls=%fused_computation.11 | convolution fusion | flops 1813708800 | bytes 6291456 | tf_op jit(solution)/shard_map/bki,bkc->bic/dot_general | solution.py:76
  67.8 4.8 %fusion.4 = f32[2,768,64]{1,2,0:T(8,128)S(1)} fusion(f32[1,768,768]{2,1,0:T(8,128)S(1)} %bitcast.71, f32[1,768,768]{2,1,0:T(8,128)S(1)} %copy-done.2, f32[2,768,128]{1,2,0:T(8,128)S(1)} %fusion.5, f32[2,768,64]{1,2,0:T(8,128)S(1)} %fusion.24), kind=kOutput, calls=%fused_computation.10 | convolution fusion | flops 907345920 | bytes 5898240 | tf_op jit(solution)/shard_map/bik,bkc->bic/dot_general | solution.py:83
  74.0 30.6 %all_gather.11 = bf16[192,512]{0,1:T(8,128)(2,1)} all-gather(bf16[192,64]{0,1:T(8,128)(2,1)S(1)} %get-tuple-element.75), channel_id=1, replica_groups=mesh['dp'=8,'wshard'=4,'tensor'=4] {'dp'}, dimensions={1}, use_global_device_ids=true | all-gather | bytes 221184 | tf_op jit(solution)/shard_map/all_gather | solution.py:92
  104.6 30.0 %all_gather.10 = bf16[1,768,512]{1,2,0:T(8,128)(2,1)S(1)} all-gather(bf16[1,768,64]{1,2,0:T(8,128)(2,1)S(1)} %get-tuple-element.77), channel_id=1, replica_groups=mesh['dp'=8,'wshard'=4,'tensor'=4] {'dp'}, dimensions={2}, use_global_device_ids=true | all-gather | bytes 884736 | tf_op jit(solution)/shard_map/all_gather | solution.py:91
  134.6 26.8 %all-reduce.2.cloned.1.call-done = f32[2,768,768]{2,1,0:T(8,128)} async-done(((f32[2,768,768]{2,1,0:T(8,128)}), f32[2,768,768]{2,1,0:T(8,128)}) %all-reduce.2.cloned.1.call-update) | async-done | bytes 4718608 | tf_op jit(solution)/shard_map/psum | solution.py:107
  161.4 5.5 %fusion.12 = f32[1,768,768]{2,1,0:T(8,128)S(1)} fusion(s32[]{:T(128)S(6)} %select_n.62, f32[1,768,768]{2,1,0:T(8,128)} %param.20, f32[1,768,768]{2,1,0:T(8,128)S(1)} %bitcast.72, f32[2,768,768]{2,1,0:T(8,128)} %all-reduce.2.cloned.1.call-done), kind=kOutput, calls=%fused_computation.20 | convolution fusion | flops 2718498816 | bytes 9438208 | tf_op jit(solution)/shard_map/bik,bkj->bij/dot_general | solution.py:119
  166.9 1.4 copy-done
  168.3 1.2 multiply_reduce_fusion
  170.2 1.8 broadcast_multiply_fusion
  172.0 30.6 %while.10 = (s32[]{:T(128)}, f32[1,768,768]{2,1,0:T(8,128)S(1)}, s32[]{:T(128)}) while((s32[]{:T(128)}, f32[1,768,768]{2,1,0:T(8,128)S(1)}, s32[]{:T(128)}) %tuple.34), condition=%wide.region_4.5_spmd, body=%wide.region_3.4_spmd.sunk | while | flops 8156676096 | bytes 21233708 | solution.py:127
  172.3 3.0 %fusion.59 = f32[768,768]{1,0:T(8,128)S(1)} fusion(f32[1,768,768]{2,1,0:T(8,128)S(1)} %get-tuple-element.105), kind=kOutput, calls=%fused_computation.4.clone.1 | convolution fusion | flops 2717908992 | bytes 4718592 | tf_op jit(solution)/shard_map/while/body/eval_jaxpr/bik,bjk->bij/dot_general | solution.py:17
  175.3 3.0 %fusion.60 = f32[768,768]{1,0:T(8,128)S(1)} fusion(f32[768,768]{1,0:T(8,128)S(1)} %fusion.59, f32[1,768,768]{2,1,0:T(8,128)S(1)} %get-tuple-element.105), kind=kOutput, calls=%fused_computation.2.clone.1 | convolution fusion | flops 2717908992 | bytes 7077888 | tf_op jit(solution)/shard_map/while/body/eval_jaxpr/bik,bkj->bij/dot_general | solution.py:21
  178.3 4.0 %bitcast_add_fusion.4 = f32[1,768,768]{2,1,0:T(8,128)S(1)} fusion(f32[768,768]{1,0:T(8,128)S(1)} %fusion.60, f32[1,768,768]{2,1,0:T(8,128)S(1)} %get-tuple-element.105, f32[768,768]{1,0:T(8,128)S(1)} %fusion.59), kind=kOutput, calls=%fused_computation.clone.1 | convolution fusion | flops 2720858112 | bytes 9437184 | tf_op jit(solution)/shard_map/while/body/eval_jaxpr/bik,bkj->bij/dot_general | solution.py:22
  182.4 3.0 %fusion.59 = f32[768,768]{1,0:T(8,128)S(1)} fusion(f32[1,768,768]{2,1,0:T(8,128)S(1)} %get-tuple-element.105), kind=kOutput, calls=%fused_computation.4.clone.1 | convolution fusion | flops 2717908992 | bytes 4718592 | tf_op jit(solution)/shard_map/while/body/eval_jaxpr/bik,bjk->bij/dot_general | solution.py:17
  185.4 3.0 %fusion.60 = f32[768,768]{1,0:T(8,128)S(1)} fusion(f32[768,768]{1,0:T(8,128)S(1)} %fusion.59, f32[1,768,768]{2,1,0:T(8,128)S(1)} %get-tuple-element.105), kind=kOutput, calls=%fused_computation.2.clone.1 | convolution fusion | flops 2717908992 | bytes 7077888 | tf_op jit(solution)/shard_map/while/body/eval_jaxpr/bik,bkj->bij/dot_general | solution.py:21
  188.5 4.0 %bitcast_add_fusion.4 = f32[1,768,768]{2,1,0:T(8,128)S(1)} fusion(f32[768,768]{1,0:T(8,128)S(1)} %fusion.60, f32[1,768,768]{2,1,0:T(8,128)S(1)} %get-tuple-element.105, f32[768,768]{1,0:T(8,128)S(1)} %fusion.59), kind=kOutput, calls=%fused_computation.clone.1 | convolution fusion | flops 2720858112 | bytes 9437184 | tf_op jit(solution)/shard_map/while/body/eval_jaxpr/bik,bkj->bij/dot_general | solution.py:22
  192.5 3.0 %fusion.59 = f32[768,768]{1,0:T(8,128)S(1)} fusion(f32[1,768,768]{2,1,0:T(8,128)S(1)} %get-tuple-element.105), kind=kOutput, calls=%fused_computation.4.clone.1 | convolution fusion | flops 2717908992 | bytes 4718592 | tf_op jit(solution)/shard_map/while/body/eval_jaxpr/bik,bjk->bij/dot_general | solution.py:17
  195.6 3.0 %fusion.60 = f32[768,768]{1,0:T(8,128)S(1)} fusion(f32[768,768]{1,0:T(8,128)S(1)} %fusion.59, f32[1,768,768]{2,1,0:T(8,128)S(1)} %get-tuple-element.105), kind=kOutput, calls=%fused_computation.2.clone.1 | convolution fusion | flops 2717908992 | bytes 7077888 | tf_op jit(solution)/shard_map/while/body/eval_jaxpr/bik,bkj->bij/dot_general | solution.py:21
  198.6 4.0 %bitcast_add_fusion.4 = f32[1,768,768]{2,1,0:T(8,128)S(1)} fusion(f32[768,768]{1,0:T(8,128)S(1)} %fusion.60, f32[1,768,768]{2,1,0:T(8,128)S(1)} %get-tuple-element.105, f32[768,768]{1,0:T(8,128)S(1)} %fusion.59), kind=kOutput, calls=%fused_computation.clone.1 | convolution fusion | flops 2720858112 | bytes 9437184 | tf_op jit(solution)/shard_map/while/body/eval_jaxpr/bik,bkj->bij/dot_general | solution.py:22
  203.5 1.8 copy.36
  206.4 1.6 dynamic-slice_bitcast_fusion
  208.0 4.2 %select_bitcast_fusion = (f32[768,768]{1,0:T(8,128)}, f32[1,768,768]{2,1,0:T(8,128)}) fusion(f32[1,768,768]{2,1,0:T(8,128)} %collective-permute-done.3, f32[1,768,768]{2,1,0:T(8,128)S(1)} %get-tuple-element.31, pred[]{:T(512)S(6)} %eq.9), kind=kLoop, calls=%fused_computation.16 | loop fusion | flops 1179648 | bytes 9437185 | tf_op jit(solution)/shard_map/squeeze | solution.py:132
  (51 shorter events, 10.6 us)
Async XLA Ops:
  9.7 22.5 %copy-start.12 = (f32[192,64]{0,1:T(8,128)S(1)}, f32[192,64]{0,1:T(8,128)}, u32[]{:S(2)}) copy-start(f32[192,64]{0,1:T(8,128)} %param.22) | copy-start | bytes 147460
  10.8 21.2 %all-to-all-start = ((bf16[8,960,64]{1,2,0:T(8,128)(2,1)}), bf16[8,960,64]{1,2,0:T(8,128)(2,1)S(1)}, u32[]{:S(2)}, u32[]{:S(2)}) async-start(bf16[8,960,64]{1,2,0:T(8,128)(2,1)} %maximum_bitcast_fusion), calls=%async_computation | async-start | bytes 2097152 | tf_op jit(solution)/shard_map/all_to_all | solution.py:61
  17.1 144.2 %all-reduce.2.cloned.1.call-start = ((), (), s32[]{:S(2)}) async-start(), calls=%async_computation.1 | async-start | bytes 9437184 | tf_op jit(solution)/shard_map/psum | solution.py:107
  32.2 17.9 %copy-start.4 = (f32[192,64]{0,1:T(8,128)}, f32[192,64]{0,1:T(8,128)S(1)}, u32[]{:S(2)}) copy-start(f32[192,64]{0,1:T(8,128)S(1)} %get-tuple-element.86) | copy-start | bytes 147460
  32.2 10.7 %collective-permute-start.2 = (f32[192,64]{0,1:T(8,128)S(1)}, f32[192,64]{0,1:T(8,128)S(1)}, u32[]{:S(2)}, u32[]{:S(2)}) collective-permute-start(f32[192,64]{0,1:T(8,128)S(1)} %get-tuple-element.87), channel_id=1, source_target_pairs={{0,12},{4,0},{8,4},{12,8},{1,13},{5,1},{9,5},{13,9},{2,14},{6,2},{... | collective-permute-start | bytes 147464 | tf_op jit(solution)/shard_map/ppermute | solution.py:33
  35.2 7.0 %collective-permute-start.1 = (f32[192,64]{0,1:T(8,128)S(1)}, f32[192,64]{0,1:T(8,128)S(1)}, u32[]{:S(2)}, u32[]{:S(2)}) collective-permute-start(f32[192,64]{0,1:T(8,128)S(1)} %get-tuple-element.87), channel_id=1, source_target_pairs={{0,8},{4,12},{8,0},{12,4},{1,9},{5,13},{9,1},{13,5},{2,10},{6,14},... | collective-permute-start | bytes 147464 | tf_op jit(solution)/shard_map/ppermute | solution.py:33
  35.9 5.8 %collective-permute-start = (f32[192,64]{0,1:T(8,128)S(1)}, f32[192,64]{0,1:T(8,128)S(1)}, u32[]{:S(2)}, u32[]{:S(2)}) collective-permute-start(f32[192,64]{0,1:T(8,128)S(1)} %get-tuple-element.87), channel_id=1, source_target_pairs={{0,4},{4,8},{8,12},{12,0},{1,5},{5,9},{9,13},{13,1},{2,6},{6,10},{... | collective-permute-start | bytes 147464 | tf_op jit(solution)/shard_map/ppermute | solution.py:33
  45.7 2.6 %copy-start.9 = (f32[24,768]{1,0:T(8,128)S(1)}, f32[24,768]{1,0:T(8,128)}, u32[]{:S(2)}) copy-start(f32[24,768]{1,0:T(8,128)} %param.24) | copy-start | bytes 221188
  45.7 2.6 %copy-start.10 = (f32[1,24,768]{2,1,0:T(8,128)S(1)}, f32[1,24,768]{2,1,0:T(8,128)}, u32[]{:S(2)}) copy-start(f32[1,24,768]{2,1,0:T(8,128)} %param.19) | copy-start | bytes 221188
  50.0 13.0 %copy-start.7 = (f32[1,768,64]{1,2,0:T(8,128)S(1)}, f32[1,768,64]{1,2,0:T(8,128)}, u32[]{:S(2)}) copy-start(f32[1,768,64]{1,2,0:T(8,128)} %param.17) | copy-start | bytes 589828
  50.0 13.1 %copy-start.1 = (f32[768,768]{1,0:T(8,128)S(1)}, f32[768,768]{1,0:T(8,128)}, u32[]{:S(2)}) copy-start(f32[768,768]{1,0:T(8,128)} %param.25) | copy-start | bytes 7077892
  63.0 4.6 %copy-start.3 = (f32[1,768,64]{1,2,0:T(8,128)}, f32[1,768,64]{1,2,0:T(8,128)S(1)}, u32[]{:S(2)}) copy-start(f32[1,768,64]{1,2,0:T(8,128)S(1)} %bitcast_add_fusion.2) | copy-start | bytes 589828
  63.0 4.6 %copy-start.5 = (f32[768,64]{0,1:T(8,128)S(1)}, f32[768,64]{0,1:T(8,128)}, u32[]{:S(2)}) copy-start(f32[768,64]{0,1:T(8,128)} %param.23) | copy-start | bytes 589828
  63.1 4.6 %copy-start.6 = (f32[1,768,64]{1,2,0:T(8,128)S(1)}, f32[1,768,64]{1,2,0:T(8,128)}, u32[]{:S(2)}) copy-start(f32[1,768,64]{1,2,0:T(8,128)} %param.18) | copy-start | bytes 589828
  63.1 4.7 %copy-start.2 = (f32[1,768,768]{2,1,0:T(8,128)S(1)}, f32[1,768,768]{2,1,0:T(8,128)}, u32[]{:S(2)}) copy-start(f32[1,768,768]{2,1,0:T(8,128)} %param.20) | copy-start | bytes 7077892
  67.8 4.8 %copy-start.8 = (f32[1,768,64]{1,2,0:T(8,128)S(1)}, f32[1,768,64]{1,2,0:T(8,128)}, u32[]{:S(2)}) copy-start(f32[1,768,64]{1,2,0:T(8,128)} %param.16) | copy-start | bytes 589828
  67.8 5.5 %copy-start.11 = (f32[192,64]{0,1:T(8,128)S(1)}, f32[192,64]{0,1:T(8,128)}, u32[]{:S(2)}) copy-start(f32[192,64]{0,1:T(8,128)} %param.21) | copy-start | bytes 147460
  166.9 1.4 copy-start
  202.6 5.4 %collective-permute-start.3 = (f32[1,768,768]{2,1,0:T(8,128)S(1)}, f32[1,768,768]{2,1,0:T(8,128)}, u32[]{:S(2)}, u32[]{:S(2)}) collective-permute-start(f32[1,768,768]{2,1,0:T(8,128)S(1)} %get-tuple-element.31), channel_id=1, source_target_pairs={{0,1},{1,0},{2,3},{3,2},{4,5},{5,4},{6,7},{7,6},{8,9},{9,8},{10,11... | collective-permute-start | bytes 7077896 | tf_op jit(solution)/shard_map/ppermute | solution.py:128
Sparse Core Ops, SparseCore 0:
  50.1 111.2 all-reduce.1

commit v13 on v11

--- a/solution.py
+++ b/solution.py
@@ -58,8 +58,14 @@
     joined = jnp.concatenate([expert_local, dense_local], 0)
     owned = joined.shape[1] // replicas
     joined = joined.reshape(joined.shape[0], replicas, owned).transpose(1, 0, 2)
-    received = lax.all_to_all(joined, "dp", 0, 0, tiled=True)
-    joined_sum = jnp.sum(received.astype(jnp.float32), 0)
+    here = lax.axis_index("dp")
+    joined_sum = lax.dynamic_index_in_dim(joined, here, 0, keepdims=False).astype(jnp.float32)
+    for shift in range(1, replicas):
+        outgoing = lax.dynamic_index_in_dim(joined, (here + shift) % replicas, 0, keepdims=False)
+        incoming = lax.ppermute(
+            outgoing, "dp", perm=[(i, (i + shift) % replicas) for i in range(replicas)]
+        )
+        joined_sum = joined_sum + incoming.astype(jnp.float32)
     expert_sum = joined_sum[None, :expert_rows]
     dense_sum = joined_sum[expert_rows:]
     expert_mean = expert_sum / replicas

time: 220 us -> 220 us (level)
  waiting for transfers between devices: 43.6 us -> 39.1 us
  starting transfers between devices: 11.2 us -> 15.5 us
    all_to_all x1 -> x0, waiting for transfers between devices: 14.7 us -> none  [shards(): received = lax.all_to_all(joined, 'dp', 0, 0, tiled=True)]
    ppermute x0 -> x7, waiting for transfers between devices: none -> 11.7 us  [shards(): lax.ppermute(outgoing, 'dp', perm=[(i, (i + shift) % replicas) for i in r...]
    ppermute x0 -> x7, starting transfers between devices: none -> 10.7 us  [shards(): lax.ppermute(outgoing, 'dp', perm=[(i, (i + shift) % replicas) for i in r...]
    all_to_all x1 -> x0, starting transfers between devices: 6.35 us -> none  [shards(): received = lax.all_to_all(joined, 'dp', 0, 0, tiled=True)]
    unnamed x28 -> x26, local copies, waits for them, and re-layouts: 5.45 us -> 5.44 us
  transfers between devices with their start and end apart: 6 -> 12, of which waited for: 3 -> 5; matrix products, arithmetic and copies ran while one was open for 9% -> 10% of each run, Pallas kernels for 0% -> 0%
where the time goes in v13:
time: 220 us; the launch traced here: 218 us
  blocking collectives  73.4 us (33%)
  matrix products  51.3 us (23%)
  waiting for transfers between devices  39.1 us (18%)
  starting transfers between devices  15.5 us (7%)
  between operations  15.1 us (7%)
  other arithmetic  12.9 us (6%)
  local copies, waits for them, and re-layouts  10.7 us (5%)
    all_gather x1, blocking collectives, shards(): lax.all_gather(dense_master_out.astype(jnp.bfloat16), 'dp', axis=1, tiled...  30.8 us
    all_gather x1, blocking collectives, shards(): lax.all_gather(expert_master_out.astype(jnp.bfloat16), 'dp', axis=2, tile...  30 us
    psum x1, waiting for transfers between devices, shards(): stats_full = lax.psum(placed + 0.05 * partial_stat, ('tensor', 'dp'))  25.2 us
    all_gather x1, blocking collectives, shards(): lax.all_gather(dense_first_out, 'wshard', axis=0, tiled=True)  12.6 us
    dot_general x3, matrix products, quintic_step(): jnp.einsum('bik,bkj->bij', gram_matrix, first_prod, precision=HIGH)  12.1 us
    ppermute x7, waiting for transfers between devices, shards(): lax.ppermute(outgoing, 'dp', perm=[(i, (i + shift) % replicas) for i in r...  11.7 us
    ppermute x7, starting transfers between devices, shards(): lax.ppermute(outgoing, 'dp', perm=[(i, (i + shift) % replicas) for i in r...  10.7 us
    dot_general x3, matrix products, quintic_step(): jnp.einsum('bik,bkj->bij', gram_matrix, current, precision=HIGH)  9.11 us
  transfers between devices with their start and end apart: 12, of which 5 were waited for; matrix products, arithmetic and copies ran while one was open for 10% of the time, Pallas kernels for 0%

profile of v13, /device:TPU:0, one launch (start us, length us, event | category | flops | bytes accessed | tf_op | source)
XLA Modules:
  0.0 218.4 jit_solution(17317904083812047786)
XLA Ops:
  9.8 5.1 %collective-permute-start.6 = (bf16[960,64]{0,1:T(8,128)(2,1)S(1)}, bf16[960,64]{0,1:T(8,128)(2,1)S(1)}, u32[]{:S(2)}, u32[]{:S(2)}) collective-permute-start(bf16[960,64]{0,1:T(8,128)(2,1)S(1)} %fusion.47), channel_id=1, source_target_pairs={{0,112},{16,0},{32,16},{48,32},{64,48},{80,64},{96,80},{112,96},{1... | collective-permute-start | bytes 368648 | tf_op jit(solution)/shard_map/ppermute | solution.py:65
  16.0 2.3 %collective-permute-start.2 = (bf16[960,64]{0,1:T(8,128)(2,1)S(1)}, bf16[960,64]{0,1:T(8,128)(2,1)S(1)}, u32[]{:S(2)}, u32[]{:S(2)}) collective-permute-start(bf16[960,64]{0,1:T(8,128)(2,1)S(1)} %get-tuple-element.73), channel_id=1, source_target_pairs={{0,48},{16,64},{32,80},{48,96},{64,112},{80,0},{96,16},{112,32},{1... | collective-permute-start | bytes 368648 | tf_op jit(solution)/shard_map/ppermute | solution.py:65
  20.6 4.4 %collective-permute-done = bf16[960,64]{0,1:T(8,128)(2,1)S(1)} collective-permute-done((bf16[960,64]{0,1:T(8,128)(2,1)S(1)}, bf16[960,64]{0,1:T(8,128)(2,1)S(1)}, u32[]{:S(2)}, u32[]{:S(2)}) %collective-permute-start) | collective-permute-done | bytes 122912 | tf_op jit(solution)/shard_map/ppermute | solution.py:65
  25.1 4.1 %collective-permute-done.4 = bf16[960,64]{0,1:T(8,128)(2,1)S(1)} collective-permute-done((bf16[960,64]{0,1:T(8,128)(2,1)S(1)}, bf16[960,64]{0,1:T(8,128)(2,1)S(1)}, u32[]{:S(2)}, u32[]{:S(2)}) %collective-permute-start.4) | collective-permute-done | bytes 122912 | tf_op jit(solution)/shard_map/ppermute | solution.py:65
  29.2 3.2 %collective-permute-done.5 = bf16[960,64]{0,1:T(8,128)(2,1)S(1)} collective-permute-done((bf16[960,64]{0,1:T(8,128)(2,1)S(1)}, bf16[960,64]{0,1:T(8,128)(2,1)S(1)}, u32[]{:S(2)}, u32[]{:S(2)}) %collective-permute-start.5) | collective-permute-done | bytes 122912 | tf_op jit(solution)/shard_map/ppermute | solution.py:65
  32.6 3.1 %collective-permute-start.9 = (f32[192,64]{0,1:T(8,128)S(1)}, f32[192,64]{0,1:T(8,128)S(1)}, u32[]{:S(2)}, u32[]{:S(2)}) collective-permute-start(f32[192,64]{0,1:T(8,128)S(1)} %get-tuple-element.81), channel_id=1, source_target_pairs={{0,12},{4,0},{8,4},{12,8},{1,13},{5,1},{9,5},{13,9},{2,14},{6,2},{... | collective-permute-start | bytes 147464 | tf_op jit(solution)/shard_map/ppermute | solution.py:33
  37.3 2.1 convolution_bitcast_fusion.1
  40.0 2.1 collective-permute-done.7
  44.1 2.1 convolution_bitcast_fusion
  46.2 2.6 %maximum_multiply_fusion = f32[2,768,768]{2,1,0:T(8,128)} fusion(f32[1,768,768]{2,1,0:T(8,128)S(1)} %convolution_bitcast_fusion, f32[1,768,768]{2,1,0:T(8,128)S(1)} %convolution_bitcast_fusion.1), kind=kLoop, calls=%fused_computation.9 | loop fusion | flops 2359296 | bytes 9437184 | tf_op jit(solution)/shard_map/mul | solution.py:113
  48.8 1.6 fusion.32
  50.4 12.6 %all-gather = f32[4,192,64]{1,2,0:T(8,128)S(1)} all-gather(f32[1,192,64]{1,2,0:T(8,128)S(1)} %bitcast.95), channel_id=1, replica_groups=mesh['dp'=8,'wshard'=4,'tensor'=4] {'wshard'}, dimensions={0}, use_global_device_ids=true | all-gather | bytes 245760 | tf_op jit(solution)/shard_map/all_gather | solution.py:76
  64.4 4.6 %fusion.5 = f32[2,768,128]{1,2,0:T(8,128)S(1)} fusion(f32[1,768,768]{2,1,0:T(8,128)S(1)} %bitcast.88, f32[1,768,768]{2,1,0:T(8,128)} %param.20, f32[1,768,64]{1,2,0:T(8,128)S(1)} %broadcast_in_dim.29, f32[1,768,64]{1,2,0:T(8,128)S(1)} %bitcast_add_fusion.2, f32[1,768,64]{1,2,0:T(8,128)S(1)} %bitcast.94, f32[1,768,64]{1,2,0:T(8,128)S(1)} %fusion.30), kind=kOutput, calls=%fused_computation.11 | convolution fusion | flops 1813708800 | bytes 6291456 | tf_op jit(solution)/shard_map/bki,bkc->bic/dot_general | solution.py:82
  69.2 4.8 %fusion.4 = f32[2,768,64]{1,2,0:T(8,128)S(1)} fusion(f32[1,768,768]{2,1,0:T(8,128)S(1)} %bitcast.89, f32[1,768,768]{2,1,0:T(8,128)S(1)} %copy-done.1, f32[2,768,128]{1,2,0:T(8,128)S(1)} %fusion.5, f32[2,768,64]{1,2,0:T(8,128)S(1)} %fusion.19), kind=kOutput, calls=%fused_computation.10 | convolution fusion | flops 907345920 | bytes 5898240 | tf_op jit(solution)/shard_map/bik,bkc->bic/dot_general | solution.py:89
  75.4 30.8 %all_gather.11 = bf16[192,512]{0,1:T(8,128)(2,1)} all-gather(bf16[192,64]{0,1:T(8,128)(2,1)S(1)} %get-tuple-element.63), channel_id=1, replica_groups=mesh['dp'=8,'wshard'=4,'tensor'=4] {'dp'}, dimensions={1}, use_global_device_ids=true | all-gather | bytes 221184 | tf_op jit(solution)/shard_map/all_gather | solution.py:98
  106.2 30.0 %all_gather.10 = bf16[1,768,512]{1,2,0:T(8,128)(2,1)S(1)} all-gather(bf16[1,768,64]{1,2,0:T(8,128)(2,1)S(1)} %get-tuple-element.65), channel_id=1, replica_groups=mesh['dp'=8,'wshard'=4,'tensor'=4] {'dp'}, dimensions={2}, use_global_device_ids=true | all-gather | bytes 884736 | tf_op jit(solution)/shard_map/all_gather | solution.py:97
  136.2 25.2 %all-reduce.2.cloned.1.call-done = f32[2,768,768]{2,1,0:T(8,128)} async-done(((f32[2,768,768]{2,1,0:T(8,128)}), f32[2,768,768]{2,1,0:T(8,128)}) %all-reduce.2.cloned.1.call-update) | async-done | bytes 4718608 | tf_op jit(solution)/shard_map/psum | solution.py:113
  161.4 7.5 %multiply_reduce_fusion = (f32[]{:T(128)}, f32[768,768]{1,0:T(8,128)}) fusion(s32[]{:T(128)S(6)} %select_n.130, f32[1,768,768]{2,1,0:T(8,128)} %param.20, f32[1,768,768]{2,1,0:T(8,128)S(1)} %bitcast.90, f32[2,768,768]{2,1,0:T(8,128)} %all-reduce.2.cloned.1.call-done), kind=kOutput, calls=%fused_computation.26 | convolution fusion | flops 2719678464 | bytes 9438212 | tf_op jit(solution)/shard_map/bik,bkj->bij/dot_general | solution.py:124
  169.6 1.8 multiply_bitcast_fusion
  171.5 30.6 %while.10 = (s32[]{:T(128)}, f32[1,768,768]{2,1,0:T(8,128)S(1)}, s32[]{:T(128)}) while((s32[]{:T(128)}, f32[1,768,768]{2,1,0:T(8,128)S(1)}, s32[]{:T(128)}) %tuple.39), condition=%wide.region_3.4_spmd, body=%wide.region_2.3_spmd.sunk | while | flops 8156676096 | bytes 21233708 | solution.py:131
  171.7 3.0 %fusion.75 = f32[768,768]{1,0:T(8,128)S(1)} fusion(f32[1,768,768]{2,1,0:T(8,128)S(1)} %get-tuple-element.101), kind=kOutput, calls=%fused_computation.4.clone.1 | convolution fusion | flops 2717908992 | bytes 4718592 | tf_op jit(solution)/shard_map/while/body/eval_jaxpr/bik,bjk->bij/dot_general | solution.py:17
  174.7 3.0 %fusion.76 = f32[768,768]{1,0:T(8,128)S(1)} fusion(f32[768,768]{1,0:T(8,128)S(1)} %fusion.75, f32[1,768,768]{2,1,0:T(8,128)S(1)} %get-tuple-element.101), kind=kOutput, calls=%fused_computation.2.clone.1 | convolution fusion | flops 2717908992 | bytes 7077888 | tf_op jit(solution)/shard_map/while/body/eval_jaxpr/bik,bkj->bij/dot_general | solution.py:21
  177.8 4.0 %bitcast_add_fusion.4 = f32[1,768,768]{2,1,0:T(8,128)S(1)} fusion(f32[768,768]{1,0:T(8,128)S(1)} %fusion.76, f32[1,768,768]{2,1,0:T(8,128)S(1)} %get-tuple-element.101, f32[768,768]{1,0:T(8,128)S(1)} %fusion.75), kind=kOutput, calls=%fused_computation.clone.1 | convolution fusion | flops 2720858112 | bytes 9437184 | tf_op jit(solution)/shard_map/while/body/eval_jaxpr/bik,bkj->bij/dot_general | solution.py:22
  181.8 3.0 %fusion.75 = f32[768,768]{1,0:T(8,128)S(1)} fusion(f32[1,768,768]{2,1,0:T(8,128)S(1)} %get-tuple-element.101), kind=kOutput, calls=%fused_computation.4.clone.1 | convolution fusion | flops 2717908992 | bytes 4718592 | tf_op jit(solution)/shard_map/while/body/eval_jaxpr/bik,bjk->bij/dot_general | solution.py:17
  184.8 3.0 %fusion.76 = f32[768,768]{1,0:T(8,128)S(1)} fusion(f32[768,768]{1,0:T(8,128)S(1)} %fusion.75, f32[1,768,768]{2,1,0:T(8,128)S(1)} %get-tuple-element.101), kind=kOutput, calls=%fused_computation.2.clone.1 | convolution fusion | flops 2717908992 | bytes 7077888 | tf_op jit(solution)/shard_map/while/body/eval_jaxpr/bik,bkj->bij/dot_general | solution.py:21
  187.9 4.0 %bitcast_add_fusion.4 = f32[1,768,768]{2,1,0:T(8,128)S(1)} fusion(f32[768,768]{1,0:T(8,128)S(1)} %fusion.76, f32[1,768,768]{2,1,0:T(8,128)S(1)} %get-tuple-element.101, f32[768,768]{1,0:T(8,128)S(1)} %fusion.75), kind=kOutput, calls=%fused_computation.clone.1 | convolution fusion | flops 2720858112 | bytes 9437184 | tf_op jit(solution)/shard_map/while/body/eval_jaxpr/bik,bkj->bij/dot_general | solution.py:22
  191.9 3.0 %fusion.75 = f32[768,768]{1,0:T(8,128)S(1)} fusion(f32[1,768,768]{2,1,0:T(8,128)S(1)} %get-tuple-element.101), kind=kOutput, calls=%fused_computation.4.clone.1 | convolution fusion | flops 2717908992 | bytes 4718592 | tf_op jit(solution)/shard_map/while/body/eval_jaxpr/bik,bjk->bij/dot_general | solution.py:17
  195.0 3.0 %fusion.76 = f32[768,768]{1,0:T(8,128)S(1)} fusion(f32[768,768]{1,0:T(8,128)S(1)} %fusion.75, f32[1,768,768]{2,1,0:T(8,128)S(1)} %get-tuple-element.101), kind=kOutput, calls=%fused_computation.2.clone.1 | convolution fusion | flops 2717908992 | bytes 7077888 | tf_op jit(solution)/shard_map/while/body/eval_jaxpr/bik,bkj->bij/dot_general | solution.py:21
  198.0 4.0 %bitcast_add_fusion.4 = f32[1,768,768]{2,1,0:T(8,128)S(1)} fusion(f32[768,768]{1,0:T(8,128)S(1)} %fusion.76, f32[1,768,768]{2,1,0:T(8,128)S(1)} %get-tuple-element.101, f32[768,768]{1,0:T(8,128)S(1)} %fusion.75), kind=kOutput, calls=%fused_computation.clone.1 | convolution fusion | flops 2720858112 | bytes 9437184 | tf_op jit(solution)/shard_map/while/body/eval_jaxpr/bik,bkj->bij/dot_general | solution.py:22
  202.9 1.8 copy.33
  205.8 1.6 dynamic-slice_bitcast_fusion
  207.4 4.2 %select_bitcast_fusion = (f32[768,768]{1,0:T(8,128)}, f32[1,768,768]{2,1,0:T(8,128)}) fusion(f32[1,768,768]{2,1,0:T(8,128)} %collective-permute-done.10, f32[1,768,768]{2,1,0:T(8,128)S(1)} %get-tuple-element.31, pred[]{:T(512)S(6)} %eq.16), kind=kLoop, calls=%fused_computation.24 | loop fusion | flops 1179648 | bytes 9437185 | tf_op jit(solution)/shard_map/squeeze | solution.py:136
  (59 shorter events, 15.3 us)
Async XLA Ops:
  7.2 154.3 %all-reduce.2.cloned.1.call-start = ((), (), s32[]{:S(2)}) async-start(), calls=%async_computation | async-start | bytes 9437184 | tf_op jit(solution)/shard_map/psum | solution.py:113
  9.8 22.8 %copy-start.10 = (f32[192,64]{0,1:T(8,128)S(1)}, f32[192,64]{0,1:T(8,128)}, u32[]{:S(2)}) copy-start(f32[192,64]{0,1:T(8,128)} %param.22) | copy-start | bytes 147460
  9.8 10.0 %collective-permute-start.6 = (bf16[960,64]{0,1:T(8,128)(2,1)S(1)}, bf16[960,64]{0,1:T(8,128)(2,1)S(1)}, u32[]{:S(2)}, u32[]{:S(2)}) collective-permute-start(bf16[960,64]{0,1:T(8,128)(2,1)S(1)} %fusion.47), channel_id=1, source_target_pairs={{0,112},{16,0},{32,16},{48,32},{64,48},{80,64},{96,80},{112,96},{1... | collective-permute-start | bytes 368648 | tf_op jit(solution)/shard_map/ppermute | solution.py:65
  15.0 10.0 %collective-permute-start = (bf16[960,64]{0,1:T(8,128)(2,1)S(1)}, bf16[960,64]{0,1:T(8,128)(2,1)S(1)}, u32[]{:S(2)}, u32[]{:S(2)}) collective-permute-start(bf16[960,64]{0,1:T(8,128)(2,1)S(1)} %get-tuple-element.71), channel_id=1, source_target_pairs={{0,16},{16,32},{32,48},{48,64},{64,80},{80,96},{96,112},{112,0},{1... | collective-permute-start | bytes 368648 | tf_op jit(solution)/shard_map/ppermute | solution.py:65
  15.1 10.0 %collective-permute-start.1 = (bf16[960,64]{0,1:T(8,128)(2,1)S(1)}, bf16[960,64]{0,1:T(8,128)(2,1)S(1)}, u32[]{:S(2)}, u32[]{:S(2)}) collective-permute-start(bf16[960,64]{0,1:T(8,128)(2,1)S(1)} %get-tuple-element.72), channel_id=1, source_target_pairs={{0,32},{16,48},{32,64},{48,80},{64,96},{80,112},{96,0},{112,16},{1... | collective-permute-start | bytes 368648 | tf_op jit(solution)/shard_map/ppermute | solution.py:65
  16.0 9.0 %collective-permute-start.2 = (bf16[960,64]{0,1:T(8,128)(2,1)S(1)}, bf16[960,64]{0,1:T(8,128)(2,1)S(1)}, u32[]{:S(2)}, u32[]{:S(2)}) collective-permute-start(bf16[960,64]{0,1:T(8,128)(2,1)S(1)} %get-tuple-element.73), channel_id=1, source_target_pairs={{0,48},{16,64},{32,80},{48,96},{64,112},{80,0},{96,16},{112,32},{1... | collective-permute-start | bytes 368648 | tf_op jit(solution)/shard_map/ppermute | solution.py:65
  18.3 6.8 %collective-permute-start.3 = (bf16[960,64]{0,1:T(8,128)(2,1)S(1)}, bf16[960,64]{0,1:T(8,128)(2,1)S(1)}, u32[]{:S(2)}, u32[]{:S(2)}) collective-permute-start(bf16[960,64]{0,1:T(8,128)(2,1)S(1)} %get-tuple-element.74), channel_id=1, source_target_pairs={{0,64},{16,80},{32,96},{48,112},{64,0},{80,16},{96,32},{112,48},{1... | collective-permute-start | bytes 368648 | tf_op jit(solution)/shard_map/ppermute | solution.py:65
  19.8 9.4 %collective-permute-start.4 = (bf16[960,64]{0,1:T(8,128)(2,1)S(1)}, bf16[960,64]{0,1:T(8,128)(2,1)S(1)}, u32[]{:S(2)}, u32[]{:S(2)}) collective-permute-start(bf16[960,64]{0,1:T(8,128)(2,1)S(1)} %get-tuple-element.75), channel_id=1, source_target_pairs={{0,80},{16,96},{32,112},{48,0},{64,16},{80,32},{96,48},{112,64},{1... | collective-permute-start | bytes 368648 | tf_op jit(solution)/shard_map/ppermute | solution.py:65
  25.0 7.3 %collective-permute-start.5 = (bf16[960,64]{0,1:T(8,128)(2,1)S(1)}, bf16[960,64]{0,1:T(8,128)(2,1)S(1)}, u32[]{:S(2)}, u32[]{:S(2)}) collective-permute-start(bf16[960,64]{0,1:T(8,128)(2,1)S(1)} %get-tuple-element.76), channel_id=1, source_target_pairs={{0,96},{16,112},{32,0},{48,16},{64,32},{80,48},{96,64},{112,80},{1... | collective-permute-start | bytes 368648 | tf_op jit(solution)/shard_map/ppermute | solution.py:65
  32.6 17.8 %copy-start.3 = (f32[192,64]{0,1:T(8,128)}, f32[192,64]{0,1:T(8,128)S(1)}, u32[]{:S(2)}) copy-start(f32[192,64]{0,1:T(8,128)S(1)} %get-tuple-element.80) | copy-start | bytes 147460
  32.6 10.7 %collective-permute-start.9 = (f32[192,64]{0,1:T(8,128)S(1)}, f32[192,64]{0,1:T(8,128)S(1)}, u32[]{:S(2)}, u32[]{:S(2)}) collective-permute-start(f32[192,64]{0,1:T(8,128)S(1)} %get-tuple-element.81), channel_id=1, source_target_pairs={{0,12},{4,0},{8,4},{12,8},{1,13},{5,1},{9,5},{13,9},{2,14},{6,2},{... | collective-permute-start | bytes 147464 | tf_op jit(solution)/shard_map/ppermute | solution.py:33
  35.7 7.0 %collective-permute-start.8 = (f32[192,64]{0,1:T(8,128)S(1)}, f32[192,64]{0,1:T(8,128)S(1)}, u32[]{:S(2)}, u32[]{:S(2)}) collective-permute-start(f32[192,64]{0,1:T(8,128)S(1)} %get-tuple-element.81), channel_id=1, source_target_pairs={{0,8},{4,12},{8,0},{12,4},{1,9},{5,13},{9,1},{13,5},{2,10},{6,14},... | collective-permute-start | bytes 147464 | tf_op jit(solution)/shard_map/ppermute | solution.py:33
  36.3 5.8 %collective-permute-start.7 = (f32[192,64]{0,1:T(8,128)S(1)}, f32[192,64]{0,1:T(8,128)S(1)}, u32[]{:S(2)}, u32[]{:S(2)}) collective-permute-start(f32[192,64]{0,1:T(8,128)S(1)} %get-tuple-element.81), channel_id=1, source_target_pairs={{0,4},{4,8},{8,12},{12,0},{1,5},{5,9},{9,13},{13,1},{2,6},{6,10},{... | collective-permute-start | bytes 147464 | tf_op jit(solution)/shard_map/ppermute | solution.py:33
  46.2 2.6 %copy-start.7 = (f32[24,768]{1,0:T(8,128)S(1)}, f32[24,768]{1,0:T(8,128)}, u32[]{:S(2)}) copy-start(f32[24,768]{1,0:T(8,128)} %param.24) | copy-start | bytes 221188
  46.2 2.6 %copy-start.8 = (f32[1,24,768]{2,1,0:T(8,128)S(1)}, f32[1,24,768]{2,1,0:T(8,128)}, u32[]{:S(2)}) copy-start(f32[1,24,768]{2,1,0:T(8,128)} %param.19) | copy-start | bytes 221188
  50.4 14.0 %copy-start = (f32[768,768]{1,0:T(8,128)S(1)}, f32[768,768]{1,0:T(8,128)}, u32[]{:S(2)}) copy-start(f32[768,768]{1,0:T(8,128)} %param.25) | copy-start | bytes 7077892
  64.3 4.7 %copy-start.2 = (f32[1,768,64]{1,2,0:T(8,128)}, f32[1,768,64]{1,2,0:T(8,128)S(1)}, u32[]{:S(2)}) copy-start(f32[1,768,64]{1,2,0:T(8,128)S(1)} %bitcast_add_fusion.2) | copy-start | bytes 589828
  64.3 4.7 %copy-start.4 = (f32[768,64]{0,1:T(8,128)S(1)}, f32[768,64]{0,1:T(8,128)}, u32[]{:S(2)}) copy-start(f32[768,64]{0,1:T(8,128)} %param.23) | copy-start | bytes 589828
  64.4 4.7 %copy-start.5 = (f32[1,768,64]{1,2,0:T(8,128)S(1)}, f32[1,768,64]{1,2,0:T(8,128)}, u32[]{:S(2)}) copy-start(f32[1,768,64]{1,2,0:T(8,128)} %param.18) | copy-start | bytes 589828
  64.4 4.8 %copy-start.1 = (f32[1,768,768]{2,1,0:T(8,128)S(1)}, f32[1,768,768]{2,1,0:T(8,128)}, u32[]{:S(2)}) copy-start(f32[1,768,768]{2,1,0:T(8,128)} %param.20) | copy-start | bytes 7077892
  69.2 4.8 %copy-start.6 = (f32[1,768,64]{1,2,0:T(8,128)S(1)}, f32[1,768,64]{1,2,0:T(8,128)}, u32[]{:S(2)}) copy-start(f32[1,768,64]{1,2,0:T(8,128)} %param.16) | copy-start | bytes 589828
  69.2 5.5 %copy-start.9 = (f32[192,64]{0,1:T(8,128)S(1)}, f32[192,64]{0,1:T(8,128)}, u32[]{:S(2)}) copy-start(f32[192,64]{0,1:T(8,128)} %param.21) | copy-start | bytes 147460
  202.0 5.4 %collective-permute-start.10 = (f32[1,768,768]{2,1,0:T(8,128)S(1)}, f32[1,768,768]{2,1,0:T(8,128)}, u32[]{:S(2)}, u32[]{:S(2)}) collective-permute-start(f32[1,768,768]{2,1,0:T(8,128)S(1)} %get-tuple-element.31), channel_id=1, source_target_pairs={{0,1},{1,0},{2,3},{3,2},{4,5},{5,4},{6,7},{7,6},{8,9},{9,8},{10,11... | collective-permute-start | bytes 7077896 | tf_op jit(solution)/shard_map/ppermute | solution.py:132
Sparse Core Ops, SparseCore 0:
  50.5 110.8 all-reduce.1

commit v14 on v11

--- a/solution.py
+++ b/solution.py
@@ -21,6 +21,21 @@
     first_prod = jnp.einsum("bik,bkj->bij", gram_matrix, current, precision=HIGH)
     second_prod = jnp.einsum("bik,bkj->bij", gram_matrix, first_prod, precision=HIGH)
     return linear_coef * current + cubic_coef * first_prod + quintic_coef * second_prod
+
+
+def replica_sum(local, axis):
+    replicas = lax.axis_size(axis)
+    here = lax.axis_index(axis)
+    owned = local.shape[1] // replicas
+    chunks = local.reshape(local.shape[0], replicas, owned).transpose(1, 0, 2)
+    total = lax.dynamic_index_in_dim(chunks, here, 0, keepdims=False).astype(jnp.float32)
+    for shift in range(1, replicas):
+        outgoing = lax.dynamic_index_in_dim(chunks, (here + shift) % replicas, 0, keepdims=False)
+        incoming = lax.ppermute(
+            outgoing, axis, perm=[(i, (i + shift) % replicas) for i in range(replicas)]
+        )
+        total = total + incoming.astype(jnp.float32)
+    return total
 
 
 def gather_rows(block, axis):
@@ -54,14 +69,8 @@
     experts_here = expert_grads.shape[1]
     expert_local = expert_grads.reshape(expert_grads.shape[2:])
     dense_local = dense_grads.reshape(dense_grads.shape[1:])
-    expert_rows = expert_local.shape[0]
-    joined = jnp.concatenate([expert_local, dense_local], 0)
-    owned = joined.shape[1] // replicas
-    joined = joined.reshape(joined.shape[0], replicas, owned).transpose(1, 0, 2)
-    received = lax.all_to_all(joined, "dp", 0, 0, tiled=True)
-    joined_sum = jnp.sum(received.astype(jnp.float32), 0)
-    expert_sum = joined_sum[None, :expert_rows]
-    dense_sum = joined_sum[expert_rows:]
+    dense_sum = replica_sum(dense_local, "dp")
+    expert_sum = replica_sum(expert_local, "dp")[None]
     expert_mean = expert_sum / replicas
     dense_mean = dense_sum / replicas
     expert_first_out = 0.9 * expert_first + 0.1 * expert_mean

time: 220 us -> 225 us (1.023)
  starting transfers between devices: 11.2 us -> 30.8 us
  waiting for transfers between devices: 43.6 us -> 28.9 us
    ppermute x0 -> x14, starting transfers between devices: none -> 24.8 us  [replica_sum(): lax.ppermute(outgoing, axis, perm=[(i, (i + shift) % replicas) for i in r...]
    all_to_all x1 -> x0, waiting for transfers between devices: 14.7 us -> none  [shards(): received = lax.all_to_all(joined, 'dp', 0, 0, tiled=True)]
    all_to_all x1 -> x0, starting transfers between devices: 6.35 us -> none  [shards(): received = lax.all_to_all(joined, 'dp', 0, 0, tiled=True)]
    ppermute x0 -> x14, waiting for transfers between devices: none -> 2.85 us  [replica_sum(): lax.ppermute(outgoing, axis, perm=[(i, (i + shift) % replicas) for i in r...]
    unnamed x28 -> x26, local copies, waits for them, and re-layouts: 5.45 us -> 5.44 us
  transfers between devices with their start and end apart: 6 -> 19, of which waited for: 3 -> 3; matrix products, arithmetic and copies ran while one was open for 9% -> 11% of each run, Pallas kernels for 0% -> 0%
where the time goes in v14:
time: 225 us; the launch traced here: 223 us
  blocking collectives  73 us (32%)
  matrix products  51.3 us (23%)
  starting transfers between devices  30.8 us (14%)
  waiting for transfers between devices  28.9 us (13%)
  between operations  15.3 us (7%)
  other arithmetic  12.8 us (6%)
  local copies, waits for them, and re-layouts  10.6 us (5%)
    all_gather x1, blocking collectives, shards(): lax.all_gather(dense_master_out.astype(jnp.bfloat16), 'dp', axis=1, tiled...  30.8 us
    all_gather x1, blocking collectives, shards(): lax.all_gather(expert_master_out.astype(jnp.bfloat16), 'dp', axis=2, tile...  29.8 us
    psum x1, waiting for transfers between devices, shards(): stats_full = lax.psum(placed + 0.05 * partial_stat, ('tensor', 'dp'))  26 us
    ppermute x14, starting transfers between devices, replica_sum(): lax.ppermute(outgoing, axis, perm=[(i, (i + shift) % replicas) for i in r...  24.8 us
    all_gather x1, blocking collectives, shards(): lax.all_gather(dense_first_out, 'wshard', axis=0, tiled=True)  12.4 us
    dot_general x3, matrix products, quintic_step(): jnp.einsum('bik,bkj->bij', gram_matrix, first_prod, precision=HIGH)  12.1 us
    dot_general x3, matrix products, quintic_step(): jnp.einsum('bik,bkj->bij', gram_matrix, current, precision=HIGH)  9.11 us
    dot_general x3, matrix products, local_gram(): return jnp.einsum('bik,bjk->bij', current, current, precision=HIGH)  9.09 us
  transfers between devices with their start and end apart: 19, of which 3 were waited for; matrix products, arithmetic and copies ran while one was open for 11% of the time, Pallas kernels for 0%

profile of v14, /device:TPU:0, one launch (start us, length us, event | category | flops | bytes accessed | tf_op | source)
XLA Modules:
  0.0 222.7 jit_solution(5709652222327140399)
XLA Ops:
  8.5 2.1 collective-permute-start.7
  10.6 3.1 %collective-permute-start.13 = (bf16[192,64]{0,1:T(8,128)(2,1)S(1)}, bf16[192,64]{0,1:T(8,128)(2,1)S(1)}, u32[]{:S(2)}, u32[]{:S(2)}) collective-permute-start(bf16[192,64]{0,1:T(8,128)(2,1)S(1)} %get-tuple-element.86), channel_id=1, source_target_pairs={{0,112},{16,0},{32,16},{48,32},{64,48},{80,64},{96,80},{112,96},{1... | collective-permute-start | bytes 73736 | tf_op jit(solution)/shard_map/ppermute | solution.py:34
  13.7 1.8 collective-permute-start.12
  22.4 4.1 %collective-permute-start.6 = (bf16[768,64]{0,1:T(8,128)(2,1)S(1)}, bf16[768,64]{0,1:T(8,128)(2,1)S(1)}, u32[]{:S(2)}, u32[]{:S(2)}) collective-permute-start(bf16[768,64]{0,1:T(8,128)(2,1)S(1)} %get-tuple-element.76), channel_id=1, source_target_pairs={{0,112},{16,0},{32,16},{48,32},{64,48},{80,64},{96,80},{112,96},{1... | collective-permute-start | bytes 294920 | tf_op jit(solution)/shard_map/ppermute | solution.py:34
  27.1 1.6 collective-permute-start.14
  28.8 2.9 %collective-permute-start.15 = (f32[192,64]{0,1:T(8,128)S(1)}, f32[192,64]{0,1:T(8,128)S(1)}, u32[]{:S(2)}, u32[]{:S(2)}) collective-permute-start(f32[192,64]{0,1:T(8,128)S(1)} %broadcast_multiply_fusion), channel_id=1, source_target_pairs={{0,8},{4,12},{8,0},{12,4},{1,9},{5,13},{9,1},{13,5},{2,10},{6,14},... | collective-permute-start | bytes 147464 | tf_op jit(solution)/shard_map/ppermute | solution.py:48
  38.6 2.5 %collective-permute-start.2 = (bf16[768,64]{0,1:T(8,128)(2,1)S(1)}, bf16[768,64]{0,1:T(8,128)(2,1)S(1)}, u32[]{:S(2)}, u32[]{:S(2)}) collective-permute-start(bf16[768,64]{0,1:T(8,128)(2,1)S(1)} %get-tuple-element.80), channel_id=1, source_target_pairs={{0,48},{16,64},{32,80},{48,96},{64,112},{80,0},{96,16},{112,32},{1... | collective-permute-start | bytes 294920 | tf_op jit(solution)/shard_map/ppermute | solution.py:34
  41.1 2.7 %collective-permute-start.1 = (bf16[768,64]{0,1:T(8,128)(2,1)S(1)}, bf16[768,64]{0,1:T(8,128)(2,1)S(1)}, u32[]{:S(2)}, u32[]{:S(2)}) collective-permute-start(bf16[768,64]{0,1:T(8,128)(2,1)S(1)} %get-tuple-element.81), channel_id=1, source_target_pairs={{0,32},{16,48},{32,64},{48,80},{64,96},{80,112},{96,0},{112,16},{1... | collective-permute-start | bytes 294920 | tf_op jit(solution)/shard_map/ppermute | solution.py:34
  43.8 2.0 convolution_bitcast_fusion
  45.9 2.3 %collective-permute-done.1 = bf16[768,64]{0,1:T(8,128)(2,1)S(1)} collective-permute-done((bf16[768,64]{0,1:T(8,128)(2,1)S(1)}, bf16[768,64]{0,1:T(8,128)(2,1)S(1)}, u32[]{:S(2)}, u32[]{:S(2)}) %collective-permute-start.1) | collective-permute-done | bytes 98336 | tf_op jit(solution)/shard_map/ppermute | solution.py:34
  48.3 2.1 convolution_bitcast_fusion.1
  50.4 2.6 %maximum_multiply_fusion = f32[2,768,768]{2,1,0:T(8,128)} fusion(f32[1,768,768]{2,1,0:T(8,128)S(1)} %convolution_bitcast_fusion, f32[1,768,768]{2,1,0:T(8,128)S(1)} %convolution_bitcast_fusion.1), kind=kLoop, calls=%fused_computation.9 | loop fusion | flops 2359296 | bytes 9437184 | tf_op jit(solution)/shard_map/mul | solution.py:116
  54.6 12.4 %all-gather = f32[4,192,64]{1,2,0:T(8,128)S(1)} all-gather(f32[1,192,64]{1,2,0:T(8,128)S(1)} %bitcast.112), channel_id=1, replica_groups=mesh['dp'=8,'wshard'=4,'tensor'=4] {'wshard'}, dimensions={0}, use_global_device_ids=true | all-gather | bytes 245760 | tf_op jit(solution)/shard_map/all_gather | solution.py:79
  68.4 4.6 %fusion.5 = f32[2,768,128]{1,2,0:T(8,128)S(1)} fusion(f32[1,768,768]{2,1,0:T(8,128)S(1)} %bitcast.104, f32[1,768,768]{2,1,0:T(8,128)} %param.20, f32[1,768,64]{1,2,0:T(8,128)S(1)} %broadcast_in_dim.29, f32[1,768,64]{1,2,0:T(8,128)S(1)} %bitcast_add_fusion.2, f32[1,768,64]{1,2,0:T(8,128)S(1)} %bitcast.107, f32[1,768,64]{1,2,0:T(8,128)S(1)} %get-tuple-element.67), kind=kOutput, calls=%fused_computation.11 | convolution fusion | flops 1813708800 | bytes 6291456 | tf_op jit(solution)/shard_map/bki,bkc->bic/dot_general | solution.py:85
  73.2 4.8 %fusion.4 = f32[2,768,64]{1,2,0:T(8,128)S(1)} fusion(f32[1,768,768]{2,1,0:T(8,128)S(1)} %bitcast.105, f32[1,768,768]{2,1,0:T(8,128)S(1)} %copy-done.1, f32[2,768,128]{1,2,0:T(8,128)S(1)} %fusion.5, f32[2,768,64]{1,2,0:T(8,128)S(1)} %fusion.19), kind=kOutput, calls=%fused_computation.10 | convolution fusion | flops 907345920 | bytes 5898240 | tf_op jit(solution)/shard_map/bik,bkc->bic/dot_general | solution.py:92
  79.4 30.8 %all_gather.11 = bf16[192,512]{0,1:T(8,128)(2,1)} all-gather(bf16[192,64]{0,1:T(8,128)(2,1)S(1)} %get-tuple-element.63), channel_id=1, replica_groups=mesh['dp'=8,'wshard'=4,'tensor'=4] {'dp'}, dimensions={1}, use_global_device_ids=true | all-gather | bytes 221184 | tf_op jit(solution)/shard_map/all_gather | solution.py:101
  110.2 29.8 %all_gather.10 = bf16[1,768,512]{1,2,0:T(8,128)(2,1)S(1)} all-gather(bf16[1,768,64]{1,2,0:T(8,128)(2,1)S(1)} %get-tuple-element.65), channel_id=1, replica_groups=mesh['dp'=8,'wshard'=4,'tensor'=4] {'dp'}, dimensions={2}, use_global_device_ids=true | all-gather | bytes 884736 | tf_op jit(solution)/shard_map/all_gather | solution.py:100
  140.0 26.0 %all-reduce.2.cloned.1.call-done = f32[2,768,768]{2,1,0:T(8,128)} async-done(((f32[2,768,768]{2,1,0:T(8,128)}), f32[2,768,768]{2,1,0:T(8,128)}) %all-reduce.2.cloned.1.call-update) | async-done | bytes 4718608 | tf_op jit(solution)/shard_map/psum | solution.py:116
  166.0 7.5 %multiply_reduce_fusion = (f32[]{:T(128)}, f32[768,768]{1,0:T(8,128)}) fusion(s32[]{:T(128)S(6)} %select_n.153, f32[1,768,768]{2,1,0:T(8,128)} %param.20, f32[1,768,768]{2,1,0:T(8,128)S(1)} %bitcast.106, f32[2,768,768]{2,1,0:T(8,128)} %all-reduce.2.cloned.1.call-done), kind=kOutput, calls=%fused_computation.18 | convolution fusion | flops 2719678464 | bytes 9438212 | tf_op jit(solution)/shard_map/bik,bkj->bij/dot_general | solution.py:127
  174.2 1.8 multiply_bitcast_fusion
  176.0 30.4 %while.10 = (s32[]{:T(128)}, f32[1,768,768]{2,1,0:T(8,128)S(1)}, s32[]{:T(128)}) while((s32[]{:T(128)}, f32[1,768,768]{2,1,0:T(8,128)S(1)}, s32[]{:T(128)}) %tuple.47), condition=%wide.region_3.4_spmd, body=%wide.region_2.3_spmd.sunk | while | flops 8156676096 | bytes 21233708 | solution.py:134
  176.0 3.0 %fusion.68 = f32[768,768]{1,0:T(8,128)S(1)} fusion(f32[1,768,768]{2,1,0:T(8,128)S(1)} %get-tuple-element.111), kind=kOutput, calls=%fused_computation.4.clone.1 | convolution fusion | flops 2717908992 | bytes 4718592 | tf_op jit(solution)/shard_map/while/body/eval_jaxpr/bik,bjk->bij/dot_general | solution.py:17
  179.0 3.0 %fusion.69 = f32[768,768]{1,0:T(8,128)S(1)} fusion(f32[768,768]{1,0:T(8,128)S(1)} %fusion.68, f32[1,768,768]{2,1,0:T(8,128)S(1)} %get-tuple-element.111), kind=kOutput, calls=%fused_computation.2.clone.1 | convolution fusion | flops 2717908992 | bytes 7077888 | tf_op jit(solution)/shard_map/while/body/eval_jaxpr/bik,bkj->bij/dot_general | solution.py:21
  182.1 4.0 %bitcast_add_fusion.4 = f32[1,768,768]{2,1,0:T(8,128)S(1)} fusion(f32[768,768]{1,0:T(8,128)S(1)} %fusion.69, f32[1,768,768]{2,1,0:T(8,128)S(1)} %get-tuple-element.111, f32[768,768]{1,0:T(8,128)S(1)} %fusion.68), kind=kOutput, calls=%fused_computation.clone.1 | convolution fusion | flops 2720858112 | bytes 9437184 | tf_op jit(solution)/shard_map/while/body/eval_jaxpr/bik,bkj->bij/dot_general | solution.py:22
  186.1 3.0 %fusion.68 = f32[768,768]{1,0:T(8,128)S(1)} fusion(f32[1,768,768]{2,1,0:T(8,128)S(1)} %get-tuple-element.111), kind=kOutput, calls=%fused_computation.4.clone.1 | convolution fusion | flops 2717908992 | bytes 4718592 | tf_op jit(solution)/shard_map/while/body/eval_jaxpr/bik,bjk->bij/dot_general | solution.py:17
  189.2 3.0 %fusion.69 = f32[768,768]{1,0:T(8,128)S(1)} fusion(f32[768,768]{1,0:T(8,128)S(1)} %fusion.68, f32[1,768,768]{2,1,0:T(8,128)S(1)} %get-tuple-element.111), kind=kOutput, calls=%fused_computation.2.clone.1 | convolution fusion | flops 2717908992 | bytes 7077888 | tf_op jit(solution)/shard_map/while/body/eval_jaxpr/bik,bkj->bij/dot_general | solution.py:21
  192.2 4.0 %bitcast_add_fusion.4 = f32[1,768,768]{2,1,0:T(8,128)S(1)} fusion(f32[768,768]{1,0:T(8,128)S(1)} %fusion.69, f32[1,768,768]{2,1,0:T(8,128)S(1)} %get-tuple-element.111, f32[768,768]{1,0:T(8,128)S(1)} %fusion.68), kind=kOutput, calls=%fused_computation.clone.1 | convolution fusion | flops 2720858112 | bytes 9437184 | tf_op jit(solution)/shard_map/while/body/eval_jaxpr/bik,bkj->bij/dot_general | solution.py:22
  196.2 3.0 %fusion.68 = f32[768,768]{1,0:T(8,128)S(1)} fusion(f32[1,768,768]{2,1,0:T(8,128)S(1)} %get-tuple-element.111), kind=kOutput, calls=%fused_computation.4.clone.1 | convolution fusion | flops 2717908992 | bytes 4718592 | tf_op jit(solution)/shard_map/while/body/eval_jaxpr/bik,bjk->bij/dot_general | solution.py:17
  199.3 3.0 %fusion.69 = f32[768,768]{1,0:T(8,128)S(1)} fusion(f32[768,768]{1,0:T(8,128)S(1)} %fusion.68, f32[1,768,768]{2,1,0:T(8,128)S(1)} %get-tuple-element.111), kind=kOutput, calls=%fused_computation.2.clone.1 | convolution fusion | flops 2717908992 | bytes 7077888 | tf_op jit(solution)/shard_map/while/body/eval_jaxpr/bik,bkj->bij/dot_general | solution.py:21
  202.3 4.0 %bitcast_add_fusion.4 = f32[1,768,768]{2,1,0:T(8,128)S(1)} fusion(f32[768,768]{1,0:T(8,128)S(1)} %fusion.69, f32[1,768,768]{2,1,0:T(8,128)S(1)} %get-tuple-element.111, f32[768,768]{1,0:T(8,128)S(1)} %fusion.68), kind=kOutput, calls=%fused_computation.clone.1 | convolution fusion | flops 2720858112 | bytes 9437184 | tf_op jit(solution)/shard_map/while/body/eval_jaxpr/bik,bkj->bij/dot_general | solution.py:22
  207.2 1.8 copy.33
  211.7 4.2 %select_bitcast_fusion = (f32[768,768]{1,0:T(8,128)}, f32[1,768,768]{2,1,0:T(8,128)}) fusion(f32[1,768,768]{2,1,0:T(8,128)} %collective-permute-done.17, f32[1,768,768]{2,1,0:T(8,128)S(1)} %get-tuple-element.31, pred[]{:T(512)S(6)} %eq.23), kind=kLoop, calls=%fused_computation.16 | loop fusion | flops 1179648 | bytes 9437185 | tf_op jit(solution)/shard_map/squeeze | solution.py:139
  (73 shorter events, 23.7 us)
Async XLA Ops:
  7.2 19.9 %copy-start.10 = (f32[192,64]{0,1:T(8,128)S(1)}, f32[192,64]{0,1:T(8,128)}, u32[]{:S(2)}) copy-start(f32[192,64]{0,1:T(8,128)} %param.22) | copy-start | bytes 147460
  7.2 158.8 %all-reduce.2.cloned.1.call-start = ((), (), s32[]{:S(2)}) async-start(), calls=%async_computation | async-start | bytes 9437184 | tf_op jit(solution)/shard_map/psum | solution.py:116
  8.5 10.9 %collective-permute-start.7 = (bf16[192,64]{0,1:T(8,128)(2,1)S(1)}, bf16[192,64]{0,1:T(8,128)(2,1)S(1)}, u32[]{:S(2)}, u32[]{:S(2)}) collective-permute-start(bf16[192,64]{0,1:T(8,128)(2,1)S(1)} %get-tuple-element.85), channel_id=1, source_target_pairs={{0,16},{16,32},{32,48},{48,64},{64,80},{80,96},{96,112},{112,0},{1... | collective-permute-start | bytes 73736 | tf_op jit(solution)/shard_map/ppermute | solution.py:34
  10.6 10.2 %collective-permute-start.13 = (bf16[192,64]{0,1:T(8,128)(2,1)S(1)}, bf16[192,64]{0,1:T(8,128)(2,1)S(1)}, u32[]{:S(2)}, u32[]{:S(2)}) collective-permute-start(bf16[192,64]{0,1:T(8,128)(2,1)S(1)} %get-tuple-element.86), channel_id=1, source_target_pairs={{0,112},{16,0},{32,16},{48,32},{64,48},{80,64},{96,80},{112,96},{1... | collective-permute-start | bytes 73736 | tf_op jit(solution)/shard_map/ppermute | solution.py:34
  13.7 8.6 %collective-permute-start.12 = (bf16[192,64]{0,1:T(8,128)(2,1)S(1)}, bf16[192,64]{0,1:T(8,128)(2,1)S(1)}, u32[]{:S(2)}, u32[]{:S(2)}) collective-permute-start(bf16[192,64]{0,1:T(8,128)(2,1)S(1)} %get-tuple-element.87), channel_id=1, source_target_pairs={{0,96},{16,112},{32,0},{48,16},{64,32},{80,48},{96,64},{112,80},{1... | collective-permute-start | bytes 73736 | tf_op jit(solution)/shard_map/ppermute | solution.py:34
  15.5 6.9 %collective-permute-start.11 = (bf16[192,64]{0,1:T(8,128)(2,1)S(1)}, bf16[192,64]{0,1:T(8,128)(2,1)S(1)}, u32[]{:S(2)}, u32[]{:S(2)}) collective-permute-start(bf16[192,64]{0,1:T(8,128)(2,1)S(1)} %get-tuple-element.88), channel_id=1, source_target_pairs={{0,80},{16,96},{32,112},{48,0},{64,16},{80,32},{96,48},{112,64},{1... | collective-permute-start | bytes 73736 | tf_op jit(solution)/shard_map/ppermute | solution.py:34
  16.5 10.0 %collective-permute-start.10 = (bf16[192,64]{0,1:T(8,128)(2,1)S(1)}, bf16[192,64]{0,1:T(8,128)(2,1)S(1)}, u32[]{:S(2)}, u32[]{:S(2)}) collective-permute-start(bf16[192,64]{0,1:T(8,128)(2,1)S(1)} %get-tuple-element.89), channel_id=1, source_target_pairs={{0,64},{16,80},{32,96},{48,112},{64,0},{80,16},{96,32},{112,48},{1... | collective-permute-start | bytes 73736 | tf_op jit(solution)/shard_map/ppermute | solution.py:34
  19.4 7.1 %collective-permute-start.9 = (bf16[192,64]{0,1:T(8,128)(2,1)S(1)}, bf16[192,64]{0,1:T(8,128)(2,1)S(1)}, u32[]{:S(2)}, u32[]{:S(2)}) collective-permute-start(bf16[192,64]{0,1:T(8,128)(2,1)S(1)} %get-tuple-element.90), channel_id=1, source_target_pairs={{0,48},{16,64},{32,80},{48,96},{64,112},{80,0},{96,16},{112,32},{1... | collective-permute-start | bytes 73736 | tf_op jit(solution)/shard_map/ppermute | solution.py:34
  20.7 6.3 %collective-permute-start.8 = (bf16[192,64]{0,1:T(8,128)(2,1)S(1)}, bf16[192,64]{0,1:T(8,128)(2,1)S(1)}, u32[]{:S(2)}, u32[]{:S(2)}) collective-permute-start(bf16[192,64]{0,1:T(8,128)(2,1)S(1)} %get-tuple-element.91), channel_id=1, source_target_pairs={{0,32},{16,48},{32,64},{48,80},{64,96},{80,112},{96,0},{112,16},{1... | collective-permute-start | bytes 73736 | tf_op jit(solution)/shard_map/ppermute | solution.py:34
  22.3 16.3 %collective-permute-start = (bf16[768,64]{0,1:T(8,128)(2,1)S(1)}, bf16[768,64]{0,1:T(8,128)(2,1)S(1)}, u32[]{:S(2)}, u32[]{:S(2)}) collective-permute-start(bf16[768,64]{0,1:T(8,128)(2,1)S(1)} %get-tuple-element.75), channel_id=1, source_target_pairs={{0,16},{16,32},{32,48},{48,64},{64,80},{80,96},{96,112},{112,0},{1... | collective-permute-start | bytes 294920 | tf_op jit(solution)/shard_map/ppermute | solution.py:34
  22.4 18.7 %collective-permute-start.6 = (bf16[768,64]{0,1:T(8,128)(2,1)S(1)}, bf16[768,64]{0,1:T(8,128)(2,1)S(1)}, u32[]{:S(2)}, u32[]{:S(2)}) collective-permute-start(bf16[768,64]{0,1:T(8,128)(2,1)S(1)} %get-tuple-element.76), channel_id=1, source_target_pairs={{0,112},{16,0},{32,16},{48,32},{64,48},{80,64},{96,80},{112,96},{1... | collective-permute-start | bytes 294920 | tf_op jit(solution)/shard_map/ppermute | solution.py:34
  27.1 27.5 %copy-start.3 = (f32[192,64]{0,1:T(8,128)}, f32[192,64]{0,1:T(8,128)S(1)}, u32[]{:S(2)}) copy-start(f32[192,64]{0,1:T(8,128)S(1)} %get-tuple-element.69) | copy-start | bytes 147460
  27.1 6.6 %collective-permute-start.14 = (f32[192,64]{0,1:T(8,128)S(1)}, f32[192,64]{0,1:T(8,128)S(1)}, u32[]{:S(2)}, u32[]{:S(2)}) collective-permute-start(f32[192,64]{0,1:T(8,128)S(1)} %broadcast_multiply_fusion), channel_id=1, source_target_pairs={{0,4},{4,8},{8,12},{12,0},{1,5},{5,9},{9,13},{13,1},{2,6},{6,10},{... | collective-permute-start | bytes 147464 | tf_op jit(solution)/shard_map/ppermute | solution.py:48
  28.8 7.0 %collective-permute-start.15 = (f32[192,64]{0,1:T(8,128)S(1)}, f32[192,64]{0,1:T(8,128)S(1)}, u32[]{:S(2)}, u32[]{:S(2)}) collective-permute-start(f32[192,64]{0,1:T(8,128)S(1)} %broadcast_multiply_fusion), channel_id=1, source_target_pairs={{0,8},{4,12},{8,0},{12,4},{1,9},{5,13},{9,1},{13,5},{2,10},{6,14},... | collective-permute-start | bytes 147464 | tf_op jit(solution)/shard_map/ppermute | solution.py:48
  31.7 5.2 %collective-permute-start.16 = (f32[192,64]{0,1:T(8,128)S(1)}, f32[192,64]{0,1:T(8,128)S(1)}, u32[]{:S(2)}, u32[]{:S(2)}) collective-permute-start(f32[192,64]{0,1:T(8,128)S(1)} %broadcast_multiply_fusion), channel_id=1, source_target_pairs={{0,12},{4,0},{8,4},{12,8},{1,13},{5,1},{9,5},{13,9},{2,14},{6,2},{... | collective-permute-start | bytes 147464 | tf_op jit(solution)/shard_map/ppermute | solution.py:48
  33.7 12.1 %collective-permute-start.5 = (bf16[768,64]{0,1:T(8,128)(2,1)S(1)}, bf16[768,64]{0,1:T(8,128)(2,1)S(1)}, u32[]{:S(2)}, u32[]{:S(2)}) collective-permute-start(bf16[768,64]{0,1:T(8,128)(2,1)S(1)} %get-tuple-element.77), channel_id=1, source_target_pairs={{0,96},{16,112},{32,0},{48,16},{64,32},{80,48},{96,64},{112,80},{1... | collective-permute-start | bytes 294920 | tf_op jit(solution)/shard_map/ppermute | solution.py:34
  35.8 10.1 %collective-permute-start.4 = (bf16[768,64]{0,1:T(8,128)(2,1)S(1)}, bf16[768,64]{0,1:T(8,128)(2,1)S(1)}, u32[]{:S(2)}, u32[]{:S(2)}) collective-permute-start(bf16[768,64]{0,1:T(8,128)(2,1)S(1)} %get-tuple-element.78), channel_id=1, source_target_pairs={{0,80},{16,96},{32,112},{48,0},{64,16},{80,32},{96,48},{112,64},{1... | collective-permute-start | bytes 294920 | tf_op jit(solution)/shard_map/ppermute | solution.py:34
  36.9 9.0 %collective-permute-start.3 = (bf16[768,64]{0,1:T(8,128)(2,1)S(1)}, bf16[768,64]{0,1:T(8,128)(2,1)S(1)}, u32[]{:S(2)}, u32[]{:S(2)}) collective-permute-start(bf16[768,64]{0,1:T(8,128)(2,1)S(1)} %get-tuple-element.79), channel_id=1, source_target_pairs={{0,64},{16,80},{32,96},{48,112},{64,0},{80,16},{96,32},{112,48},{1... | collective-permute-start | bytes 294920 | tf_op jit(solution)/shard_map/ppermute | solution.py:34
  38.6 7.2 %collective-permute-start.2 = (bf16[768,64]{0,1:T(8,128)(2,1)S(1)}, bf16[768,64]{0,1:T(8,128)(2,1)S(1)}, u32[]{:S(2)}, u32[]{:S(2)}) collective-permute-start(bf16[768,64]{0,1:T(8,128)(2,1)S(1)} %get-tuple-element.80), channel_id=1, source_target_pairs={{0,48},{16,64},{32,80},{48,96},{64,112},{80,0},{96,16},{112,32},{1... | collective-permute-start | bytes 294920 | tf_op jit(solution)/shard_map/ppermute | solution.py:34
  41.1 7.0 %collective-permute-start.1 = (bf16[768,64]{0,1:T(8,128)(2,1)S(1)}, bf16[768,64]{0,1:T(8,128)(2,1)S(1)}, u32[]{:S(2)}, u32[]{:S(2)}) collective-permute-start(bf16[768,64]{0,1:T(8,128)(2,1)S(1)} %get-tuple-element.81), channel_id=1, source_target_pairs={{0,32},{16,48},{32,64},{48,80},{64,96},{80,112},{96,0},{112,16},{1... | collective-permute-start | bytes 294920 | tf_op jit(solution)/shard_map/ppermute | solution.py:34
  50.3 2.6 %copy-start.7 = (f32[24,768]{1,0:T(8,128)S(1)}, f32[24,768]{1,0:T(8,128)}, u32[]{:S(2)}) copy-start(f32[24,768]{1,0:T(8,128)} %param.24) | copy-start | bytes 221188
  50.3 2.6 %copy-start.8 = (f32[1,24,768]{2,1,0:T(8,128)S(1)}, f32[1,24,768]{2,1,0:T(8,128)}, u32[]{:S(2)}) copy-start(f32[1,24,768]{2,1,0:T(8,128)} %param.19) | copy-start | bytes 221188
  54.5 13.8 %copy-start = (f32[768,768]{1,0:T(8,128)S(1)}, f32[768,768]{1,0:T(8,128)}, u32[]{:S(2)}) copy-start(f32[768,768]{1,0:T(8,128)} %param.25) | copy-start | bytes 7077892
  68.3 4.7 %copy-start.2 = (f32[1,768,64]{1,2,0:T(8,128)}, f32[1,768,64]{1,2,0:T(8,128)S(1)}, u32[]{:S(2)}) copy-start(f32[1,768,64]{1,2,0:T(8,128)S(1)} %bitcast_add_fusion.2) | copy-start | bytes 589828
  68.3 4.7 %copy-start.4 = (f32[768,64]{0,1:T(8,128)S(1)}, f32[768,64]{0,1:T(8,128)}, u32[]{:S(2)}) copy-start(f32[768,64]{0,1:T(8,128)} %param.23) | copy-start | bytes 589828
  68.3 4.7 %copy-start.5 = (f32[1,768,64]{1,2,0:T(8,128)S(1)}, f32[1,768,64]{1,2,0:T(8,128)}, u32[]{:S(2)}) copy-start(f32[1,768,64]{1,2,0:T(8,128)} %param.18) | copy-start | bytes 589828
  68.4 4.8 %copy-start.1 = (f32[1,768,768]{2,1,0:T(8,128)S(1)}, f32[1,768,768]{2,1,0:T(8,128)}, u32[]{:S(2)}) copy-start(f32[1,768,768]{2,1,0:T(8,128)} %param.20) | copy-start | bytes 7077892
  73.1 4.8 %copy-start.6 = (f32[1,768,64]{1,2,0:T(8,128)S(1)}, f32[1,768,64]{1,2,0:T(8,128)}, u32[]{:S(2)}) copy-start(f32[1,768,64]{1,2,0:T(8,128)} %param.16) | copy-start | bytes 589828
  73.1 5.5 %copy-start.9 = (f32[192,64]{0,1:T(8,128)S(1)}, f32[192,64]{0,1:T(8,128)}, u32[]{:S(2)}) copy-start(f32[192,64]{0,1:T(8,128)} %param.21) | copy-start | bytes 147460
  206.4 5.4 %collective-permute-start.17 = (f32[1,768,768]{2,1,0:T(8,128)S(1)}, f32[1,768,768]{2,1,0:T(8,128)}, u32[]{:S(2)}, u32[]{:S(2)}) collective-permute-start(f32[1,768,768]{2,1,0:T(8,128)S(1)} %get-tuple-element.31), channel_id=1, source_target_pairs={{0,1},{1,0},{2,3},{3,2},{4,5},{5,4},{6,7},{7,6},{8,9},{9,8},{10,11... | collective-permute-start | bytes 7077896 | tf_op jit(solution)/shard_map/ppermute | solution.py:135
Sparse Core Ops, SparseCore 0:
  54.7 111.2 all-reduce.1

commit v15 on v11

--- a/solution.py
+++ b/solution.py
@@ -57,9 +57,9 @@
     expert_rows = expert_local.shape[0]
     joined = jnp.concatenate([expert_local, dense_local], 0)
     owned = joined.shape[1] // replicas
-    joined = joined.reshape(joined.shape[0], replicas, owned).transpose(1, 0, 2)
-    received = lax.all_to_all(joined, "dp", 0, 0, tiled=True)
-    joined_sum = jnp.sum(received.astype(jnp.float32), 0)
+    joined = joined.reshape(joined.shape[0], replicas, owned)
+    received = lax.all_to_all(joined, "dp", 1, 1, tiled=True)
+    joined_sum = jnp.sum(received.astype(jnp.float32), 1)
     expert_sum = joined_sum[None, :expert_rows]
     dense_sum = joined_sum[expert_rows:]
     expert_mean = expert_sum / replicas

time: 220 us -> 220 us (level)
  no operation moved by 1% of the time
where the time goes in v15:
time: 220 us; the launch traced here: 218 us
  blocking collectives  73.2 us (33%)
  matrix products  51.2 us (23%)
  waiting for transfers between devices  43.6 us (20%)
  between operations  15.1 us (7%)
  other arithmetic  13 us (6%)
  starting transfers between devices  11.2 us (5%)
  local copies, waits for them, and re-layouts  10.7 us (5%)
    all_gather x1, blocking collectives, shards(): lax.all_gather(dense_master_out.astype(jnp.bfloat16), 'dp', axis=1, tiled...  30.6 us
    all_gather x1, blocking collectives, shards(): lax.all_gather(expert_master_out.astype(jnp.bfloat16), 'dp', axis=2, tile...  30 us
    psum x1, waiting for transfers between devices, shards(): stats_full = lax.psum(placed + 0.05 * partial_stat, ('tensor', 'dp'))  26.8 us
    all_to_all x1, waiting for transfers between devices, shards(): received = lax.all_to_all(joined, 'dp', 1, 1, tiled=True)  14.7 us
    all_gather x1, blocking collectives, shards(): lax.all_gather(dense_first_out, 'wshard', axis=0, tiled=True)  12.6 us
    dot_general x3, matrix products, quintic_step(): jnp.einsum('bik,bkj->bij', gram_matrix, first_prod, precision=HIGH)  12.1 us
    dot_general x3, matrix products, quintic_step(): jnp.einsum('bik,bkj->bij', gram_matrix, current, precision=HIGH)  9.11 us
    dot_general x3, matrix products, local_gram(): return jnp.einsum('bik,bjk->bij', current, current, precision=HIGH)  9.09 us
  transfers between devices with their start and end apart: 6, of which 3 were waited for; matrix products, arithmetic and copies ran while one was open for 9% of the time, Pallas kernels for 0%

profile of v15, /device:TPU:0, one launch (start us, length us, event | category | flops | bytes accessed | tf_op | source)
XLA Modules:
  0.0 218.3 jit_solution(8690092316559669434)
XLA Ops:
  8.2 1.4 copy.32
  9.7 1.1 pad_maximum_fusion.3
  10.8 6.4 %all-to-all-start = ((bf16[960,8,64]{0,2,1:T(8,128)(2,1)}), bf16[960,8,64]{0,2,1:T(8,128)(2,1)S(1)}, u32[]{:S(2)}, u32[]{:S(2)}) async-start(bf16[960,8,64]{0,2,1:T(8,128)(2,1)} %pad_maximum_fusion.3), calls=%async_computation | async-start | bytes 2097152 | tf_op jit(solution)/shard_map/all_to_all | solution.py:61
  17.3 14.7 %all-to-all-done = bf16[960,8,64]{0,2,1:T(8,128)(2,1)S(1)} async-done(((bf16[960,8,64]{0,2,1:T(8,128)(2,1)}), bf16[960,8,64]{0,2,1:T(8,128)(2,1)S(1)}, u32[]{:S(2)}, u32[]{:S(2)}) %all-to-all-start) | async-done | bytes 983072 | tf_op jit(solution)/shard_map/all_to_all | solution.py:61
  32.2 3.1 %collective-permute-start.2 = (f32[192,64]{0,1:T(8,128)S(1)}, f32[192,64]{0,1:T(8,128)S(1)}, u32[]{:S(2)}, u32[]{:S(2)}) collective-permute-start(f32[192,64]{0,1:T(8,128)S(1)} %get-tuple-element.87), channel_id=1, source_target_pairs={{0,12},{4,0},{8,4},{12,8},{1,13},{5,1},{9,5},{13,9},{2,14},{6,2},{... | collective-permute-start | bytes 147464 | tf_op jit(solution)/shard_map/ppermute | solution.py:33
  36.9 2.1 convolution_bitcast_fusion.1
  39.6 2.1 collective-permute-done
  43.7 2.0 convolution_bitcast_fusion
  45.8 2.6 %maximum_multiply_fusion = f32[2,768,768]{2,1,0:T(8,128)} fusion(f32[1,768,768]{2,1,0:T(8,128)S(1)} %convolution_bitcast_fusion, f32[1,768,768]{2,1,0:T(8,128)S(1)} %convolution_bitcast_fusion.1), kind=kLoop, calls=%fused_computation.9 | loop fusion | flops 2359296 | bytes 9437184 | tf_op jit(solution)/shard_map/mul | solution.py:107
  48.4 1.6 fusion.26
  50.0 12.6 %all-gather = f32[4,192,64]{1,2,0:T(8,128)S(1)} all-gather(f32[1,192,64]{1,2,0:T(8,128)S(1)} %bitcast.74), channel_id=1, replica_groups=mesh['dp'=8,'wshard'=4,'tensor'=4] {'wshard'}, dimensions={0}, use_global_device_ids=true | all-gather | bytes 245760 | tf_op jit(solution)/shard_map/all_gather | solution.py:70
  63.1 4.6 %fusion.5 = f32[2,768,128]{1,2,0:T(8,128)S(1)} fusion(f32[1,768,768]{2,1,0:T(8,128)S(1)} %bitcast.68, f32[1,768,768]{2,1,0:T(8,128)} %param.20, f32[1,768,64]{1,2,0:T(8,128)S(1)} %broadcast_in_dim.29, f32[1,768,64]{1,2,0:T(8,128)S(1)} %bitcast_add_fusion.2, f32[1,768,64]{1,2,0:T(8,128)S(1)} %bitcast.71, f32[1,768,64]{1,2,0:T(8,128)S(1)} %fusion.24), kind=kOutput, calls=%fused_computation.11 | convolution fusion | flops 1813708800 | bytes 6291456 | tf_op jit(solution)/shard_map/bki,bkc->bic/dot_general | solution.py:76
  67.8 4.8 %fusion.4 = f32[2,768,64]{1,2,0:T(8,128)S(1)} fusion(f32[1,768,768]{2,1,0:T(8,128)S(1)} %bitcast.69, f32[1,768,768]{2,1,0:T(8,128)S(1)} %copy-done.1, f32[2,768,128]{1,2,0:T(8,128)S(1)} %fusion.5, f32[2,768,64]{1,2,0:T(8,128)S(1)} %fusion.19), kind=kOutput, calls=%fused_computation.10 | convolution fusion | flops 907345920 | bytes 5898240 | tf_op jit(solution)/shard_map/bik,bkc->bic/dot_general | solution.py:83
  74.0 30.6 %all_gather.11 = bf16[192,512]{0,1:T(8,128)(2,1)} all-gather(bf16[192,64]{0,1:T(8,128)(2,1)S(1)} %get-tuple-element.75), channel_id=1, replica_groups=mesh['dp'=8,'wshard'=4,'tensor'=4] {'dp'}, dimensions={1}, use_global_device_ids=true | all-gather | bytes 221184 | tf_op jit(solution)/shard_map/all_gather | solution.py:92
  104.6 30.0 %all_gather.10 = bf16[1,768,512]{1,2,0:T(8,128)(2,1)S(1)} all-gather(bf16[1,768,64]{1,2,0:T(8,128)(2,1)S(1)} %get-tuple-element.77), channel_id=1, replica_groups=mesh['dp'=8,'wshard'=4,'tensor'=4] {'dp'}, dimensions={2}, use_global_device_ids=true | all-gather | bytes 884736 | tf_op jit(solution)/shard_map/all_gather | solution.py:91
  134.6 26.8 %all-reduce.2.cloned.1.call-done = f32[2,768,768]{2,1,0:T(8,128)} async-done(((f32[2,768,768]{2,1,0:T(8,128)}), f32[2,768,768]{2,1,0:T(8,128)}) %all-reduce.2.cloned.1.call-update) | async-done | bytes 4718608 | tf_op jit(solution)/shard_map/psum | solution.py:107
  161.4 7.5 %multiply_reduce_fusion = (f32[]{:T(128)}, f32[768,768]{1,0:T(8,128)}) fusion(s32[]{:T(128)S(6)} %select_n.62, f32[1,768,768]{2,1,0:T(8,128)} %param.20, f32[1,768,768]{2,1,0:T(8,128)S(1)} %bitcast.70, f32[2,768,768]{2,1,0:T(8,128)} %all-reduce.2.cloned.1.call-done), kind=kOutput, calls=%fused_computation.18 | convolution fusion | flops 2719678464 | bytes 9438212 | tf_op jit(solution)/shard_map/bik,bkj->bij/dot_general | solution.py:118
  169.6 1.8 multiply_bitcast_fusion
  171.4 30.6 %while.10 = (s32[]{:T(128)}, f32[1,768,768]{2,1,0:T(8,128)S(1)}, s32[]{:T(128)}) while((s32[]{:T(128)}, f32[1,768,768]{2,1,0:T(8,128)S(1)}, s32[]{:T(128)}) %tuple.35), condition=%wide.region_4.5_spmd, body=%wide.region_3.4_spmd.sunk | while | flops 8156676096 | bytes 21233708 | solution.py:125
  171.6 3.0 %fusion.54 = f32[768,768]{1,0:T(8,128)S(1)} fusion(f32[1,768,768]{2,1,0:T(8,128)S(1)} %get-tuple-element.107), kind=kOutput, calls=%fused_computation.4.clone.1 | convolution fusion | flops 2717908992 | bytes 4718592 | tf_op jit(solution)/shard_map/while/body/eval_jaxpr/bik,bjk->bij/dot_general | solution.py:17
  174.7 3.0 %fusion.55 = f32[768,768]{1,0:T(8,128)S(1)} fusion(f32[768,768]{1,0:T(8,128)S(1)} %fusion.54, f32[1,768,768]{2,1,0:T(8,128)S(1)} %get-tuple-element.107), kind=kOutput, calls=%fused_computation.2.clone.1 | convolution fusion | flops 2717908992 | bytes 7077888 | tf_op jit(solution)/shard_map/while/body/eval_jaxpr/bik,bkj->bij/dot_general | solution.py:21
  177.7 4.0 %bitcast_add_fusion.4 = f32[1,768,768]{2,1,0:T(8,128)S(1)} fusion(f32[768,768]{1,0:T(8,128)S(1)} %fusion.55, f32[1,768,768]{2,1,0:T(8,128)S(1)} %get-tuple-element.107, f32[768,768]{1,0:T(8,128)S(1)} %fusion.54), kind=kOutput, calls=%fused_computation.clone.1 | convolution fusion | flops 2720858112 | bytes 9437184 | tf_op jit(solution)/shard_map/while/body/eval_jaxpr/bik,bkj->bij/dot_general | solution.py:22
  181.7 3.0 %fusion.54 = f32[768,768]{1,0:T(8,128)S(1)} fusion(f32[1,768,768]{2,1,0:T(8,128)S(1)} %get-tuple-element.107), kind=kOutput, calls=%fused_computation.4.clone.1 | convolution fusion | flops 2717908992 | bytes 4718592 | tf_op jit(solution)/shard_map/while/body/eval_jaxpr/bik,bjk->bij/dot_general | solution.py:17
  184.8 3.0 %fusion.55 = f32[768,768]{1,0:T(8,128)S(1)} fusion(f32[768,768]{1,0:T(8,128)S(1)} %fusion.54, f32[1,768,768]{2,1,0:T(8,128)S(1)} %get-tuple-element.107), kind=kOutput, calls=%fused_computation.2.clone.1 | convolution fusion | flops 2717908992 | bytes 7077888 | tf_op jit(solution)/shard_map/while/body/eval_jaxpr/bik,bkj->bij/dot_general | solution.py:21
  187.8 4.0 %bitcast_add_fusion.4 = f32[1,768,768]{2,1,0:T(8,128)S(1)} fusion(f32[768,768]{1,0:T(8,128)S(1)} %fusion.55, f32[1,768,768]{2,1,0:T(8,128)S(1)} %get-tuple-element.107, f32[768,768]{1,0:T(8,128)S(1)} %fusion.54), kind=kOutput, calls=%fused_computation.clone.1 | convolution fusion | flops 2720858112 | bytes 9437184 | tf_op jit(solution)/shard_map/while/body/eval_jaxpr/bik,bkj->bij/dot_general | solution.py:22
  191.9 3.0 %fusion.54 = f32[768,768]{1,0:T(8,128)S(1)} fusion(f32[1,768,768]{2,1,0:T(8,128)S(1)} %get-tuple-element.107), kind=kOutput, calls=%fused_computation.4.clone.1 | convolution fusion | flops 2717908992 | bytes 4718592 | tf_op jit(solution)/shard_map/while/body/eval_jaxpr/bik,bjk->bij/dot_general | solution.py:17
  194.9 3.0 %fusion.55 = f32[768,768]{1,0:T(8,128)S(1)} fusion(f32[768,768]{1,0:T(8,128)S(1)} %fusion.54, f32[1,768,768]{2,1,0:T(8,128)S(1)} %get-tuple-element.107), kind=kOutput, calls=%fused_computation.2.clone.1 | convolution fusion | flops 2717908992 | bytes 7077888 | tf_op jit(solution)/shard_map/while/body/eval_jaxpr/bik,bkj->bij/dot_general | solution.py:21
  197.9 4.0 %bitcast_add_fusion.4 = f32[1,768,768]{2,1,0:T(8,128)S(1)} fusion(f32[768,768]{1,0:T(8,128)S(1)} %fusion.55, f32[1,768,768]{2,1,0:T(8,128)S(1)} %get-tuple-element.107, f32[768,768]{1,0:T(8,128)S(1)} %fusion.54), kind=kOutput, calls=%fused_computation.clone.1 | convolution fusion | flops 2720858112 | bytes 9437184 | tf_op jit(solution)/shard_map/while/body/eval_jaxpr/bik,bkj->bij/dot_general | solution.py:22
  202.9 1.8 copy.36
  204.6 1.2 copy.35
  205.8 1.6 dynamic-slice_bitcast_fusion
  207.4 4.2 %select_bitcast_fusion = (f32[768,768]{1,0:T(8,128)}, f32[1,768,768]{2,1,0:T(8,128)}) fusion(f32[1,768,768]{2,1,0:T(8,128)} %collective-permute-done.3, f32[1,768,768]{2,1,0:T(8,128)S(1)} %get-tuple-element.31, pred[]{:T(512)S(6)} %eq.9), kind=kLoop, calls=%fused_computation.16 | loop fusion | flops 1179648 | bytes 9437185 | tf_op jit(solution)/shard_map/squeeze | solution.py:130
  (48 shorter events, 8.3 us)
Async XLA Ops:
  9.7 22.5 %copy-start.11 = (f32[192,64]{0,1:T(8,128)S(1)}, f32[192,64]{0,1:T(8,128)}, u32[]{:S(2)}) copy-start(f32[192,64]{0,1:T(8,128)} %param.22) | copy-start | bytes 147460
  10.8 21.2 %all-to-all-start = ((bf16[960,8,64]{0,2,1:T(8,128)(2,1)}), bf16[960,8,64]{0,2,1:T(8,128)(2,1)S(1)}, u32[]{:S(2)}, u32[]{:S(2)}) async-start(bf16[960,8,64]{0,2,1:T(8,128)(2,1)} %pad_maximum_fusion.3), calls=%async_computation | async-start | bytes 2097152 | tf_op jit(solution)/shard_map/all_to_all | solution.py:61
  17.1 144.2 %all-reduce.2.cloned.1.call-start = ((), (), s32[]{:S(2)}) async-start(), calls=%async_computation.1 | async-start | bytes 9437184 | tf_op jit(solution)/shard_map/psum | solution.py:107
  32.2 17.9 %copy-start.3 = (f32[192,64]{0,1:T(8,128)}, f32[192,64]{0,1:T(8,128)S(1)}, u32[]{:S(2)}) copy-start(f32[192,64]{0,1:T(8,128)S(1)} %get-tuple-element.86) | copy-start | bytes 147460
  32.2 10.7 %collective-permute-start.2 = (f32[192,64]{0,1:T(8,128)S(1)}, f32[192,64]{0,1:T(8,128)S(1)}, u32[]{:S(2)}, u32[]{:S(2)}) collective-permute-start(f32[192,64]{0,1:T(8,128)S(1)} %get-tuple-element.87), channel_id=1, source_target_pairs={{0,12},{4,0},{8,4},{12,8},{1,13},{5,1},{9,5},{13,9},{2,14},{6,2},{... | collective-permute-start | bytes 147464 | tf_op jit(solution)/shard_map/ppermute | solution.py:33
  35.2 7.0 %collective-permute-start.1 = (f32[192,64]{0,1:T(8,128)S(1)}, f32[192,64]{0,1:T(8,128)S(1)}, u32[]{:S(2)}, u32[]{:S(2)}) collective-permute-start(f32[192,64]{0,1:T(8,128)S(1)} %get-tuple-element.87), channel_id=1, source_target_pairs={{0,8},{4,12},{8,0},{12,4},{1,9},{5,13},{9,1},{13,5},{2,10},{6,14},... | collective-permute-start | bytes 147464 | tf_op jit(solution)/shard_map/ppermute | solution.py:33
  35.9 5.8 %collective-permute-start = (f32[192,64]{0,1:T(8,128)S(1)}, f32[192,64]{0,1:T(8,128)S(1)}, u32[]{:S(2)}, u32[]{:S(2)}) collective-permute-start(f32[192,64]{0,1:T(8,128)S(1)} %get-tuple-element.87), channel_id=1, source_target_pairs={{0,4},{4,8},{8,12},{12,0},{1,5},{5,9},{9,13},{13,1},{2,6},{6,10},{... | collective-permute-start | bytes 147464 | tf_op jit(solution)/shard_map/ppermute | solution.py:33
  45.7 2.6 %copy-start.8 = (f32[24,768]{1,0:T(8,128)S(1)}, f32[24,768]{1,0:T(8,128)}, u32[]{:S(2)}) copy-start(f32[24,768]{1,0:T(8,128)} %param.24) | copy-start | bytes 221188
  45.7 2.6 %copy-start.9 = (f32[1,24,768]{2,1,0:T(8,128)S(1)}, f32[1,24,768]{2,1,0:T(8,128)}, u32[]{:S(2)}) copy-start(f32[1,24,768]{2,1,0:T(8,128)} %param.19) | copy-start | bytes 221188
  50.0 13.0 %copy-start.6 = (f32[1,768,64]{1,2,0:T(8,128)S(1)}, f32[1,768,64]{1,2,0:T(8,128)}, u32[]{:S(2)}) copy-start(f32[1,768,64]{1,2,0:T(8,128)} %param.17) | copy-start | bytes 589828
  50.0 13.1 %copy-start = (f32[768,768]{1,0:T(8,128)S(1)}, f32[768,768]{1,0:T(8,128)}, u32[]{:S(2)}) copy-start(f32[768,768]{1,0:T(8,128)} %param.25) | copy-start | bytes 7077892
  63.0 4.6 %copy-start.2 = (f32[1,768,64]{1,2,0:T(8,128)}, f32[1,768,64]{1,2,0:T(8,128)S(1)}, u32[]{:S(2)}) copy-start(f32[1,768,64]{1,2,0:T(8,128)S(1)} %bitcast_add_fusion.2) | copy-start | bytes 589828
  63.0 4.6 %copy-start.4 = (f32[768,64]{0,1:T(8,128)S(1)}, f32[768,64]{0,1:T(8,128)}, u32[]{:S(2)}) copy-start(f32[768,64]{0,1:T(8,128)} %param.23) | copy-start | bytes 589828
  63.1 4.6 %copy-start.5 = (f32[1,768,64]{1,2,0:T(8,128)S(1)}, f32[1,768,64]{1,2,0:T(8,128)}, u32[]{:S(2)}) copy-start(f32[1,768,64]{1,2,0:T(8,128)} %param.18) | copy-start | bytes 589828
  63.1 4.7 %copy-start.1 = (f32[1,768,768]{2,1,0:T(8,128)S(1)}, f32[1,768,768]{2,1,0:T(8,128)}, u32[]{:S(2)}) copy-start(f32[1,768,768]{2,1,0:T(8,128)} %param.20) | copy-start | bytes 7077892
  67.8 4.8 %copy-start.7 = (f32[1,768,64]{1,2,0:T(8,128)S(1)}, f32[1,768,64]{1,2,0:T(8,128)}, u32[]{:S(2)}) copy-start(f32[1,768,64]{1,2,0:T(8,128)} %param.16) | copy-start | bytes 589828
  67.8 5.5 %copy-start.10 = (f32[192,64]{0,1:T(8,128)S(1)}, f32[192,64]{0,1:T(8,128)}, u32[]{:S(2)}) copy-start(f32[192,64]{0,1:T(8,128)} %param.21) | copy-start | bytes 147460
  202.0 5.4 %collective-permute-start.3 = (f32[1,768,768]{2,1,0:T(8,128)S(1)}, f32[1,768,768]{2,1,0:T(8,128)}, u32[]{:S(2)}, u32[]{:S(2)}) collective-permute-start(f32[1,768,768]{2,1,0:T(8,128)S(1)} %get-tuple-element.31), channel_id=1, source_target_pairs={{0,1},{1,0},{2,3},{3,2},{4,5},{5,4},{6,7},{7,6},{8,9},{9,8},{10,11... | collective-permute-start | bytes 7077896 | tf_op jit(solution)/shard_map/ppermute | solution.py:126
Sparse Core Ops, SparseCore 0:
  50.1 111.2 all-reduce.1
